TPU v7x, 128 devices: a whole 4x4x4 slice. The times are simulated.
128 devices in a mesh: blk: 16 (over z, y), exp: 8 (over x, core).
Axes of the slice: x: 4, y: 4, z: 4, core: 2. Of those that a mesh axis runs over, the one named last changes fastest.
Arguments:
- stream: bfloat16 [16384, 2048], P(('blk', 'exp')), may hold values from -6 to 6
- norm_gain: float32 [2048], replicated, may hold values from 0.5 to 1.5
- query_weight: bfloat16 [2048, 1024], P(None, 'exp')
- key_weight: bfloat16 [2048, 1024], P(None, 'exp')
- value_weight: bfloat16 [2048, 1024], P(None, 'exp'), may hold values from -0.125 to 0.125
- output_weight: bfloat16 [1024, 2048], replicated, may hold values from -0.1875 to 0.1875
- post_gain: float32 [2048], replicated, may hold values from 0.5 to 1.5
- shared_gate: bfloat16 [2048, 3072], P(None, 'exp'), may hold values from -0.125 to 0.125
- shared_up: bfloat16 [2048, 3072], P(None, 'exp'), may hold values from -0.125 to 0.125
- shared_down: bfloat16 [3072, 2048], P('exp'), may hold values from -0.109375 to 0.109375
- shared_router: bfloat16 [2048], replicated, may hold values from -0.125 to 0.125
- expert_gate: bfloat16 [128, 2048, 704], P(('blk', 'exp')), may hold values from -0.125 to 0.125
- expert_up: bfloat16 [128, 2048, 704], P(('blk', 'exp')), may hold values from -0.125 to 0.125
- expert_down: bfloat16 [128, 704, 2048], P(('blk', 'exp')), may hold values from -0.15625 to 0.15625
- expert_ids: int32 [16384, 4], P(('blk', 'exp')), may hold values from 0 to 63, all different within a row; in each aligned block of 128 rows (0 to 127, 128 to 255, ...) at most 10 rows name the same one
- route_weights: float32 [16384, 4], P(('blk', 'exp')), may hold values from 0.05 to 0.5
- positions: int32 [16384], P(('blk', 'exp')), may hold values from 0 to 16383, as said below
- segment_ids: int32 [16384], P(('blk', 'exp')), may hold values from 0 to 11, as said below
- cache_slots: int32 [16384], P(('blk', 'exp')), may hold values from 0 to 1023, as said below
Outputs:
- final: bfloat16 [16384, 2048], P(('blk', 'exp'))
- cache_keys: bfloat16 [16384, 1024], P('blk', 'exp')
- cache_values: bfloat16 [16384, 1024], P('blk', 'exp')
Inputs may be any that keep to these rules, and one draw needn't show every extreme that they name: `positions`: a permutation of all positions of the stream. `segment_ids`: the document number never falls along the position in the stream, and every document holds a token. `cache_slots`: within each block of 1024 rows a permutation of 0 to 1023.
All inputs are finite; a program needn't handle non-finite values.
Results may differ from a plain program's by a relative error of at most 0.015.
Values may be sent and summed in bfloat16 or wider, within the bound.
No kernel may reach another device: no remote copies, remote signals or barrier semaphores. Data moves between devices by JAX's collectives and lax.ppermute only.
A program may use at most 128 MiB of HBM per device.

v0:
```python
import math

import jax
import jax.numpy as jnp
from jax import lax
from jax.sharding import PartitionSpec as P

D = 2048
HD = 128
TOP = 4


EPS = 1e-06
FLOOR_SCORE = -1e30


def rms_norm(rows, gain):
    wide = rows.astype(jnp.float32)
    factor = lax.rsqrt(jnp.mean(wide * wide, axis=-1, keepdims=True) + EPS)
    return (wide * factor * gain).astype(jnp.bfloat16)


def per_device(
    stream,
    norm_gain,
    query_weight,
    key_weight,
    value_weight,
    output_weight,
    post_gain,
    shared_gate,
    shared_up,
    shared_down,
    shared_router,
    expert_gate,
    expert_up,
    expert_down,
    expert_ids,
    route_weights,
    positions,
    segment_ids,
    cache_slots,
):
    local_rows = stream.shape[0]
    group_stream, group_position, group_segment, group_slot = (
        lax.all_gather(stream, "exp", axis=0, tiled=True),
        lax.all_gather(positions, "exp", axis=0, tiled=True),
        lax.all_gather(segment_ids, "exp", axis=0, tiled=True),
        lax.all_gather(cache_slots, "exp", axis=0, tiled=True),
    )
    group_size = group_stream.shape[0]
    normed = rms_norm(group_stream, norm_gain)
    queries = jnp.dot(normed, query_weight, preferred_element_type=jnp.float32).astype(jnp.bfloat16)
    keys = jnp.dot(normed, key_weight, preferred_element_type=jnp.float32).astype(jnp.bfloat16)
    values = jnp.dot(normed, value_weight, preferred_element_type=jnp.float32).astype(jnp.bfloat16)
    width = queries.shape[1]
    local_heads = width // HD
    cache_keys = jnp.zeros((group_size, width), jnp.bfloat16).at[group_slot].set(keys)
    cache_values = jnp.zeros((group_size, width), jnp.bfloat16).at[group_slot].set(values)
    query_heads = queries.reshape(group_size, local_heads, HD)
    factor = HD ** (-0.5)

    def attend(carry, block):
        highest, denom, summed = carry
        block_keys, block_values, block_position, block_segment = block
        scores = (
            jnp.einsum("qhd,khd->hqk", query_heads, block_keys, preferred_element_type=jnp.float32)
            * factor
        )
        allowed = (
            (block_segment[None, :] == group_segment[:, None])
            & (block_position[None, :] <= group_position[:, None])
        )[None]
        scores = jnp.where(allowed, scores, FLOOR_SCORE)
        newest = jnp.maximum(highest, jnp.max(scores, axis=2))
        probs = jnp.where(allowed, jnp.exp(scores - newest[:, :, None]), 0.0)
        shrink = jnp.exp(highest - newest)
        denom = denom * shrink + jnp.sum(probs, axis=2)
        summed = summed * shrink[:, :, None] + jnp.einsum(
            "hqk,khd->hqd",
            probs.astype(jnp.bfloat16),
            block_values,
            preferred_element_type=jnp.float32,
        )
        return ((newest, denom, summed), None)

    initial = (
        jnp.full((local_heads, group_size), FLOOR_SCORE, jnp.float32),
        jnp.zeros((local_heads, group_size), jnp.float32),
        jnp.zeros((local_heads, group_size, HD), jnp.float32),
    )
    key_heads = keys.reshape(group_size, local_heads, HD)
    value_heads = values.reshape(group_size, local_heads, HD)
    carry = initial
    piece = (
        lax.all_gather(key_heads, "blk", axis=0, tiled=True),
        lax.all_gather(value_heads, "blk", axis=0, tiled=True),
        lax.all_gather(group_position, "blk", axis=0, tiled=True),
        lax.all_gather(group_segment, "blk", axis=0, tiled=True),
    )
    piece_rows = piece[0].shape[0]
    block = math.gcd(piece_rows, 1024)
    count = piece_rows // block
    blocks = tuple((member.reshape((count, block) + member.shape[1:]) for member in piece))
    carry, _ = lax.scan(attend, carry, blocks)
    highest, denom, summed = carry
    heads_out = (summed / denom[:, :, None]).astype(jnp.bfloat16)
    heads_out = jnp.transpose(heads_out, (1, 0, 2)).reshape(group_size, width)
    owner = lax.axis_index("exp")
    local_output = lax.dynamic_slice_in_dim(output_weight, owner * width, width, 0)
    attended = lax.psum(
        jnp.dot(heads_out, local_output, preferred_element_type=jnp.float32).astype(jnp.bfloat16),
        "exp",
    ).astype(jnp.float32)
    resid_group = (group_stream.astype(jnp.float32) + attended).astype(jnp.bfloat16)
    resid_local = lax.dynamic_slice_in_dim(resid_group, owner * local_rows, local_rows, 0)
    normed_group = rms_norm(resid_group, post_gain)
    normed_local = lax.dynamic_slice_in_dim(normed_group, owner * local_rows, local_rows, 0)
    hidden = (
        jax.nn.silu(jnp.dot(normed_group, shared_gate, preferred_element_type=jnp.float32))
        * jnp.dot(normed_group, shared_up, preferred_element_type=jnp.float32)
    ).astype(jnp.bfloat16)
    opening = jax.nn.sigmoid(
        jnp.dot(normed_group, shared_router, preferred_element_type=jnp.float32)
    )
    shared_local = lax.psum_scatter(
        (
            jnp.dot(hidden, shared_down, preferred_element_type=jnp.float32) * opening[:, None]
        ).astype(jnp.bfloat16),
        "exp",
        scatter_dimension=0,
        tiled=True,
    ).astype(jnp.float32)
    experts = lax.axis_size(("blk", "exp")) // 2
    capacity = max(2, 5 * local_rows * TOP // (4 * experts))
    flat_ids = expert_ids.reshape(-1)
    onehot = (flat_ids[:, None] == jnp.arange(experts, dtype=jnp.int32)[None, :]).astype(jnp.int32)
    slots = jnp.sum(onehot * (jnp.cumsum(onehot, axis=0) - 1), axis=1)
    pair_token = jnp.arange(local_rows * TOP, dtype=jnp.int32) // TOP
    single = (
        jnp.zeros((experts, capacity, D), jnp.bfloat16)
        .at[flat_ids, slots]
        .set(normed_local[pair_token])
    )
    outgoing = jnp.broadcast_to(single[:, None], (experts, 2, capacity, D)).reshape(
        2 * experts, capacity, D
    )
    arrived = lax.all_to_all(outgoing, ("blk", "exp"), split_axis=0, concat_axis=0, tiled=True)
    leading = arrived.shape[:-1]
    flat_rows = arrived.reshape(-1, D)
    hidden = (
        jax.nn.silu(jnp.dot(flat_rows, expert_gate[0], preferred_element_type=jnp.float32))
        * jnp.dot(flat_rows, expert_up[0], preferred_element_type=jnp.float32)
    ).astype(jnp.bfloat16)
    returned = lax.all_to_all(
        jnp.dot(hidden, expert_down[0], preferred_element_type=jnp.float32)
        .astype(jnp.bfloat16)
        .reshape(leading + (D,)),
        ("blk", "exp"),
        split_axis=0,
        concat_axis=0,
        tiled=True,
    )
    halves = returned.reshape(experts, 2, capacity, D)
    combined = (halves[:, 0].astype(jnp.float32) + halves[:, 1].astype(jnp.float32)).reshape(
        experts * capacity, D
    )
    picked = combined[flat_ids * capacity + slots] * route_weights.reshape(-1)[:, None]
    routed = jnp.sum(picked.reshape(local_rows, TOP, D), axis=1)
    final = (resid_local.astype(jnp.float32) + shared_local + routed).astype(jnp.bfloat16)
    return (final, cache_keys, cache_values)


def solution(mesh):
    in_specs = (
        P(("blk", "exp"), None),
        P(),
        P(None, "exp"),
        P(None, "exp"),
        P(None, "exp"),
        P(),
        P(),
        P(None, "exp"),
        P(None, "exp"),
        P("exp", None),
        P(),
        P(("blk", "exp"), None, None),
        P(("blk", "exp"), None, None),
        P(("blk", "exp"), None, None),
        P(("blk", "exp"), None),
        P(("blk", "exp"), None),
        P(("blk", "exp")),
        P(("blk", "exp")),
        P(("blk", "exp")),
    )
    out_specs = (P(("blk", "exp"), None), P("blk", "exp"), P("blk", "exp"))
    return jax.shard_map(
        per_device, mesh=mesh, in_specs=in_specs, out_specs=out_specs, check_vma=False
    )
```

profile of v0, /device:TPU:1, one launch (start us, length us, event | category | flops | bytes accessed | tf_op | source)
XLA Modules:
  0.0 807.8 jit_solution(5058287328521965292)
XLA Ops:
  8.0 37.4 %all-gather.9.cloned.1.call-done = bf16[1024,2048]{1,0:T(8,128)(2,1)} async-done(((bf16[128,2048]{1,0:T(8,128)(2,1)}), bf16[1024,2048]{1,0:T(8,128)(2,1)}) %all-gather.9.cloned.1.call-update) | async-done | bytes 4194320 | tf_op jit(solution)/shard_map/all_gather | solution.py:46
  58.1 8.8 %all-gather.2 = s32[8,1,128]{2,1,0:T(1,128)S(1)} all-gather(s32[1,1,128]{2,1,0:T(1,128)S(1)} %bitcast.165), channel_id=1, replica_groups=mesh['blk'=16,'exp'=8] {'exp'}, dimensions={0}, use_global_device_ids=true | all-gather | bytes 4608 | tf_op jit(solution)/shard_map/all_gather | solution.py:48
  66.8 18.9 %all_gather.26 = s32[16384]{0:T(1024)S(1)} all-gather(s32[1024]{0:T(1024)S(1)} %bitcast.154), channel_id=1, replica_groups=mesh['blk'=16,'exp'=8] {'blk'}, dimensions={0}, use_global_device_ids=true | all-gather | bytes 69632 | tf_op jit(solution)/shard_map/all_gather | solution.py:99
  85.7 14.5 %all-gather.3 = s32[8,1,128]{2,1,0:T(1,128)S(1)} all-gather(s32[1,1,128]{2,1,0:T(1,128)} %bitcast.166), channel_id=1, replica_groups=mesh['blk'=16,'exp'=8] {'exp'}, dimensions={0}, use_global_device_ids=true | all-gather | bytes 4608 | tf_op jit(solution)/shard_map/all_gather | solution.py:47
  100.2 17.9 %all_gather.28 = s32[16384]{0:T(1024)S(1)} all-gather(s32[1024]{0:T(1024)S(1)} %bitcast.156), channel_id=1, replica_groups=mesh['blk'=16,'exp'=8] {'blk'}, dimensions={0}, use_global_device_ids=true | all-gather | bytes 69632 | tf_op jit(solution)/shard_map/all_gather | solution.py:98
  123.1 35.6 %all-gather.11.cloned.1.call-done = bf16[16384,128]{1,0:T(8,128)(2,1)} async-done(((bf16[1024,128]{1,0:T(8,128)(2,1)}), bf16[16384,128]{1,0:T(8,128)(2,1)}) %all-gather.11.cloned.1.call-update) | async-done | bytes 4194320 | tf_op jit(solution)/shard_map/all_gather | solution.py:96
  158.7 122.0 %while.15 = (s32[]{:T(128)}, f32[1,1024]{1,0:T(1,128)S(1)}, f32[1,1024]{1,0:T(1,128)S(1)}, f32[1,1024,128]{2,1,0:T(8,128)S(1)}, s32[16,1024]{1,0:T(8,128)S(1)}, ...) while((s32[]{:T(128)}, f32[1,1024]{1,0:T(1,128)S(1)}, ...), condition=%wide.region_4.5_spmd.clone, body=%wide.region_1.4_spmd.clone.sunk | while | flops 560337920 | bytes 14549149 | solution.py:105
  287.8 67.7 %all-reduce.2.cloned.1.call-done = bf16[1024,2048]{1,0:T(8,128)(2,1)} async-done(((bf16[1024,2048]{1,0:T(8,128)(2,1)}), bf16[1024,2048]{1,0:T(8,128)(2,1)}) %all-reduce.2.cloned.1.call-update) | async-done | bytes 4194320 | tf_op jit(solution)/shard_map/psum | solution.py:111
  355.5 5.5 fusion.25
  370.1 104.5 %scatter_fusion = bf16[64,10,2048]{2,0,1:T(8,128)(2,1)} fusion(bf16[64,10,2048]{2,0,1:T(8,128)(2,1)} %broadcast_in_dim.29, s32[512]{0:T(512)S(1)} %bitcast.142, bf16[512,2048]{1,0:T(8,128)(2,1)} %gather_fusion), kind=kCustom, calls=%fused_computation.2 | custom fusion | bytes 6295552 | tf_op jit(solution)/shard_map/scatter | solution.py:143
  479.9 6.8 broadcast_in_dim.30
  486.6 10.4 %all-to-all-start = ((bf16[128,10,2048]{2,1,0:T(8,128)(2,1)}), bf16[128,10,2048]{2,1,0:T(8,128)(2,1)}, u32[]{:S(2)}, u32[]{:S(2)}) async-start(bf16[128,10,2048]{2,1,0:T(8,128)(2,1)} %bitcast.143), calls=%async_computation.1 | async-start | bytes 16777216 | tf_op jit(solution)/shard_map/all_to_all | solution.py:148
  505.6 8.8 %multiply_convert_fusion = bf16[1024,2048]{1,0:T(8,128)(2,1)} fusion(bf16[384,2048]{1,0:T(8,128)(2,1)} %param.30, f32[1024]{0:T(1024)S(1)} %add_divide_fusion, f32[1024,384]{1,0:T(8,128)} %fusion.51, bf16[1024,2048]{1,0:T(8,128)(2,1)} %copy-done.2, bf16[2048,384]{1,0:T(8,128)(2,1)} %param.29), kind=kOutput, calls=%fused_computation.47 | convolution fusion | flops 3227779072 | bytes 13111296 | tf_op jit(solution)/shard_map/dot_general | solution.py:128
  514.5 99.9 %all-to-all-done = bf16[128,10,2048]{2,1,0:T(8,128)(2,1)} async-done(((bf16[128,10,2048]{2,1,0:T(8,128)(2,1)}), bf16[128,10,2048]{2,1,0:T(8,128)(2,1)}, u32[]{:S(2)}, u32[]{:S(2)}) %all-to-all-start) | async-done | bytes 5242912 | tf_op jit(solution)/shard_map/all_to_all | solution.py:148
  614.3 9.8 %reshape.249 = bf16[1280,2048]{1,0:T(8,128)(2,1)} reshape(bf16[128,10,2048]{2,1,0:T(8,128)(2,1)} %all-to-all-done) | data formatting | bytes 10485760 | tf_op jit(solution)/shard_map/reshape | solution.py:150
  624.2 7.4 fusion.35
  635.9 6.1 convolution_convert_fusion
  642.0 9.5 %reshape.250 = bf16[128,10,2048]{2,1,0:T(8,128)(2,1)} reshape(bf16[1280,2048]{1,0:T(8,128)(2,1)} %convolution_convert_fusion) | data formatting | bytes 10485760 | tf_op jit(solution)/shard_map/reshape | solution.py:158
  651.5 6.2 all-to-all-start.1
  657.8 96.8 %all-gather.4 = s32[8,1,128]{2,1,0:T(1,128)S(1)} all-gather(s32[1,1,128]{2,1,0:T(1,128)S(1)} %bitcast.167), channel_id=1, replica_groups=mesh['blk'=16,'exp'=8] {'exp'}, dimensions={0}, use_global_device_ids=true | all-gather | bytes 4608 | tf_op jit(solution)/shard_map/all_gather | solution.py:49
  763.2 8.6 %convert_add_fusion.1 = f32[64,1,10,2048]{3,2,0,1:T(8,128)} fusion(bf16[64,2,10,2048]{3,2,1,0:T(8,128)(2,1)} %bitcast.20), kind=kLoop, calls=%fused_computation.46 | loop fusion | flops 3932160 | bytes 10485760 | tf_op jit(solution)/shard_map/add | solution.py:165
  771.8 7.3 add.149
  779.1 8.0 gather_fusion.1
  792.2 6.3 multiply_reduce_fusion
  (202 shorter events, 189.9 us)
Async XLA Ops:
  7.2 628.7 %copy-start = (bf16[1,704,2048]{2,1,0:T(8,128)(2,1)S(1)}, bf16[1,704,2048]{2,1,0:T(8,128)(2,1)}, u32[]{:S(2)}) copy-start(bf16[1,704,2048]{2,1,0:T(8,128)(2,1)} %param.34) | copy-start | bytes 8650756
  7.2 41.4 %copy-start.7 = (f32[2048]{0:T(1024)S(1)}, f32[2048]{0:T(1024)}, u32[]{:S(2)}) copy-start(f32[2048]{0:T(1024)} %param.22) | copy-start | bytes 24580
  7.2 38.2 %all-gather.9.cloned.1.call-start = ((), (), s32[]{:S(2)}) async-start(), calls=%async_computation.3 | async-start | bytes 4718592 | tf_op jit(solution)/shard_map/all_gather | solution.py:46
  7.9 115.1 %all-gather.13.cloned.1.call-start = ((), (), s32[]{:S(2)}) async-start(), calls=%async_computation.7 | async-start | bytes 4456448 | tf_op jit(solution)/shard_map/all_gather | solution.py:97
  45.4 3.4 copy-start.1
  48.8 3.0 copy-start.15
  49.8 1.9 copy-start.6
  51.8 2.0 copy-start.16
  53.7 4.3 copy-start.12
  53.8 104.9 %all-gather.11.cloned.1.call-start = ((), (), s32[]{:S(2)}) async-start(), calls=%async_computation.6 | async-start | bytes 4456448 | tf_op jit(solution)/shard_map/all_gather | solution.py:96
  58.0 297.5 %all-reduce.2.cloned.1.call-start = ((), (), s32[]{:S(2)}) async-start(), calls=%async_computation.4 | async-start | bytes 8388608 | tf_op jit(solution)/shard_map/psum | solution.py:111
  285.0 0.7 copy-start.10
  287.8 73.2 %copy-start.8 = (f32[2048]{0:T(1024)S(1)}, f32[2048]{0:T(1024)}, u32[]{:S(2)}) copy-start(f32[2048]{0:T(1024)} %param.27) | copy-start | bytes 24580
  361.0 1.9 copy-start.4
  362.9 1.9 copy-start.2
  486.6 10.5 %copy-start.9 = (bf16[2048]{0:T(1024)(128)(2,1)S(1)}, bf16[2048]{0:T(1024)(128)(2,1)}, u32[]{:S(2)}) copy-start(bf16[2048]{0:T(1024)(128)(2,1)} %param.31) | copy-start | bytes 12292
  486.6 127.7 %all-to-all-start = ((bf16[128,10,2048]{2,1,0:T(8,128)(2,1)}), bf16[128,10,2048]{2,1,0:T(8,128)(2,1)}, u32[]{:S(2)}, u32[]{:S(2)}) async-start(bf16[128,10,2048]{2,1,0:T(8,128)(2,1)} %bitcast.143), calls=%async_computation.1 | async-start | bytes 16777216 | tf_op jit(solution)/shard_map/all_to_all | solution.py:148
  497.1 301.5 %reduce-scatter.2.cloned.1.call-start = ((), (), s32[]{:S(2)}) async-start(), calls=%async_computation.5 | async-start | bytes 4718592 | tf_op jit(solution)/shard_map/reduce_scatter | solution.py:126
  497.1 3.6 copy-start.3
  624.2 7.5 copy-start.5
  624.2 7.5 copy-start.14
  651.5 6.2 copy-start.11
  651.5 6.3 copy-start.13
  651.5 111.7 %all-to-all-start.1 = ((bf16[128,10,2048]{2,1,0:T(8,128)(2,1)}), bf16[128,10,2048]{2,1,0:T(8,128)(2,1)}, u32[]{:S(2)}, u32[]{:S(2)}) async-start(bf16[128,10,2048]{2,1,0:T(8,128)(2,1)} %reshape.250), calls=%async_computation.2 | async-start | bytes 16777216 | tf_op jit(solution)/shard_map/all_to_all | solution.py:155
Sparse Core Ops, SparseCore 0:
  9.7 35.6 all-gather.8
  53.9 51.1 all-gather.12
  107.8 50.8 all-gather.10
  285.2 70.2 all-reduce.1
  514.6 90.3 reduce-scatter.1
where the time goes:
time: 824 us; the launch traced here: 808 us
  waiting for transfers between devices  241 us (29%)
  local copies, waits for them, and re-layouts  190 us (23%)
  blocking collectives  157 us (19%)
  matrix products  132 us (16%)
  other arithmetic  55.8 us (7%)
  starting transfers between devices  16.8 us (2%)
  between operations  14.3 us (2%)
    scatter x2, local copies, waits for them, and re-layouts, per_device(): single = jnp.zeros((experts, capacity, D), jnp.bfloat16).at[flat_ids, slo...  110 us
    all_to_all x1, waiting for transfers between devices, per_device(): lax.all_to_all(outgoing, ('blk', 'exp'), split_axis=0, concat_axis=0, til...  99.9 us
    all_gather x1, blocking collectives, per_device(): lax.all_gather(cache_slots, 'exp', axis=0, tiled=True)  96.8 us
    psum x1, waiting for transfers between devices, per_device(): lax.psum(jnp.dot(heads_out, local_output, preferred_element_type=jnp.floa...  67.7 us
    dot_general x16, matrix products, attend(): jnp.einsum('hqk,khd->hqd', probs.astype(jnp.bfloat16), block_values, pref...  44.7 us
    dot_general x16, matrix products, attend(): jnp.einsum('qhd,khd->hqk', query_heads, block_keys, preferred_element_typ...  37.8 us
    all_gather x1, waiting for transfers between devices, per_device(): lax.all_gather(stream, 'exp', axis=0, tiled=True)  37.4 us
    all_gather x1, waiting for transfers between devices, per_device(): lax.all_gather(key_heads, 'blk', axis=0, tiled=True)  35.6 us
  transfers between devices with their start and end apart: 7, of which 4 were waited for; matrix products, arithmetic and copies ran while one was open for 14% of the time, Pallas kernels for 0%

commit v1 on v0

--- a/solution.py
+++ b/solution.py
@@ -42,12 +42,16 @@
     cache_slots,
 ):
     local_rows = stream.shape[0]
-    group_stream, group_position, group_segment, group_slot = (
-        lax.all_gather(stream, "exp", axis=0, tiled=True),
-        lax.all_gather(positions, "exp", axis=0, tiled=True),
-        lax.all_gather(segment_ids, "exp", axis=0, tiled=True),
-        lax.all_gather(cache_slots, "exp", axis=0, tiled=True),
-    )
+    n_exp = lax.axis_size("exp")
+    meta = jnp.stack([positions, segment_ids, cache_slots]).astype(jnp.float32)
+    meta_all = lax.all_gather(meta, ("blk", "exp"), axis=0)
+    all_position = meta_all[:, 0, :].reshape(-1).astype(jnp.int32)
+    all_segment = meta_all[:, 1, :].reshape(-1).astype(jnp.int32)
+    meta_group = lax.dynamic_slice_in_dim(meta_all, lax.axis_index("blk") * n_exp, n_exp, 0)
+    group_position = meta_group[:, 0, :].reshape(-1).astype(jnp.int32)
+    group_segment = meta_group[:, 1, :].reshape(-1).astype(jnp.int32)
+    group_slot = meta_group[:, 2, :].reshape(-1).astype(jnp.int32)
+    group_stream = lax.all_gather(stream, "exp", axis=0, tiled=True)
     group_size = group_stream.shape[0]
     normed = rms_norm(group_stream, norm_gain)
     queries = jnp.dot(normed, query_weight, preferred_element_type=jnp.float32).astype(jnp.bfloat16)
@@ -95,8 +99,8 @@
     piece = (
         lax.all_gather(key_heads, "blk", axis=0, tiled=True),
         lax.all_gather(value_heads, "blk", axis=0, tiled=True),
-        lax.all_gather(group_position, "blk", axis=0, tiled=True),
-        lax.all_gather(group_segment, "blk", axis=0, tiled=True),
+        all_position,
+        all_segment,
     )
     piece_rows = piece[0].shape[0]
     block = math.gcd(piece_rows, 1024)
@@ -136,14 +140,18 @@
     flat_ids = expert_ids.reshape(-1)
     onehot = (flat_ids[:, None] == jnp.arange(experts, dtype=jnp.int32)[None, :]).astype(jnp.int32)
     slots = jnp.sum(onehot * (jnp.cumsum(onehot, axis=0) - 1), axis=1)
-    pair_token = jnp.arange(local_rows * TOP, dtype=jnp.int32) // TOP
-    single = (
-        jnp.zeros((experts, capacity, D), jnp.bfloat16)
-        .at[flat_ids, slots]
-        .set(normed_local[pair_token])
-    )
-    outgoing = jnp.broadcast_to(single[:, None], (experts, 2, capacity, D)).reshape(
-        2 * experts, capacity, D
+    target = flat_ids * capacity + slots
+    slot_ids = jnp.arange(experts * capacity, dtype=jnp.int32)
+    pick = jnp.any(
+        (target[None, :] == slot_ids[:, None]).reshape(experts * capacity, local_rows, TOP), axis=2
+    )
+    pick = jnp.broadcast_to(
+        pick.reshape(experts, 1, capacity, local_rows), (experts, 2, capacity, local_rows)
+    ).reshape(2 * experts * capacity, local_rows)
+    outgoing = (
+        jnp.dot(pick.astype(jnp.bfloat16), normed_local, preferred_element_type=jnp.float32)
+        .astype(jnp.bfloat16)
+        .reshape(2 * experts, capacity, D)
     )
     arrived = lax.all_to_all(outgoing, ("blk", "exp"), split_axis=0, concat_axis=0, tiled=True)
     leading = arrived.shape[:-1]
@@ -161,11 +169,12 @@
         concat_axis=0,
         tiled=True,
     )
-    halves = returned.reshape(experts, 2, capacity, D)
-    combined = (halves[:, 0].astype(jnp.float32) + halves[:, 1].astype(jnp.float32)).reshape(
-        experts * capacity, D
-    )
-    picked = combined[flat_ids * capacity + slots] * route_weights.reshape(-1)[:, None]
+    column = jnp.arange(2 * experts * capacity, dtype=jnp.int32)
+    column_target = column // (2 * capacity) * capacity + column % capacity
+    gather_pick = (target[:, None] == column_target[None, :]).astype(jnp.bfloat16)
+    picked = jnp.dot(
+        gather_pick, returned.reshape(-1, D), preferred_element_type=jnp.float32
+    ) * route_weights.reshape(-1)[:, None]
     routed = jnp.sum(picked.reshape(local_rows, TOP, D), axis=1)
     final = (resid_local.astype(jnp.float32) + shared_local + routed).astype(jnp.bfloat16)
     return (final, cache_keys, cache_values)

time: 824 us -> 697 us (0.85)
  blocking collectives: 157 us -> 36.5 us
  local copies, waits for them, and re-layouts: 190 us -> 72.9 us
  waiting for transfers between devices: 241 us -> 352 us
  matrix products: 132 us -> 143 us
    all_gather x5 -> x1, blocking collectives: 157 us -> 36.5 us  [per_device(): meta_all = lax.all_gather(meta, ('blk', 'exp'), axis=0)]
    scatter x2 -> x0, local copies, waits for them, and re-layouts: 110 us -> none  [per_device(): single = jnp.zeros((experts, capacity, D), jnp.bfloat16).at[flat_ids, slo...]
    all_to_all x1, waiting for transfers between devices: 0.01 us -> 89.6 us  [per_device(): lax.all_to_all(jnp.dot(hidden, expert_down[0], preferred_element_type=jnp...]
    reshape x2 -> x4, local copies, waits for them, and re-layouts: 0.65 us -> 24.7 us  [the longest x1 9.84 us: per_device(): returned.reshape(-1, D)]
    all_gather x1, waiting for transfers between devices: 35.6 us -> 53.7 us  [per_device(): lax.all_gather(key_heads, 'blk', axis=0, tiled=True)]
    gather x3 -> x0, local copies, waits for them, and re-layouts: 16.4 us -> none  [the longest x2 13.1 us: per_device(): combined[flat_ids * capacity + slots] * route_weights.reshape(-1)[:, None]]
    dot_general x0 -> x2, matrix products: none -> 10.8 us  [the longest x1 7.01 us: per_device(): jnp.dot(gather_pick, returned.reshape(-1, D), preferred_element_type=jnp....]
    add x1 -> x3, other arithmetic: 8.62 us -> 0.02 us  [the longest x2 0.01 us: per_device(): target = flat_ids * capacity + slots]
  transfers between devices with their start and end apart: 7 -> 7, of which waited for: 4 -> 6; matrix products, arithmetic and copies ran while one was open for 14% -> 15% of each run, Pallas kernels for 0% -> 0%
where the time goes in v1:
time: 697 us; the launch traced here: 686 us
  waiting for transfers between devices  352 us (51%)
  matrix products  143 us (21%)
  local copies, waits for them, and re-layouts  72.9 us (10%)
  other arithmetic  48.8 us (7%)
  blocking collectives  36.5 us (5%)
  starting transfers between devices  17.4 us (2%)
  between operations  14.6 us (2%)
    all_to_all x1, waiting for transfers between devices, per_device(): lax.all_to_all(outgoing, ('blk', 'exp'), split_axis=0, concat_axis=0, til...  99.7 us
    all_to_all x1, waiting for transfers between devices, per_device(): lax.all_to_all(jnp.dot(hidden, expert_down[0], preferred_element_type=jnp...  89.6 us
    psum x1, waiting for transfers between devices, per_device(): lax.psum(jnp.dot(heads_out, local_output, preferred_element_type=jnp.floa...  67.2 us
    all_gather x1, waiting for transfers between devices, per_device(): lax.all_gather(key_heads, 'blk', axis=0, tiled=True)  53.7 us
    dot_general x16, matrix products, attend(): jnp.einsum('hqk,khd->hqd', probs.astype(jnp.bfloat16), block_values, pref...  44.8 us
    dot_general x16, matrix products, attend(): jnp.einsum('qhd,khd->hqk', query_heads, block_keys, preferred_element_typ...  37.8 us
    all_gather x1, waiting for transfers between devices, per_device(): group_stream = lax.all_gather(stream, 'exp', axis=0, tiled=True)  37.4 us
    all_gather x1, blocking collectives, per_device(): meta_all = lax.all_gather(meta, ('blk', 'exp'), axis=0)  36.5 us
  transfers between devices with their start and end apart: 7, of which 6 were waited for; matrix products, arithmetic and copies ran while one was open for 15% of the time, Pallas kernels for 0%

profile of v1, /device:TPU:1, one launch (start us, length us, event | category | flops | bytes accessed | tf_op | source)
XLA Modules:
  0.0 686.5 jit_solution(2239836811700021711)
XLA Ops:
  8.0 37.4 %all-gather.6.cloned.1.call-done = bf16[1024,2048]{1,0:T(8,128)(2,1)} async-done(((bf16[128,2048]{1,0:T(8,128)(2,1)}), bf16[1024,2048]{1,0:T(8,128)(2,1)}) %all-gather.6.cloned.1.call-update) | async-done | bytes 4194320 | tf_op jit(solution)/shard_map/all_gather | solution.py:54
  58.1 36.5 %all_gather.14 = f32[128,3,128]{2,1,0:T(4,128)S(1)} all-gather(f32[1,3,128]{2,1,0:T(4,128)S(1)} %add_convert_fusion.1), channel_id=1, replica_groups=mesh['blk'=16,'exp'=8] {'blk','exp'}, dimensions={0}, use_global_device_ids=true | all-gather | bytes 198144 | tf_op jit(solution)/shard_map/all_gather | solution.py:47
  97.2 4.4 fusion.41
  105.1 53.7 %all-gather.8.cloned.1.call-done = bf16[16384,128]{1,0:T(8,128)(2,1)} async-done(((bf16[1024,128]{1,0:T(8,128)(2,1)}), bf16[16384,128]{1,0:T(8,128)(2,1)}) %all-gather.8.cloned.1.call-update) | async-done | bytes 4194320 | tf_op jit(solution)/shard_map/all_gather | solution.py:100
  158.8 122.2 %while.15 = (s32[]{:T(128)}, f32[1,1024]{1,0:T(1,128)S(1)}, f32[1,1024]{1,0:T(1,128)S(1)}, f32[1,1024,128]{2,1,0:T(8,128)S(1)}, s32[16,1024]{1,0:T(8,128)S(1)}, ...) while((s32[]{:T(128)}, f32[1,1024]{1,0:T(1,128)S(1)}, ...), condition=%wide.region_4.5_spmd.clone, body=%wide.region_1.4_spmd.clone.sunk | while | flops 560337920 | bytes 14549149 | solution.py:109
  281.0 4.3 convolution_convert_fusion.2
  288.7 67.2 %all-reduce.2.cloned.1.call-done = bf16[1024,2048]{1,0:T(8,128)(2,1)} async-done(((bf16[1024,2048]{1,0:T(8,128)(2,1)}), bf16[1024,2048]{1,0:T(8,128)(2,1)}) %all-reduce.2.cloned.1.call-update) | async-done | bytes 4194320 | tf_op jit(solution)/shard_map/psum | solution.py:115
  355.8 5.5 fusion.25
  369.0 9.5 %reshape.245 = bf16[128,10,2048]{2,1,0:T(8,128)(2,1)} reshape(bf16[1280,2048]{1,0:T(8,128)(2,1)} %convolution_convert_fusion.1) | data formatting | bytes 10485760 | tf_op jit(solution)/shard_map/reshape | solution.py:154
  378.5 10.5 %all-to-all-start = ((bf16[128,10,2048]{2,1,0:T(8,128)(2,1)}), bf16[128,10,2048]{2,1,0:T(8,128)(2,1)}, u32[]{:S(2)}, u32[]{:S(2)}) async-start(bf16[128,10,2048]{2,1,0:T(8,128)(2,1)} %reshape.245), calls=%async_computation.1 | async-start | bytes 16777216 | tf_op jit(solution)/shard_map/all_to_all | solution.py:156
  392.7 4.9 fusion.69
  397.7 9.0 %multiply_convert_fusion = bf16[1024,2048]{1,0:T(8,128)(2,1)} fusion(bf16[384,2048]{1,0:T(8,128)(2,1)} %param.30, f32[1024]{0:T(1024)S(1)} %add_divide_fusion, f32[1024,384]{1,0:T(8,128)} %fusion.69, bf16[1024,2048]{1,0:T(8,128)(2,1)} %copy-done.2, bf16[2048,384]{1,0:T(8,128)(2,1)} %param.29), kind=kOutput, calls=%fused_computation.43 | convolution fusion | flops 3227779072 | bytes 13111296 | tf_op jit(solution)/shard_map/dot_general | solution.py:132
  406.7 99.7 %all-to-all-done = bf16[128,10,2048]{2,1,0:T(8,128)(2,1)} async-done(((bf16[128,10,2048]{2,1,0:T(8,128)(2,1)}), bf16[128,10,2048]{2,1,0:T(8,128)(2,1)}, u32[]{:S(2)}, u32[]{:S(2)}) %all-to-all-start) | async-done | bytes 5242912 | tf_op jit(solution)/shard_map/all_to_all | solution.py:156
  506.4 9.8 %reshape.246 = bf16[1280,2048]{1,0:T(8,128)(2,1)} reshape(bf16[128,10,2048]{2,1,0:T(8,128)(2,1)} %all-to-all-done) | data formatting | bytes 10485760 | tf_op jit(solution)/shard_map/reshape | solution.py:158
  516.2 7.4 %fusion.35 = f32[1280,704]{0,1:T(8,128)S(1)} fusion(bf16[1280,2048]{1,0:T(8,128)(2,1)} %reshape.246, bf16[1,2048,704]{1,2,0:T(8,128)(2,1)} %param.32), kind=kOutput, calls=%fused_computation.52 | convolution fusion | flops 3690987520 | bytes 11730944 | tf_op jit(solution)/shard_map/dot_general | solution.py:160
  523.7 4.2 fusion.32
  527.9 6.1 convolution_convert_fusion
  534.0 9.5 %reshape.247 = bf16[128,10,2048]{2,1,0:T(8,128)(2,1)} reshape(bf16[1280,2048]{1,0:T(8,128)(2,1)} %convolution_convert_fusion) | data formatting | bytes 10485760 | tf_op jit(solution)/shard_map/reshape | solution.py:166
  543.5 6.6 all-to-all-start.1
  559.5 89.6 %all-to-all-done.1 = bf16[128,10,2048]{2,1,0:T(8,128)(2,1)} async-done(((bf16[128,10,2048]{2,1,0:T(8,128)(2,1)}), bf16[128,10,2048]{2,1,0:T(8,128)(2,1)}, u32[]{:S(2)}, u32[]{:S(2)}) %all-to-all-start.1) | async-done | bytes 5242912 | tf_op jit(solution)/shard_map/all_to_all | solution.py:163
  649.1 9.8 %reshape.248 = bf16[1280,2048]{1,0:T(8,128)(2,1)} reshape(bf16[128,10,2048]{2,1,0:T(8,128)(2,1)} %all-to-all-done.1) | data formatting | bytes 10485760 | tf_op jit(solution)/shard_map/reshape | solution.py:176
  659.0 7.0 %convolution_multiply_fusion.1 = f32[512,2048]{1,0:T(8,128)} fusion(bf16[1280,2048]{1,0:T(8,128)(2,1)} %reshape.248, f32[512]{0:T(512)S(1)} %mul.154, s32[1280]{0:T(1024)S(1)} %fusion.59, s32[512]{0:T(512)S(1)} %multiply_add_fusion.1), kind=kOutput, calls=%fused_computation.49 | convolution fusion | flops 2686058496 | bytes 9446400 | tf_op jit(solution)/shard_map/dot_general | solution.py:175
  666.0 5.2 reshape.249
  671.2 5.8 reduce_sum.53
  (205 shorter events, 167.0 us)
Async XLA Ops:
  7.2 520.7 %copy-start = (bf16[1,704,2048]{2,1,0:T(8,128)(2,1)S(1)}, bf16[1,704,2048]{2,1,0:T(8,128)(2,1)}, u32[]{:S(2)}) copy-start(bf16[1,704,2048]{2,1,0:T(8,128)(2,1)} %param.34) | copy-start | bytes 8650756
  7.2 41.4 %copy-start.8 = (f32[2048]{0:T(1024)S(1)}, f32[2048]{0:T(1024)}, u32[]{:S(2)}) copy-start(f32[2048]{0:T(1024)} %param.22) | copy-start | bytes 24580
  7.2 38.2 %all-gather.6.cloned.1.call-start = ((), (), s32[]{:S(2)}) async-start(), calls=%async_computation.3 | async-start | bytes 4718592 | tf_op jit(solution)/shard_map/all_gather | solution.py:54
  7.9 97.2 %all-gather.10.cloned.1.call-start = ((), (), s32[]{:S(2)}) async-start(), calls=%async_computation.7 | async-start | bytes 4456448 | tf_op jit(solution)/shard_map/all_gather | solution.py:101
  45.4 3.4 copy-start.1
  48.8 3.0 copy-start.17
  49.8 2.0 copy-start.6
  51.8 2.0 copy-start.18
  53.7 4.3 copy-start.13
  53.7 4.4 copy-start.14
  53.8 4.4 copy-start.15
  53.8 105.0 %all-gather.8.cloned.1.call-start = ((), (), s32[]{:S(2)}) async-start(), calls=%async_computation.6 | async-start | bytes 4456448 | tf_op jit(solution)/shard_map/all_gather | solution.py:100
  58.0 297.8 %all-reduce.2.cloned.1.call-start = ((), (), s32[]{:S(2)}) async-start(), calls=%async_computation.4 | async-start | bytes 8388608 | tf_op jit(solution)/shard_map/psum | solution.py:115
  288.7 72.7 %copy-start.9 = (f32[2048]{0:T(1024)S(1)}, f32[2048]{0:T(1024)}, u32[]{:S(2)}) copy-start(f32[2048]{0:T(1024)} %param.27) | copy-start | bytes 24580
  361.3 1.9 copy-start.4
  363.2 2.0 copy-start.2
  378.5 10.6 %copy-start.11 = (bf16[2048]{0:T(1024)(128)(2,1)S(1)}, bf16[2048]{0:T(1024)(128)(2,1)}, u32[]{:S(2)}) copy-start(bf16[2048]{0:T(1024)(128)(2,1)} %param.31) | copy-start | bytes 12292
  378.5 127.8 %all-to-all-start = ((bf16[128,10,2048]{2,1,0:T(8,128)(2,1)}), bf16[128,10,2048]{2,1,0:T(8,128)(2,1)}, u32[]{:S(2)}, u32[]{:S(2)}) async-start(bf16[128,10,2048]{2,1,0:T(8,128)(2,1)} %reshape.245), calls=%async_computation.1 | async-start | bytes 16777216 | tf_op jit(solution)/shard_map/all_to_all | solution.py:156
  389.1 287.9 %reduce-scatter.2.cloned.1.call-start = ((), (), s32[]{:S(2)}) async-start(), calls=%async_computation.5 | async-start | bytes 4718592 | tf_op jit(solution)/shard_map/reduce_scatter | solution.py:130
  389.1 3.6 copy-start.3
  516.2 7.4 %copy-start.5 = (bf16[1280,2048]{1,0:T(8,128)(2,1)S(1)}, bf16[1280,2048]{1,0:T(8,128)(2,1)}, u32[]{:S(2)}) copy-start(bf16[1280,2048]{1,0:T(8,128)(2,1)} %reshape.246) | copy-start | bytes 15728644
  516.2 7.5 %copy-start.16 = (bf16[1,2048,704]{1,2,0:T(8,128)(2,1)S(1)}, bf16[1,2048,704]{1,2,0:T(8,128)(2,1)}, u32[]{:S(2)}) copy-start(bf16[1,2048,704]{1,2,0:T(8,128)(2,1)} %param.33) | copy-start | bytes 8650756
  543.5 6.7 copy-start.12
  543.5 105.6 %all-to-all-start.1 = ((bf16[128,10,2048]{2,1,0:T(8,128)(2,1)}), bf16[128,10,2048]{2,1,0:T(8,128)(2,1)}, u32[]{:S(2)}, u32[]{:S(2)}) async-start(bf16[128,10,2048]{2,1,0:T(8,128)(2,1)} %reshape.247), calls=%async_computation.2 | async-start | bytes 16777216 | tf_op jit(solution)/shard_map/all_to_all | solution.py:163
  (2 other events, 1.4 us)
Sparse Core Ops, SparseCore 0:
  9.7 35.6 all-gather.5
  53.9 51.1 all-gather.9
  107.8 50.9 all-gather.7
  285.5 70.2 all-reduce.1
  406.8 90.1 reduce-scatter.1

commit v2 on v1

--- a/solution.py
+++ b/solution.py
@@ -3,7 +3,7 @@
 import jax
 import jax.numpy as jnp
 from jax import lax
-from jax.sharding import PartitionSpec as P
+from jax.sharding import Mesh, PartitionSpec as P
 
 D = 2048
 HD = 128
@@ -12,6 +12,8 @@
 
 EPS = 1e-06
 FLOOR_SCORE = -1e30
+EXP = ("x", "core")
+CHIPS = ("blk", "x")
 
 
 def rms_norm(rows, gain):
@@ -42,16 +44,16 @@
     cache_slots,
 ):
     local_rows = stream.shape[0]
-    n_exp = lax.axis_size("exp")
+    n_exp = lax.axis_size(EXP)
     meta = jnp.stack([positions, segment_ids, cache_slots]).astype(jnp.float32)
-    meta_all = lax.all_gather(meta, ("blk", "exp"), axis=0)
+    meta_all = lax.all_gather(meta, ("blk",) + EXP, axis=0)
     all_position = meta_all[:, 0, :].reshape(-1).astype(jnp.int32)
     all_segment = meta_all[:, 1, :].reshape(-1).astype(jnp.int32)
     meta_group = lax.dynamic_slice_in_dim(meta_all, lax.axis_index("blk") * n_exp, n_exp, 0)
     group_position = meta_group[:, 0, :].reshape(-1).astype(jnp.int32)
     group_segment = meta_group[:, 1, :].reshape(-1).astype(jnp.int32)
     group_slot = meta_group[:, 2, :].reshape(-1).astype(jnp.int32)
-    group_stream = lax.all_gather(stream, "exp", axis=0, tiled=True)
+    group_stream = lax.all_gather(stream, EXP, axis=0, tiled=True)
     group_size = group_stream.shape[0]
     normed = rms_norm(group_stream, norm_gain)
     queries = jnp.dot(normed, query_weight, preferred_element_type=jnp.float32).astype(jnp.bfloat16)
@@ -110,16 +112,14 @@
     highest, denom, summed = carry
     heads_out = (summed / denom[:, :, None]).astype(jnp.bfloat16)
     heads_out = jnp.transpose(heads_out, (1, 0, 2)).reshape(group_size, width)
-    owner = lax.axis_index("exp")
-    local_output = lax.dynamic_slice_in_dim(output_weight, owner * width, width, 0)
-    attended = lax.psum(
-        jnp.dot(heads_out, local_output, preferred_element_type=jnp.float32).astype(jnp.bfloat16),
-        "exp",
-    ).astype(jnp.float32)
-    resid_group = (group_stream.astype(jnp.float32) + attended).astype(jnp.bfloat16)
-    resid_local = lax.dynamic_slice_in_dim(resid_group, owner * local_rows, local_rows, 0)
-    normed_group = rms_norm(resid_group, post_gain)
-    normed_local = lax.dynamic_slice_in_dim(normed_group, owner * local_rows, local_rows, 0)
+    heads_local = lax.all_to_all(heads_out, EXP, split_axis=0, concat_axis=0, tiled=True)
+    heads_local = jnp.transpose(
+        heads_local.reshape(n_exp, local_rows, width), (1, 0, 2)
+    ).reshape(local_rows, n_exp * width)
+    attended = jnp.dot(heads_local, output_weight, preferred_element_type=jnp.float32)
+    resid_local = (stream.astype(jnp.float32) + attended).astype(jnp.bfloat16)
+    normed_local = rms_norm(resid_local, post_gain)
+    normed_group = lax.all_gather(normed_local, EXP, axis=0, tiled=True)
     hidden = (
         jax.nn.silu(jnp.dot(normed_group, shared_gate, preferred_element_type=jnp.float32))
         * jnp.dot(normed_group, shared_up, preferred_element_type=jnp.float32)
@@ -131,11 +131,11 @@
         (
             jnp.dot(hidden, shared_down, preferred_element_type=jnp.float32) * opening[:, None]
         ).astype(jnp.bfloat16),
-        "exp",
+        EXP,
         scatter_dimension=0,
         tiled=True,
     ).astype(jnp.float32)
-    experts = lax.axis_size(("blk", "exp")) // 2
+    experts = lax.axis_size(CHIPS)
     capacity = max(2, 5 * local_rows * TOP // (4 * experts))
     flat_ids = expert_ids.reshape(-1)
     onehot = (flat_ids[:, None] == jnp.arange(experts, dtype=jnp.int32)[None, :]).astype(jnp.int32)
@@ -145,64 +145,65 @@
     pick = jnp.any(
         (target[None, :] == slot_ids[:, None]).reshape(experts * capacity, local_rows, TOP), axis=2
     )
-    pick = jnp.broadcast_to(
-        pick.reshape(experts, 1, capacity, local_rows), (experts, 2, capacity, local_rows)
-    ).reshape(2 * experts * capacity, local_rows)
     outgoing = (
         jnp.dot(pick.astype(jnp.bfloat16), normed_local, preferred_element_type=jnp.float32)
         .astype(jnp.bfloat16)
-        .reshape(2 * experts, capacity, D)
-    )
-    arrived = lax.all_to_all(outgoing, ("blk", "exp"), split_axis=0, concat_axis=0, tiled=True)
+        .reshape(experts, capacity, D)
+    )
+    arrived = lax.all_to_all(outgoing, CHIPS, split_axis=0, concat_axis=0, tiled=True)
+    arrived = lax.all_gather(arrived, "core", axis=0)
     leading = arrived.shape[:-1]
     flat_rows = arrived.reshape(-1, D)
     hidden = (
         jax.nn.silu(jnp.dot(flat_rows, expert_gate[0], preferred_element_type=jnp.float32))
         * jnp.dot(flat_rows, expert_up[0], preferred_element_type=jnp.float32)
     ).astype(jnp.bfloat16)
-    returned = lax.all_to_all(
+    half_out = (
         jnp.dot(hidden, expert_down[0], preferred_element_type=jnp.float32)
         .astype(jnp.bfloat16)
-        .reshape(leading + (D,)),
-        ("blk", "exp"),
-        split_axis=0,
-        concat_axis=0,
-        tiled=True,
-    )
-    column = jnp.arange(2 * experts * capacity, dtype=jnp.int32)
-    column_target = column // (2 * capacity) * capacity + column % capacity
-    gather_pick = (target[:, None] == column_target[None, :]).astype(jnp.bfloat16)
+        .reshape(leading + (D,))
+    )
+    both_halves = lax.all_to_all(half_out, "core", split_axis=0, concat_axis=0, tiled=True)
+    summed_halves = (
+        both_halves[0].astype(jnp.float32) + both_halves[1].astype(jnp.float32)
+    ).astype(jnp.bfloat16)
+    returned = lax.all_to_all(summed_halves, CHIPS, split_axis=0, concat_axis=0, tiled=True)
+    gather_pick = (target[:, None] == slot_ids[None, :]).astype(jnp.bfloat16)
     picked = jnp.dot(
         gather_pick, returned.reshape(-1, D), preferred_element_type=jnp.float32
     ) * route_weights.reshape(-1)[:, None]
     routed = jnp.sum(picked.reshape(local_rows, TOP, D), axis=1)
+    routed = jnp.sum(picked.reshape(local_rows, TOP, D), axis=1)
     final = (resid_local.astype(jnp.float32) + shared_local + routed).astype(jnp.bfloat16)
     return (final, cache_keys, cache_values)
 
 
 def solution(mesh):
+    blk, exp = mesh.shape["blk"], mesh.shape["exp"]
+    chip_mesh = Mesh(mesh.devices.reshape(blk, exp // 2, 2), ("blk", "x", "core"))
+    rows = ("blk",) + EXP
     in_specs = (
-        P(("blk", "exp"), None),
-        P(),
-        P(None, "exp"),
-        P(None, "exp"),
-        P(None, "exp"),
-        P(),
-        P(),
-        P(None, "exp"),
-        P(None, "exp"),
-        P("exp", None),
-        P(),
-        P(("blk", "exp"), None, None),
-        P(("blk", "exp"), None, None),
-        P(("blk", "exp"), None, None),
-        P(("blk", "exp"), None),
-        P(("blk", "exp"), None),
-        P(("blk", "exp")),
-        P(("blk", "exp")),
-        P(("blk", "exp")),
-    )
-    out_specs = (P(("blk", "exp"), None), P("blk", "exp"), P("blk", "exp"))
+        P(rows, None),
+        P(),
+        P(None, EXP),
+        P(None, EXP),
+        P(None, EXP),
+        P(),
+        P(),
+        P(None, EXP),
+        P(None, EXP),
+        P(EXP, None),
+        P(),
+        P(rows, None, None),
+        P(rows, None, None),
+        P(rows, None, None),
+        P(rows, None),
+        P(rows, None),
+        P(rows),
+        P(rows),
+        P(rows),
+    )
+    out_specs = (P(rows, None), P("blk", EXP), P("blk", EXP))
     return jax.shard_map(
-        per_device, mesh=mesh, in_specs=in_specs, out_specs=out_specs, check_vma=False
-    )
+        per_device, mesh=chip_mesh, in_specs=in_specs, out_specs=out_specs, check_vma=False
+    )

time: 697 us -> 570 us (0.82)
  waiting for transfers between devices: 352 us -> 142 us
  blocking collectives: 36.5 us -> 123 us
  local copies, waits for them, and re-layouts: 72.9 us -> 84.7 us
  starting transfers between devices: 17.4 us -> 6.25 us
    all_to_all x2 -> x1, waiting for transfers between devices: 189 us -> 44.3 us  [per_device(): lax.all_to_all(summed_halves, CHIPS, split_axis=0, concat_axis=0, tiled=T...]
    all_to_all x0 -> x3, blocking collectives: none -> 86.8 us  [the longest x1 66.6 us: per_device(): lax.all_to_all(outgoing, CHIPS, split_axis=0, concat_axis=0, tiled=True)]
    psum x1 -> x0, waiting for transfers between devices: 67.2 us -> none  [per_device(): lax.psum(jnp.dot(heads_out, local_output, preferred_element_type=jnp.floa...]
    while x16 -> x80, local copies, waits for them, and re-layouts: 0.04 us -> 12.6 us
    dynamic_slice x16, local copies, waits for them, and re-layouts: 12.3 us -> 0.16 us  [per_device(): carry, _ = lax.scan(attend, carry, blocks)]
    all_to_all x2 -> x1, starting transfers between devices: 17.2 us -> 5.79 us  [per_device(): lax.all_to_all(summed_halves, CHIPS, split_axis=0, concat_axis=0, tiled=T...]
    all_gather x0 -> x1, local copies, waits for them, and re-layouts: none -> 9 us  [per_device(): arrived = lax.all_gather(arrived, 'core', axis=0)]
    all_gather x1 -> x3, waiting for transfers between devices: 37.4 us -> 37.4 us  [the longest x1 37.4 us: per_device(): group_stream = lax.all_gather(stream, EXP, axis=0, tiled=True)]
  transfers between devices with their start and end apart: 7 -> 7, of which waited for: 6 -> 4; matrix products, arithmetic and copies ran while one was open for 15% -> 23% of each run, Pallas kernels for 0% -> 0%
where the time goes in v2:
time: 570 us; the launch traced here: 560 us
  matrix products  143 us (25%)
  waiting for transfers between devices  142 us (25%)
  blocking collectives  123 us (22%)
  local copies, waits for them, and re-layouts  84.7 us (15%)
  other arithmetic  45 us (8%)
  between operations  14.7 us (3%)
  starting transfers between devices  6.25 us (1%)
    all_to_all x1, blocking collectives, per_device(): lax.all_to_all(outgoing, CHIPS, split_axis=0, concat_axis=0, tiled=True)  66.6 us
    all_gather x1, waiting for transfers between devices, per_device(): lax.all_gather(key_heads, 'blk', axis=0, tiled=True)  53.7 us
    dot_general x16, matrix products, attend(): jnp.einsum('hqk,khd->hqd', probs.astype(jnp.bfloat16), block_values, pref...  44.8 us
    all_to_all x1, waiting for transfers between devices, per_device(): lax.all_to_all(summed_halves, CHIPS, split_axis=0, concat_axis=0, tiled=T...  44.3 us
    dot_general x16, matrix products, attend(): jnp.einsum('qhd,khd->hqk', query_heads, block_keys, preferred_element_typ...  38.6 us
    all_gather x1, waiting for transfers between devices, per_device(): group_stream = lax.all_gather(stream, EXP, axis=0, tiled=True)  37.4 us
    all_gather x1, blocking collectives, per_device(): meta_all = lax.all_gather(meta, ('blk',) + EXP, axis=0)  36.5 us
    reduce_sum x16, other arithmetic, attend(): denom = denom * shrink + jnp.sum(probs, axis=2)  25.6 us
  transfers between devices with their start and end apart: 7, of which 4 were waited for; matrix products, arithmetic and copies ran while one was open for 23% of the time, Pallas kernels for 0%

profile of v2, /device:TPU:1, one launch (start us, length us, event | category | flops | bytes accessed | tf_op | source)
XLA Modules:
  0.0 559.6 jit_solution(8249165089885462816)
XLA Ops:
  8.0 37.4 %all-gather.9.cloned.1.call-done = bf16[1024,2048]{1,0:T(8,128)(2,1)} async-done(((bf16[128,2048]{1,0:T(8,128)(2,1)}), bf16[1024,2048]{1,0:T(8,128)(2,1)}) %all-gather.9.cloned.1.call-update) | async-done | bytes 4194320 | tf_op jit(solution)/shard_map/all_gather | solution.py:56
  58.2 36.5 %all_gather.22 = f32[128,3,128]{2,1,0:T(4,128)S(1)} all-gather(f32[1,3,128]{2,1,0:T(4,128)S(1)} %add_convert_fusion.2), channel_id=1, replica_groups=mesh['blk'=16,'x'=4,'core'=2] {'blk','x','core'}, dimensions={0}, use_global_device_ids=true | all-gather | bytes 198144 | tf_op jit(solution)/shard_map/all_gather | solution.py:49
  99.6 5.5 all-gather.15.cloned.1.call-done
  105.1 53.7 %all-gather.13.cloned.1.call-done = bf16[16384,128]{1,0:T(8,128)(2,1)} async-done(((bf16[1024,128]{1,0:T(8,128)(2,1)}), bf16[16384,128]{1,0:T(8,128)(2,1)}) %all-gather.13.cloned.1.call-update) | async-done | bytes 4194320 | tf_op jit(solution)/shard_map/all_gather | solution.py:102
  158.8 123.4 %while.15 = (s32[]{:T(128)}, f32[1,1024]{1,0:T(1,128)S(1)}, f32[1,1024]{1,0:T(1,128)S(1)}, f32[1,1024,128]{2,1,0:T(8,128)}, s32[16,1024]{1,0:T(8,128)S(1)}, /*in...) while((s32[]{:T(128)}, f32[1,1024]{1,0:T(1,128)S(1)}, ...), condition=%wide.region_4.5_spmd.clone, body=%wide.region_1.4_spmd.clone.sunk | while | flops 560337920 | bytes 18743508 | solution.py:111
  283.5 11.5 %all_to_all.24 = bf16[8,128,128]{2,1,0:T(8,128)(2,1)} all-to-all(bf16[8,128,128]{2,1,0:T(8,128)(2,1)S(1)} %bitcast.139), channel_id=1, replica_groups=mesh['blk'=16,'x'=4,'core'=2] {'x','core'}, dimensions={0} | all-to-all | bytes 524288 | tf_op jit(solution)/shard_map/all_to_all | solution.py:115
  307.9 5.5 reshape.230
  313.4 66.6 %all_to_all.25 = bf16[64,10,2048]{2,1,0:T(8,128)(2,1)S(1)} all-to-all(bf16[64,10,2048]{2,1,0:T(8,128)(2,1)} %reshape.230), channel_id=1, replica_groups=mesh['blk'=16,'x'=4,'core'=2] {'blk','x'}, dimensions={0} | all-to-all | bytes 5242880 | tf_op jit(solution)/shard_map/all_to_all | solution.py:153
  386.6 5.0 fusion.50
  391.6 10.0 %multiply_convert_fusion = bf16[1024,2048]{1,0:T(8,128)(2,1)} fusion(bf16[384,2048]{1,0:T(8,128)(2,1)} %param.30, f32[1024]{0:T(1024)S(1)} %add_divide_fusion, f32[1024,384]{1,0:T(8,128)} %fusion.50, bf16[1024,2048]{1,0:T(8,128)(2,1)} %all-gather.11.cloned.1.call-done, bf16[2048,384]{1,0:T(8,128)(2,1)} %param.29), kind=kOutput, calls=%fused_computation.36 | convolution fusion | flops 3227779072 | bytes 13111296 | tf_op jit(solution)/shard_map/dot_general | solution.py:132
  401.7 9.0 %copy.91 = bf16[128,10,2048]{2,1,0:T(8,128)(2,1)} copy(bf16[128,10,2048]{2,0,1:T(8,128)(2,1)} %all-gather.17.cloned.1.call-done) | data formatting | bytes 10485760 | tf_op jit(solution)/shard_map/all_gather | solution.py:154
  410.7 9.9 %reshape.231 = bf16[1280,2048]{1,0:T(8,128)(2,1)} reshape(bf16[128,10,2048]{2,1,0:T(8,128)(2,1)} %copy.91) | data formatting | bytes 10485760 | tf_op jit(solution)/shard_map/reshape | solution.py:156
  420.6 7.6 %fusion.31 = f32[1280,704]{0,1:T(8,128)S(1)} fusion(bf16[1280,2048]{1,0:T(8,128)(2,1)} %reshape.231, bf16[1,2048,704]{1,2,0:T(8,128)(2,1)} %param.32), kind=kOutput, calls=%fused_computation.45 | convolution fusion | flops 3690987520 | bytes 11730944 | tf_op jit(solution)/shard_map/dot_general | solution.py:158
  432.5 6.3 %convolution_convert_fusion = bf16[1280,2048]{1,0:T(8,128)(2,1)} fusion(bf16[1280,704]{0,1:T(8,128)(2,1)S(1)} %fusion.28, bf16[1,704,2048]{2,1,0:T(8,128)(2,1)S(1)} %copy-done), kind=kOutput, calls=%fused_computation.37 | convolution fusion | flops 3693608960 | bytes 9928704 | tf_op jit(solution)/shard_map/dot_general | solution.py:162
  438.7 9.6 %reshape.232 = bf16[2,64,10,2048]{3,2,1,0:T(8,128)(2,1)} reshape(bf16[1280,2048]{1,0:T(8,128)(2,1)} %convolution_convert_fusion) | data formatting | bytes 10485760 | tf_op jit(solution)/shard_map/reshape | solution.py:164
  448.3 6.3 %copy.92 = bf16[2,64,10,2048]{3,1,2,0:T(8,128)(2,1)S(1)} copy(bf16[2,64,10,2048]{3,2,1,0:T(8,128)(2,1)} %reshape.232) | data formatting | bytes 10485760 | tf_op jit(solution)/shard_map/reshape | solution.py:164
  454.6 8.8 %all_to_all.26 = bf16[2,64,10,2048]{3,1,2,0:T(8,128)(2,1)S(1)} all-to-all(bf16[2,64,10,2048]{3,1,2,0:T(8,128)(2,1)S(1)} %copy.92), channel_id=1, replica_groups=mesh['blk'=16,'x'=4,'core'=2] {'core'}, dimensions={0} | all-to-all | bytes 10485760 | tf_op jit(solution)/shard_map/all_to_all | solution.py:166
  468.1 5.8 %all-to-all-start.3 = ((bf16[64,10,2048]{2,1,0:T(8,128)(2,1)}), bf16[64,10,2048]{2,1,0:T(8,128)(2,1)}, u32[]{:S(2)}, u32[]{:S(2)}) async-start(bf16[64,10,2048]{2,1,0:T(8,128)(2,1)} %copy.93), calls=%async_computation.4 | async-start | bytes 8388608 | tf_op jit(solution)/shard_map/all_to_all | solution.py:170
  479.1 4.4 scatter_custom_fusion.1
  483.5 44.3 %all-to-all-done.3 = bf16[64,10,2048]{2,1,0:T(8,128)(2,1)} async-done(((bf16[64,10,2048]{2,1,0:T(8,128)(2,1)}), bf16[64,10,2048]{2,1,0:T(8,128)(2,1)}, u32[]{:S(2)}, u32[]{:S(2)}) %all-to-all-start.3) | async-done | bytes 2621472 | tf_op jit(solution)/shard_map/all_to_all | solution.py:170
  527.8 5.6 reshape.233
  533.4 5.5 convolution_multiply_fusion.1
  538.9 5.2 reshape.234
  544.1 5.8 %reduce_sum.53 = f32[128,2048]{1,0:T(8,128)} reduce(f32[128,4,2048]{2,1,0:T(4,128)} %reshape.234, f32[]{:T(128)} %constant.23.clone.1), dimensions={1}, to_apply=%region_11.12 | reduce | flops 786432 | bytes 5242884 | tf_op jit(solution)/shard_map/reduce_sum | solution.py:176
  (273 shorter events, 178.2 us)
Async XLA Ops:
  7.2 425.3 %copy-start = (bf16[1,704,2048]{2,1,0:T(8,128)(2,1)S(1)}, bf16[1,704,2048]{2,1,0:T(8,128)(2,1)}, u32[]{:S(2)}) copy-start(bf16[1,704,2048]{2,1,0:T(8,128)(2,1)} %param.34) | copy-start | bytes 8650756
  7.2 41.4 %copy-start.10 = (f32[2048]{0:T(1024)S(1)}, f32[2048]{0:T(1024)}, u32[]{:S(2)}) copy-start(f32[2048]{0:T(1024)} %param.22) | copy-start | bytes 24580
  7.2 38.2 %all-gather.9.cloned.1.call-start = ((), (), s32[]{:S(2)}) async-start(), calls=%async_computation.5 | async-start | bytes 4718592 | tf_op jit(solution)/shard_map/all_gather | solution.py:56
  7.9 97.2 %all-gather.15.cloned.1.call-start = ((), (), s32[]{:S(2)}) async-start(), calls=%async_computation.9 | async-start | bytes 4456448 | tf_op jit(solution)/shard_map/all_gather | solution.py:103
  53.7 4.5 copy-start.15
  53.7 4.5 copy-start.16
  53.7 4.5 copy-start.17
  53.8 105.0 %all-gather.13.cloned.1.call-start = ((), (), s32[]{:S(2)}) async-start(), calls=%async_computation.8 | async-start | bytes 4456448 | tf_op jit(solution)/shard_map/all_gather | solution.py:102
  58.1 324.9 %all-gather.11.cloned.1.call-start = ((), (), s32[]{:S(2)}) async-start(), calls=%async_computation.6 | async-start | bytes 4718592 | tf_op jit(solution)/shard_map/all_gather | solution.py:122
  94.8 64.0 %copy-start.7 = (f32[128,3,128]{2,1,0:T(4,128)}, f32[128,3,128]{2,1,0:T(4,128)S(1)}, u32[]{:S(2)}) copy-start(f32[128,3,128]{2,1,0:T(4,128)S(1)} %all_gather.22) | copy-start | bytes 589828
  158.8 138.0 %copy-start.6 = (bf16[128,2048]{1,0:T(8,128)(2,1)S(1)}, bf16[128,2048]{1,0:T(8,128)(2,1)}, u32[]{:S(2)}) copy-start(bf16[128,2048]{1,0:T(8,128)(2,1)} %param.21) | copy-start | bytes 1572868
  158.8 4.1 copy-start.8
  174.3 4.1 copy-start.8
  182.0 4.1 copy-start.8
  189.7 4.1 copy-start.8
  236.0 4.1 copy-start.8
  282.2 18.7 %copy-start.11 = (f32[2048]{0:T(1024)S(1)}, f32[2048]{0:T(1024)}, u32[]{:S(2)}) copy-start(f32[2048]{0:T(1024)} %param.27) | copy-start | bytes 24580
  296.8 5.4 copy-start.12
  301.9 99.8 %all-gather.17.cloned.1.call-start = ((), (), s32[]{:S(2)}) async-start(), calls=%async_computation.10 | async-start | bytes 7864320 | tf_op jit(solution)/shard_map/all_gather | solution.py:154
  383.0 167.0 %reduce-scatter.2.cloned.1.call-start = ((), (), s32[]{:S(2)}) async-start(), calls=%async_computation.7 | async-start | bytes 4718592 | tf_op jit(solution)/shard_map/reduce_scatter | solution.py:130
  420.6 7.6 %copy-start.4 = (bf16[1280,2048]{1,0:T(8,128)(2,1)S(1)}, bf16[1280,2048]{1,0:T(8,128)(2,1)}, u32[]{:S(2)}) copy-start(bf16[1280,2048]{1,0:T(8,128)(2,1)} %reshape.231) | copy-start | bytes 15728644
  420.6 7.6 %copy-start.18 = (bf16[1,2048,704]{1,2,0:T(8,128)(2,1)S(1)}, bf16[1,2048,704]{1,2,0:T(8,128)(2,1)}, u32[]{:S(2)}) copy-start(bf16[1,2048,704]{1,2,0:T(8,128)(2,1)} %param.33) | copy-start | bytes 8650756
  468.1 5.8 %copy-start.14 = (f32[128,4]{0,1:T(4,128)S(1)}, f32[128,4]{0,1:T(4,128)}, u32[]{:S(2)}) copy-start(f32[128,4]{0,1:T(4,128)} %param.36) | copy-start | bytes 6148
  468.1 59.7 %all-to-all-start.3 = ((bf16[64,10,2048]{2,1,0:T(8,128)(2,1)}), bf16[64,10,2048]{2,1,0:T(8,128)(2,1)}, u32[]{:S(2)}, u32[]{:S(2)}) async-start(bf16[64,10,2048]{2,1,0:T(8,128)(2,1)} %copy.93), calls=%async_computation.4 | async-start | bytes 8388608 | tf_op jit(solution)/shard_map/all_to_all | solution.py:170
  (33 other events, 73.7 us)
Sparse Core Ops, SparseCore 0:
  9.7 35.6 all-gather.8
  53.9 51.1 all-gather.14
  107.8 50.9 all-gather.12
  302.0 45.0 all-gather.10
  383.1 14.2 all-gather.16
  401.8 33.7 reduce-scatter.1

commit v3 on v2

--- a/solution.py
+++ b/solution.py
@@ -136,7 +136,7 @@
         tiled=True,
     ).astype(jnp.float32)
     experts = lax.axis_size(CHIPS)
-    capacity = max(2, 5 * local_rows * TOP // (4 * experts))
+    capacity = -(-max(2, 5 * local_rows * TOP // (4 * experts)) // 16) * 16
     flat_ids = expert_ids.reshape(-1)
     onehot = (flat_ids[:, None] == jnp.arange(experts, dtype=jnp.int32)[None, :]).astype(jnp.int32)
     slots = jnp.sum(onehot * (jnp.cumsum(onehot, axis=0) - 1), axis=1)

time: 570 us -> 546 us (0.958)
  local copies, waits for them, and re-layouts: 84.7 us -> 32.9 us
  matrix products: 143 us -> 155 us
  blocking collectives: 123 us -> 134 us
    reshape x5 -> x0, local copies, waits for them, and re-layouts: 36.7 us -> none  [the longest x2 15.8 us: per_device(): half_out = jnp.dot(hidden, expert_down[0], preferred_element_type=jnp.flo...]
    dot_general x1, matrix products: 6.26 us -> 19.4 us  [per_device(): jnp.dot(hidden, expert_down[0], preferred_element_type=jnp.float32)]
    all_gather x1 -> x0, local copies, waits for them, and re-layouts: 9 us -> none  [per_device(): arrived = lax.all_gather(arrived, 'core', axis=0)]
    all_to_all x1, blocking collectives: 66.6 us -> 73 us  [per_device(): lax.all_to_all(outgoing, CHIPS, split_axis=0, concat_axis=0, tiled=True)]
  transfers between devices with their start and end apart: 7 -> 7, of which waited for: 4 -> 4; matrix products, arithmetic and copies ran while one was open for 23% -> 17% of each run, Pallas kernels for 0% -> 0%
where the time goes in v3:
time: 546 us; the launch traced here: 536 us
  matrix products  155 us (28%)
  waiting for transfers between devices  141 us (26%)
  blocking collectives  134 us (25%)
  other arithmetic  47 us (9%)
  local copies, waits for them, and re-layouts  32.9 us (6%)
  between operations  14.6 us (3%)
  starting transfers between devices  10.5 us (2%)
    all_to_all x1, blocking collectives, per_device(): lax.all_to_all(outgoing, CHIPS, split_axis=0, concat_axis=0, tiled=True)  73 us
    all_gather x1, waiting for transfers between devices, per_device(): lax.all_gather(key_heads, 'blk', axis=0, tiled=True)  53.7 us
    dot_general x16, matrix products, attend(): jnp.einsum('hqk,khd->hqd', probs.astype(jnp.bfloat16), block_values, pref...  44.8 us
    all_to_all x1, waiting for transfers between devices, per_device(): lax.all_to_all(summed_halves, CHIPS, split_axis=0, concat_axis=0, tiled=T...  43.9 us
    dot_general x16, matrix products, attend(): jnp.einsum('qhd,khd->hqk', query_heads, block_keys, preferred_element_typ...  38.6 us
    all_gather x1, waiting for transfers between devices, per_device(): group_stream = lax.all_gather(stream, EXP, axis=0, tiled=True)  37.4 us
    all_gather x1, blocking collectives, per_device(): meta_all = lax.all_gather(meta, ('blk',) + EXP, axis=0)  36.5 us
    reduce_sum x16, other arithmetic, attend(): denom = denom * shrink + jnp.sum(probs, axis=2)  25.6 us
  transfers between devices with their start and end apart: 7, of which 4 were waited for; matrix products, arithmetic and copies ran while one was open for 17% of the time, Pallas kernels for 0%

profile of v3, /device:TPU:1, one launch (start us, length us, event | category | flops | bytes accessed | tf_op | source)
XLA Modules:
  0.0 535.8 jit_solution(15133201243881351824)
XLA Ops:
  8.0 37.4 %all-gather.9.cloned.1.call-done = bf16[1024,2048]{1,0:T(8,128)(2,1)} async-done(((bf16[128,2048]{1,0:T(8,128)(2,1)}), bf16[1024,2048]{1,0:T(8,128)(2,1)}) %all-gather.9.cloned.1.call-update) | async-done | bytes 4194320 | tf_op jit(solution)/shard_map/all_gather | solution.py:56
  45.4 3.2 fusion.25
  53.8 4.3 convolution_convert_fusion.4
  58.2 36.5 %all_gather.22 = f32[128,3,128]{2,1,0:T(4,128)S(1)} all-gather(f32[1,3,128]{2,1,0:T(4,128)S(1)} %add_convert_fusion.2), channel_id=1, replica_groups=mesh['blk'=16,'x'=4,'core'=2] {'blk','x','core'}, dimensions={0}, use_global_device_ids=true | all-gather | bytes 198144 | tf_op jit(solution)/shard_map/all_gather | solution.py:49
  95.2 4.4 fusion.38
  99.6 5.5 %all-gather.15.cloned.1.call-done = bf16[16384,128]{1,0:T(8,128)(2,1)} async-done(((bf16[1024,128]{1,0:T(8,128)(2,1)}), bf16[16384,128]{1,0:T(8,128)(2,1)}) %all-gather.15.cloned.1.call-update) | async-done | bytes 4194320 | tf_op jit(solution)/shard_map/all_gather | solution.py:103
  105.1 53.7 %all-gather.13.cloned.1.call-done = bf16[16384,128]{1,0:T(8,128)(2,1)} async-done(((bf16[1024,128]{1,0:T(8,128)(2,1)}), bf16[16384,128]{1,0:T(8,128)(2,1)}) %all-gather.13.cloned.1.call-update) | async-done | bytes 4194320 | tf_op jit(solution)/shard_map/all_gather | solution.py:102
  158.8 123.4 %while.15 = (s32[]{:T(128)}, f32[1,1024]{1,0:T(1,128)S(1)}, f32[1,1024]{1,0:T(1,128)S(1)}, f32[1,1024,128]{2,1,0:T(8,128)}, s32[16,1024]{1,0:T(8,128)S(1)}, /*in...) while((s32[]{:T(128)}, f32[1,1024]{1,0:T(1,128)S(1)}, ...), condition=%wide.region_4.5_spmd.clone, body=%wide.region_1.4_spmd.clone.sunk | while | flops 560337920 | bytes 18743508 | solution.py:111
  283.5 11.5 %all_to_all.24 = bf16[8,128,128]{2,1,0:T(8,128)(2,1)} all-to-all(bf16[8,128,128]{2,1,0:T(8,128)(2,1)S(1)} %bitcast.145), channel_id=1, replica_groups=mesh['blk'=16,'x'=4,'core'=2] {'x','core'}, dimensions={0} | all-to-all | bytes 524288 | tf_op jit(solution)/shard_map/all_to_all | solution.py:115
  296.8 3.1 multiply_reduce_fusion
  307.1 73.0 %all_to_all.25 = bf16[64,16,2048]{2,1,0:T(8,128)(2,1)} all-to-all(bf16[64,16,2048]{2,1,0:T(8,128)(2,1)S(1)} %bitcast.140), channel_id=1, replica_groups=mesh['blk'=16,'x'=4,'core'=2] {'blk','x'}, dimensions={0} | all-to-all | bytes 8388608 | tf_op jit(solution)/shard_map/all_to_all | solution.py:153
  380.8 3.5 fusion.53
  384.3 5.2 fusion.52
  389.5 9.8 %multiply_convert_fusion = bf16[1024,2048]{1,0:T(8,128)(2,1)} fusion(bf16[384,2048]{1,0:T(8,128)(2,1)} %param.30, f32[1024]{0:T(1024)S(1)} %add_divide_fusion, f32[1024,384]{1,0:T(8,128)} %fusion.52, bf16[1024,2048]{1,0:T(8,128)(2,1)} %all-gather.11.cloned.1.call-done, bf16[2048,384]{1,0:T(8,128)(2,1)} %param.29), kind=kOutput, calls=%fused_computation.37 | convolution fusion | flops 3227779072 | bytes 13111296 | tf_op jit(solution)/shard_map/dot_general | solution.py:132
  399.4 11.1 %fusion.32 = f32[2048,704]{0,1:T(8,128)} fusion(bf16[2048,2048]{1,0:T(8,128)(2,1)} %bitcast.165, bf16[1,2048,704]{1,2,0:T(8,128)(2,1)} %param.32), kind=kOutput, calls=%fused_computation.45 | convolution fusion | flops 5905580032 | bytes 17039360 | tf_op jit(solution)/shard_map/dot_general | solution.py:158
  410.5 19.4 %convolution_convert_fusion = bf16[2048,2048]{1,0:T(8,128)(2,1)} fusion(f32[2048,704]{0,1:T(8,128)} %fusion.32, bf16[2048,2048]{1,0:T(8,128)(2,1)} %bitcast.166, bf16[1,704,2048]{2,1,0:T(8,128)(2,1)S(1)} %copy-done, bf16[1,2048,704]{1,2,0:T(8,128)(2,1)} %param.33), kind=kOutput, calls=%fused_computation.38 | convolution fusion | flops 11824005120 | bytes 28311552 | tf_op jit(solution)/shard_map/dot_general | solution.py:162
  429.9 12.6 %all_to_all.26 = bf16[2,64,16,2048]{3,2,1,0:T(8,128)(2,1)S(1)} all-to-all(bf16[2,64,16,2048]{3,2,1,0:T(8,128)(2,1)} %bitcast.141), channel_id=1, replica_groups=mesh['blk'=16,'x'=4,'core'=2] {'core'}, dimensions={0} | all-to-all | bytes 16777216 | tf_op jit(solution)/shard_map/all_to_all | solution.py:166
  445.5 9.9 %all-to-all-start.3 = ((bf16[64,16,2048]{2,1,0:T(8,128)(2,1)}), bf16[64,16,2048]{2,1,0:T(8,128)(2,1)}, u32[]{:S(2)}, u32[]{:S(2)}) async-start(bf16[64,16,2048]{2,1,0:T(8,128)(2,1)} %fusion.28), calls=%async_computation.4 | async-start | bytes 8388608 | tf_op jit(solution)/shard_map/all_to_all | solution.py:170
  456.4 4.2 scatter_custom_fusion
  460.6 4.2 scatter_custom_fusion.1
  464.7 43.9 %all-to-all-done.3 = bf16[64,16,2048]{2,1,0:T(8,128)(2,1)} async-done(((bf16[64,16,2048]{2,1,0:T(8,128)(2,1)}), bf16[64,16,2048]{2,1,0:T(8,128)(2,1)}, u32[]{:S(2)}, u32[]{:S(2)}) %all-to-all-start.3) | async-done | bytes 4194336 | tf_op jit(solution)/shard_map/all_to_all | solution.py:170
  508.6 6.5 %convolution_multiply_fusion = f32[512,2048]{1,0:T(8,128)} fusion(bf16[1024,2048]{1,0:T(8,128)(2,1)} %bitcast.23, f32[512]{0:T(512)S(1)} %mul.136, s32[512]{0:T(512)S(1)} %multiply_add_fusion.1), kind=kOutput, calls=%fused_computation.42 | convolution fusion | flops 2149056512 | bytes 8392704 | tf_op jit(solution)/shard_map/dot_general | solution.py:172
  515.1 5.2 reshape.234
  520.3 5.8 %reduce_sum.53 = f32[128,2048]{1,0:T(8,128)} reduce(f32[128,4,2048]{2,1,0:T(4,128)} %reshape.234, f32[]{:T(128)} %constant.23.clone.1), dimensions={1}, to_apply=%region_11.12 | reduce | flops 786432 | bytes 5242884 | tf_op jit(solution)/shard_map/reduce_sum | solution.py:176
  (260 shorter events, 146.3 us)
Async XLA Ops:
  7.2 403.3 %copy-start = (bf16[1,704,2048]{2,1,0:T(8,128)(2,1)S(1)}, bf16[1,704,2048]{2,1,0:T(8,128)(2,1)}, u32[]{:S(2)}) copy-start(bf16[1,704,2048]{2,1,0:T(8,128)(2,1)} %param.34) | copy-start | bytes 8650756
  7.2 41.4 %copy-start.9 = (f32[2048]{0:T(1024)S(1)}, f32[2048]{0:T(1024)}, u32[]{:S(2)}) copy-start(f32[2048]{0:T(1024)} %param.22) | copy-start | bytes 24580
  7.2 38.2 %all-gather.9.cloned.1.call-start = ((), (), s32[]{:S(2)}) async-start(), calls=%async_computation.5 | async-start | bytes 4718592 | tf_op jit(solution)/shard_map/all_gather | solution.py:56
  7.9 97.2 %all-gather.15.cloned.1.call-start = ((), (), s32[]{:S(2)}) async-start(), calls=%async_computation.9 | async-start | bytes 4456448 | tf_op jit(solution)/shard_map/all_gather | solution.py:103
  53.7 4.5 copy-start.14
  53.7 4.5 copy-start.15
  53.7 4.5 copy-start.16
  53.8 105.0 %all-gather.13.cloned.1.call-start = ((), (), s32[]{:S(2)}) async-start(), calls=%async_computation.8 | async-start | bytes 4456448 | tf_op jit(solution)/shard_map/all_gather | solution.py:102
  58.1 322.6 %all-gather.11.cloned.1.call-start = ((), (), s32[]{:S(2)}) async-start(), calls=%async_computation.6 | async-start | bytes 4718592 | tf_op jit(solution)/shard_map/all_gather | solution.py:122
  94.8 64.0 %copy-start.6 = (f32[128,3,128]{2,1,0:T(4,128)}, f32[128,3,128]{2,1,0:T(4,128)S(1)}, u32[]{:S(2)}) copy-start(f32[128,3,128]{2,1,0:T(4,128)S(1)} %all_gather.22) | copy-start | bytes 589828
  158.8 138.0 %copy-start.5 = (bf16[128,2048]{1,0:T(8,128)(2,1)S(1)}, bf16[128,2048]{1,0:T(8,128)(2,1)}, u32[]{:S(2)}) copy-start(bf16[128,2048]{1,0:T(8,128)(2,1)} %param.21) | copy-start | bytes 1572868
  158.8 4.1 copy-start.7
  166.6 4.1 copy-start.7
  174.3 4.1 copy-start.7
  182.0 4.1 copy-start.7
  228.3 4.1 copy-start.7
  236.0 4.1 copy-start.7
  243.7 4.1 copy-start.7
  282.2 18.6 %copy-start.10 = (f32[2048]{0:T(1024)S(1)}, f32[2048]{0:T(1024)}, u32[]{:S(2)}) copy-start(f32[2048]{0:T(1024)} %param.27) | copy-start | bytes 24580
  296.8 5.5 %copy-start.11 = (s32[128,4]{0,1:T(4,128)S(1)}, s32[128,4]{0,1:T(4,128)}, u32[]{:S(2)}) copy-start(s32[128,4]{0,1:T(4,128)} %param.35) | copy-start | bytes 6148
  301.9 97.5 %all-gather.17.cloned.1.call-start = ((), (), s32[]{:S(2)}) async-start(), calls=%async_computation.10 | async-start | bytes 12582912 | tf_op jit(solution)/shard_map/all_gather | solution.py:154
  380.1 146.1 %reduce-scatter.2.cloned.1.call-start = ((), (), s32[]{:S(2)}) async-start(), calls=%async_computation.7 | async-start | bytes 4718592 | tf_op jit(solution)/shard_map/reduce_scatter | solution.py:130
  445.5 10.0 %copy-start.13 = (f32[128,4]{0,1:T(4,128)S(1)}, f32[128,4]{0,1:T(4,128)}, u32[]{:S(2)}) copy-start(f32[128,4]{0,1:T(4,128)} %param.36) | copy-start | bytes 6148
  445.5 63.1 %all-to-all-start.3 = ((bf16[64,16,2048]{2,1,0:T(8,128)(2,1)}), bf16[64,16,2048]{2,1,0:T(8,128)(2,1)}, u32[]{:S(2)}, u32[]{:S(2)}) async-start(bf16[64,16,2048]{2,1,0:T(8,128)(2,1)} %fusion.28), calls=%async_computation.4 | async-start | bytes 8388608 | tf_op jit(solution)/shard_map/all_to_all | solution.py:170
  (31 other events, 63.2 us)
Sparse Core Ops, SparseCore 0:
  9.7 35.6 all-gather.8
  53.9 51.1 all-gather.14
  107.8 50.9 all-gather.12
  302.0 57.3 all-gather.10
  380.2 18.9 all-gather.16
  401.4 35.9 reduce-scatter.1

commit v4 on v3

--- a/solution.py
+++ b/solution.py
@@ -45,14 +45,11 @@
 ):
     local_rows = stream.shape[0]
     n_exp = lax.axis_size(EXP)
-    meta = jnp.stack([positions, segment_ids, cache_slots]).astype(jnp.float32)
-    meta_all = lax.all_gather(meta, ("blk",) + EXP, axis=0)
-    all_position = meta_all[:, 0, :].reshape(-1).astype(jnp.int32)
-    all_segment = meta_all[:, 1, :].reshape(-1).astype(jnp.int32)
-    meta_group = lax.dynamic_slice_in_dim(meta_all, lax.axis_index("blk") * n_exp, n_exp, 0)
-    group_position = meta_group[:, 0, :].reshape(-1).astype(jnp.int32)
-    group_segment = meta_group[:, 1, :].reshape(-1).astype(jnp.int32)
-    group_slot = meta_group[:, 2, :].reshape(-1).astype(jnp.int32)
+    meta = jnp.stack([positions, segment_ids, cache_slots]).astype(jnp.int32)
+    meta_group = lax.all_gather(meta, EXP, axis=0)
+    group_position = meta_group[:, 0, :].reshape(-1)
+    group_segment = meta_group[:, 1, :].reshape(-1)
+    group_slot = meta_group[:, 2, :].reshape(-1)
     group_stream = lax.all_gather(stream, EXP, axis=0, tiled=True)
     group_size = group_stream.shape[0]
     normed = rms_norm(group_stream, norm_gain)
@@ -97,18 +94,18 @@
     )
     key_heads = keys.reshape(group_size, local_heads, HD)
     value_heads = values.reshape(group_size, local_heads, HD)
-    carry = initial
-    piece = (
-        lax.all_gather(key_heads, "blk", axis=0, tiled=True),
-        lax.all_gather(value_heads, "blk", axis=0, tiled=True),
-        all_position,
-        all_segment,
-    )
-    piece_rows = piece[0].shape[0]
-    block = math.gcd(piece_rows, 1024)
-    count = piece_rows // block
-    blocks = tuple((member.reshape((count, block) + member.shape[1:]) for member in piece))
-    carry, _ = lax.scan(attend, carry, blocks)
+    n_blk = lax.axis_size("blk")
+    ring = [(i, (i + 1) % n_blk) for i in range(n_blk)]
+
+    def ring_step(state, _):
+        carry, block = state
+        carry, _ = attend(carry, block)
+        block = lax.ppermute(block, "blk", ring)
+        return ((carry, block), None)
+
+    block = (key_heads, value_heads, group_position, group_segment)
+    (carry, block), _ = lax.scan(ring_step, (initial, block), None, length=n_blk - 1)
+    carry, _ = attend(carry, block)
     highest, denom, summed = carry
     heads_out = (summed / denom[:, :, None]).astype(jnp.bfloat16)
     heads_out = jnp.transpose(heads_out, (1, 0, 2)).reshape(group_size, width)

time: 546 us -> 564 us (1.033)
  starting transfers between devices: 10.5 us -> 48.1 us
  local copies, waits for them, and re-layouts: 32.9 us -> 50.1 us
  waiting for transfers between devices: 141 us -> 124 us
  blocking collectives: 134 us -> 125 us
  matrix products: 155 us -> 148 us
    all_gather x2 -> x0, waiting for transfers between devices: 59.2 us -> none  [the longest x1 53.7 us: per_device(): lax.all_gather(key_heads, 'blk', axis=0, tiled=True)]
    ppermute x0 -> x60, waiting for transfers between devices: none -> 55.5 us  [ring_step(): block = lax.ppermute(block, 'blk', ring)]
    ppermute x0 -> x60, starting transfers between devices: none -> 38.1 us  [ring_step(): block = lax.ppermute(block, 'blk', ring)]
    all_gather x1, blocking collectives: 36.5 us -> 13.3 us  [per_device(): meta_group = lax.all_gather(meta, EXP, axis=0)]
    while x80 -> x135, local copies, waits for them, and re-layouts: 12.6 us -> 32.9 us
    all_to_all x1, blocking collectives: 11.5 us -> 26 us  [per_device(): lax.all_to_all(heads_out, EXP, split_axis=0, concat_axis=0, tiled=True)]
    all_gather x1, waiting for transfers between devices: 37.4 us -> 23.3 us  [per_device(): group_stream = lax.all_gather(stream, EXP, axis=0, tiled=True)]
  transfers between devices with their start and end apart: 7 -> 65, of which waited for: 4 -> 20; matrix products, arithmetic and copies ran while one was open for 17% -> 37% of each run, Pallas kernels for 0% -> 0%
where the time goes in v4:
time: 564 us; the launch traced here: 557 us
  matrix products  148 us (26%)
  blocking collectives  125 us (22%)
  waiting for transfers between devices  124 us (22%)
  local copies, waits for them, and re-layouts  50.1 us (9%)
  starting transfers between devices  48.1 us (9%)
  other arithmetic  45.4 us (8%)
  between operations  14.5 us (3%)
    all_to_all x1, blocking collectives, per_device(): lax.all_to_all(outgoing, CHIPS, split_axis=0, concat_axis=0, tiled=True)  73.4 us
    ppermute x60, waiting for transfers between devices, ring_step(): block = lax.ppermute(block, 'blk', ring)  55.5 us
    all_to_all x1, waiting for transfers between devices, per_device(): lax.all_to_all(summed_halves, CHIPS, split_axis=0, concat_axis=0, tiled=T...  44.5 us
    dot_general x16, matrix products, attend(): jnp.einsum('hqk,khd->hqd', probs.astype(jnp.bfloat16), block_values, pref...  43.9 us
    dot_general x16, matrix products, attend(): jnp.einsum('qhd,khd->hqk', query_heads, block_keys, preferred_element_typ...  38.6 us
    ppermute x60, starting transfers between devices, ring_step(): block = lax.ppermute(block, 'blk', ring)  38.1 us
    while x135, local copies, waits for them, and re-layouts  32.9 us
    all_to_all x1, blocking collectives, per_device(): lax.all_to_all(heads_out, EXP, split_axis=0, concat_axis=0, tiled=True)  26 us
  transfers between devices with their start and end apart: 65, of which 20 were waited for; matrix products, arithmetic and copies ran while one was open for 37% of the time, Pallas kernels for 0%

profile of v4, /device:TPU:1, one launch (start us, length us, event | category | flops | bytes accessed | tf_op | source)
XLA Modules:
  0.0 556.8 jit_solution(3946511828274063218)
XLA Ops:
  8.7 13.3 %all-gather.2 = s32[8,3,128]{2,1,0:T(4,128)S(1)} all-gather(s32[1,3,128]{2,1,0:T(4,128)S(1)} %add_bitcast_fusion.1), channel_id=2, replica_groups=mesh['blk'=16,'x'=4,'core'=2] {'x','core'}, dimensions={0}, use_global_device_ids=true | all-gather | bytes 13824 | tf_op jit(solution)/shard_map/all_gather | solution.py:49
  22.1 23.3 %all-gather.7.cloned.1.call-done = bf16[1024,2048]{1,0:T(8,128)(2,1)} async-done(((bf16[128,2048]{1,0:T(8,128)(2,1)}), bf16[1024,2048]{1,0:T(8,128)(2,1)}) %all-gather.7.cloned.1.call-update) | async-done | bytes 4194320 | tf_op jit(solution)/shard_map/all_gather | solution.py:53
  55.1 231.0 %while.23 = (s32[]{:T(128)}, f32[1,1024]{1,0:T(1,128)S(1)}, f32[1,1024]{1,0:T(1,128)S(1)}, f32[1,1024,128]{2,1,0:T(8,128)}, bf16[1024,1,128]{2,0,1:T(8,128)(2,1)...) while((s32[]{:T(128)}, f32[1,1024]{1,0:T(1,128)S(1)}, ...), condition=%wide.region_4.0_spmd.clone, body=%wide.region_1.4_spmd.clone.sunk | while | flops 560337920 | bytes 21922144 | solution.py:107
  69.0 5.6 %collective-permute-done.1 = bf16[1024,1,128]{2,0,1:T(8,128)(2,1)S(1)} collective-permute-done((bf16[1024,1,128]{2,0,1:T(8,128)(2,1)}, bf16[1024,1,128]{2,0,1:T(8,128)(2,1)S(1)}, u32[]{:S(2)}, u32[]{:S(2)}) %collective-permute-start.1) | collective-permute-done | bytes 262176 | tf_op jit(solution)/shard_map/while/body/eval_jaxpr/ppermute | solution.py:103
  101.7 4.4 collective-permute-done.1
  215.7 4.0 collective-permute-done.1
  231.8 5.6 %collective-permute-done.1 = bf16[1024,1,128]{2,0,1:T(8,128)(2,1)S(1)} collective-permute-done((bf16[1024,1,128]{2,0,1:T(8,128)(2,1)}, bf16[1024,1,128]{2,0,1:T(8,128)(2,1)S(1)}, u32[]{:S(2)}, u32[]{:S(2)}) %collective-permute-start.1) | collective-permute-done | bytes 262176 | tf_op jit(solution)/shard_map/while/body/eval_jaxpr/ppermute | solution.py:103
  248.8 5.6 %collective-permute-done.1 = bf16[1024,1,128]{2,0,1:T(8,128)(2,1)S(1)} collective-permute-done((bf16[1024,1,128]{2,0,1:T(8,128)(2,1)}, bf16[1024,1,128]{2,0,1:T(8,128)(2,1)S(1)}, u32[]{:S(2)}, u32[]{:S(2)}) %collective-permute-start.1) | collective-permute-done | bytes 262176 | tf_op jit(solution)/shard_map/while/body/eval_jaxpr/ppermute | solution.py:103
  265.0 5.6 %collective-permute-done.1 = bf16[1024,1,128]{2,0,1:T(8,128)(2,1)S(1)} collective-permute-done((bf16[1024,1,128]{2,0,1:T(8,128)(2,1)}, bf16[1024,1,128]{2,0,1:T(8,128)(2,1)S(1)}, u32[]{:S(2)}, u32[]{:S(2)}) %collective-permute-start.1) | collective-permute-done | bytes 262176 | tf_op jit(solution)/shard_map/while/body/eval_jaxpr/ppermute | solution.py:103
  280.2 5.8 %collective-permute-done.1 = bf16[1024,1,128]{2,0,1:T(8,128)(2,1)S(1)} collective-permute-done((bf16[1024,1,128]{2,0,1:T(8,128)(2,1)}, bf16[1024,1,128]{2,0,1:T(8,128)(2,1)S(1)}, u32[]{:S(2)}, u32[]{:S(2)}) %collective-permute-start.1) | collective-permute-done | bytes 262176 | tf_op jit(solution)/shard_map/while/body/eval_jaxpr/ppermute | solution.py:103
  291.8 26.0 %all_to_all.24 = bf16[8,128,128]{1,2,0:T(8,128)(2,1)S(1)} all-to-all(bf16[8,128,128]{1,2,0:T(8,128)(2,1)S(1)} %copy.48), channel_id=1, replica_groups=mesh['blk'=16,'x'=4,'core'=2] {'x','core'}, dimensions={0} | all-to-all | bytes 524288 | tf_op jit(solution)/shard_map/all_to_all | solution.py:112
  327.8 73.4 %all_to_all.25 = bf16[64,16,2048]{2,1,0:T(8,128)(2,1)} all-to-all(bf16[64,16,2048]{2,1,0:T(8,128)(2,1)S(1)} %bitcast.138), channel_id=1, replica_groups=mesh['blk'=16,'x'=4,'core'=2] {'blk','x'}, dimensions={0} | all-to-all | bytes 8388608 | tf_op jit(solution)/shard_map/all_to_all | solution.py:150
  405.4 5.2 fusion.68
  410.6 10.0 %multiply_convert_fusion = bf16[1024,2048]{1,0:T(8,128)(2,1)} fusion(bf16[384,2048]{1,0:T(8,128)(2,1)} %param.30, f32[1024]{0:T(1024)S(1)} %add_divide_fusion, f32[1024,384]{1,0:T(8,128)} %fusion.68, bf16[1024,2048]{1,0:T(8,128)(2,1)} %all-gather.9.cloned.1.call-done, bf16[2048,384]{1,0:T(8,128)(2,1)} %param.29), kind=kOutput, calls=%fused_computation.31 | convolution fusion | flops 3227779072 | bytes 13111296 | tf_op jit(solution)/shard_map/dot_general | solution.py:129
  420.6 11.0 %fusion.29 = f32[2048,704]{0,1:T(8,128)} fusion(bf16[2048,2048]{1,0:T(8,128)(2,1)} %bitcast.175, bf16[1,2048,704]{1,2,0:T(8,128)(2,1)} %param.32), kind=kOutput, calls=%fused_computation.43 | convolution fusion | flops 5905580032 | bytes 17039360 | tf_op jit(solution)/shard_map/dot_general | solution.py:155
  431.7 19.3 %convolution_convert_fusion = bf16[2048,2048]{1,0:T(8,128)(2,1)} fusion(f32[2048,704]{0,1:T(8,128)} %fusion.29, bf16[2048,2048]{1,0:T(8,128)(2,1)} %bitcast.176, bf16[1,704,2048]{2,1,0:T(8,128)(2,1)S(1)} %copy-done, bf16[1,2048,704]{1,2,0:T(8,128)(2,1)} %param.33), kind=kOutput, calls=%fused_computation.32 | convolution fusion | flops 11824005120 | bytes 28311552 | tf_op jit(solution)/shard_map/dot_general | solution.py:159
  451.0 12.7 %all_to_all.26 = bf16[2,64,16,2048]{3,2,1,0:T(8,128)(2,1)S(1)} all-to-all(bf16[2,64,16,2048]{3,2,1,0:T(8,128)(2,1)} %bitcast.139), channel_id=1, replica_groups=mesh['blk'=16,'x'=4,'core'=2] {'core'}, dimensions={0} | all-to-all | bytes 16777216 | tf_op jit(solution)/shard_map/all_to_all | solution.py:163
  466.6 9.9 %all-to-all-start.3 = ((bf16[64,16,2048]{2,1,0:T(8,128)(2,1)}), bf16[64,16,2048]{2,1,0:T(8,128)(2,1)}, u32[]{:S(2)}, u32[]{:S(2)}) async-start(bf16[64,16,2048]{2,1,0:T(8,128)(2,1)} %fusion.24), calls=%async_computation.4 | async-start | bytes 8388608 | tf_op jit(solution)/shard_map/all_to_all | solution.py:167
  476.8 4.2 scatter_custom_fusion
  481.0 4.2 scatter_custom_fusion.1
  485.1 44.5 %all-to-all-done.3 = bf16[64,16,2048]{2,1,0:T(8,128)(2,1)} async-done(((bf16[64,16,2048]{2,1,0:T(8,128)(2,1)}), bf16[64,16,2048]{2,1,0:T(8,128)(2,1)}, u32[]{:S(2)}, u32[]{:S(2)}) %all-to-all-start.3) | async-done | bytes 4194336 | tf_op jit(solution)/shard_map/all_to_all | solution.py:167
  529.6 6.5 %convolution_multiply_fusion = f32[512,2048]{1,0:T(8,128)} fusion(bf16[1024,2048]{1,0:T(8,128)(2,1)} %bitcast.29, f32[512]{0:T(512)S(1)} %mul.151, s32[512]{0:T(512)S(1)} %multiply_add_fusion.2), kind=kOutput, calls=%fused_computation.40 | convolution fusion | flops 2149056512 | bytes 8392704 | tf_op jit(solution)/shard_map/dot_general | solution.py:169
  536.2 5.2 reshape.213
  541.3 5.8 %reduce_sum.66 = f32[128,2048]{1,0:T(8,128)} reduce(f32[128,4,2048]{2,1,0:T(4,128)} %reshape.213, f32[]{:T(128)} %constant.15.clone.1), dimensions={1}, to_apply=%region_13.14 | reduce | flops 786432 | bytes 5242884 | tf_op jit(solution)/shard_map/reduce_sum | solution.py:173
  (411 shorter events, 229.8 us)
Async XLA Ops:
  7.2 38.2 %all-gather.7.cloned.1.call-start = ((), (), s32[]{:S(2)}) async-start(), calls=%async_computation.5 | async-start | bytes 4718592 | tf_op jit(solution)/shard_map/all_gather | solution.py:53
  7.9 393.9 %all-gather.9.cloned.1.call-start = ((), (), s32[]{:S(2)}) async-start(), calls=%async_computation.6 | async-start | bytes 4718592 | tf_op jit(solution)/shard_map/all_gather | solution.py:119
  55.2 13.7 %collective-permute-start.2 = (s32[1024]{0:T(1024)S(1)}, s32[1024]{0:T(1024)S(1)}, u32[]{:S(2)}, u32[]{:S(2)}) collective-permute-start(s32[1024]{0:T(1024)S(1)} %copy.70), channel_id=1, source_target_pairs={{0,8},{8,16},{16,24},{24,32},{32,40},{40,48},{48,56},{56,64},{64,7... | collective-permute-start | bytes 12296 | tf_op jit(solution)/shard_map/while/body/eval_jaxpr/ppermute | solution.py:103
  56.5 12.5 %collective-permute-start.3 = (s32[1024]{0:T(1024)S(1)}, s32[1024]{0:T(1024)S(1)}, u32[]{:S(2)}, u32[]{:S(2)}) collective-permute-start(s32[1024]{0:T(1024)S(1)} %copy.71), channel_id=1, source_target_pairs={{0,8},{8,16},{16,24},{24,32},{32,40},{40,48},{48,56},{56,64},{64,7... | collective-permute-start | bytes 12296 | tf_op jit(solution)/shard_map/while/body/eval_jaxpr/ppermute | solution.py:103
  60.0 14.6 %collective-permute-start.1 = (bf16[1024,1,128]{2,0,1:T(8,128)(2,1)}, bf16[1024,1,128]{2,0,1:T(8,128)(2,1)S(1)}, u32[]{:S(2)}, u32[]{:S(2)}) collective-permute-start(bf16[1024,1,128]{2,0,1:T(8,128)(2,1)} %copy.69), channel_id=1, source_target_pairs={{0,8},{8,16},{16,24},{24,32},{32,40},{40,48},{48,56},{56,64},{64,7... | collective-permute-start | bytes 786440 | tf_op jit(solution)/shard_map/while/body/eval_jaxpr/ppermute | solution.py:103
  74.6 12.5 %collective-permute-start.2 = (s32[1024]{0:T(1024)S(1)}, s32[1024]{0:T(1024)S(1)}, u32[]{:S(2)}, u32[]{:S(2)}) collective-permute-start(s32[1024]{0:T(1024)S(1)} %copy.70), channel_id=1, source_target_pairs={{0,8},{8,16},{16,24},{24,32},{32,40},{40,48},{48,56},{56,64},{64,7... | collective-permute-start | bytes 12296 | tf_op jit(solution)/shard_map/while/body/eval_jaxpr/ppermute | solution.py:103
  74.6 12.5 %collective-permute-start.3 = (s32[1024]{0:T(1024)S(1)}, s32[1024]{0:T(1024)S(1)}, u32[]{:S(2)}, u32[]{:S(2)}) collective-permute-start(s32[1024]{0:T(1024)S(1)} %copy.71), channel_id=1, source_target_pairs={{0,8},{8,16},{16,24},{24,32},{32,40},{40,48},{48,56},{56,64},{64,7... | collective-permute-start | bytes 12296 | tf_op jit(solution)/shard_map/while/body/eval_jaxpr/ppermute | solution.py:103
  76.1 14.8 %collective-permute-start.1 = (bf16[1024,1,128]{2,0,1:T(8,128)(2,1)}, bf16[1024,1,128]{2,0,1:T(8,128)(2,1)S(1)}, u32[]{:S(2)}, u32[]{:S(2)}) collective-permute-start(bf16[1024,1,128]{2,0,1:T(8,128)(2,1)} %copy.69), channel_id=1, source_target_pairs={{0,8},{8,16},{16,24},{24,32},{32,40},{40,48},{48,56},{56,64},{64,7... | collective-permute-start | bytes 786440 | tf_op jit(solution)/shard_map/while/body/eval_jaxpr/ppermute | solution.py:103
  92.4 13.7 %collective-permute-start.1 = (bf16[1024,1,128]{2,0,1:T(8,128)(2,1)}, bf16[1024,1,128]{2,0,1:T(8,128)(2,1)S(1)}, u32[]{:S(2)}, u32[]{:S(2)}) collective-permute-start(bf16[1024,1,128]{2,0,1:T(8,128)(2,1)} %copy.69), channel_id=1, source_target_pairs={{0,8},{8,16},{16,24},{24,32},{32,40},{40,48},{48,56},{56,64},{64,7... | collective-permute-start | bytes 786440 | tf_op jit(solution)/shard_map/while/body/eval_jaxpr/ppermute | solution.py:103
  107.6 12.9 %collective-permute-start.1 = (bf16[1024,1,128]{2,0,1:T(8,128)(2,1)}, bf16[1024,1,128]{2,0,1:T(8,128)(2,1)S(1)}, u32[]{:S(2)}, u32[]{:S(2)}) collective-permute-start(bf16[1024,1,128]{2,0,1:T(8,128)(2,1)} %copy.69), channel_id=1, source_target_pairs={{0,8},{8,16},{16,24},{24,32},{32,40},{40,48},{48,56},{56,64},{64,7... | collective-permute-start | bytes 786440 | tf_op jit(solution)/shard_map/while/body/eval_jaxpr/ppermute | solution.py:103
  159.6 14.3 %collective-permute-start.2 = (s32[1024]{0:T(1024)S(1)}, s32[1024]{0:T(1024)S(1)}, u32[]{:S(2)}, u32[]{:S(2)}) collective-permute-start(s32[1024]{0:T(1024)S(1)} %copy.70), channel_id=1, source_target_pairs={{0,8},{8,16},{16,24},{24,32},{32,40},{40,48},{48,56},{56,64},{64,7... | collective-permute-start | bytes 12296 | tf_op jit(solution)/shard_map/while/body/eval_jaxpr/ppermute | solution.py:103
  159.8 14.2 %collective-permute-start.3 = (s32[1024]{0:T(1024)S(1)}, s32[1024]{0:T(1024)S(1)}, u32[]{:S(2)}, u32[]{:S(2)}) collective-permute-start(s32[1024]{0:T(1024)S(1)} %copy.71), channel_id=1, source_target_pairs={{0,8},{8,16},{16,24},{24,32},{32,40},{40,48},{48,56},{56,64},{64,7... | collective-permute-start | bytes 12296 | tf_op jit(solution)/shard_map/while/body/eval_jaxpr/ppermute | solution.py:103
  161.5 12.5 %collective-permute-start = (bf16[1024,1,128]{2,0,1:T(8,128)(2,1)}, bf16[1024,1,128]{2,0,1:T(8,128)(2,1)S(1)}, u32[]{:S(2)}, u32[]{:S(2)}) collective-permute-start(bf16[1024,1,128]{2,0,1:T(8,128)(2,1)} %copy.68), channel_id=1, source_target_pairs={{0,8},{8,16},{16,24},{24,32},{32,40},{40,48},{48,56},{56,64},{64,7... | collective-permute-start | bytes 786440 | tf_op jit(solution)/shard_map/while/body/eval_jaxpr/ppermute | solution.py:103
  174.0 13.6 %collective-permute-start.2 = (s32[1024]{0:T(1024)S(1)}, s32[1024]{0:T(1024)S(1)}, u32[]{:S(2)}, u32[]{:S(2)}) collective-permute-start(s32[1024]{0:T(1024)S(1)} %copy.70), channel_id=1, source_target_pairs={{0,8},{8,16},{16,24},{24,32},{32,40},{40,48},{48,56},{56,64},{64,7... | collective-permute-start | bytes 12296 | tf_op jit(solution)/shard_map/while/body/eval_jaxpr/ppermute | solution.py:103
  174.2 13.5 %collective-permute-start.3 = (s32[1024]{0:T(1024)S(1)}, s32[1024]{0:T(1024)S(1)}, u32[]{:S(2)}, u32[]{:S(2)}) collective-permute-start(s32[1024]{0:T(1024)S(1)} %copy.71), channel_id=1, source_target_pairs={{0,8},{8,16},{16,24},{24,32},{32,40},{40,48},{48,56},{56,64},{64,7... | collective-permute-start | bytes 12296 | tf_op jit(solution)/shard_map/while/body/eval_jaxpr/ppermute | solution.py:103
  189.7 13.3 %collective-permute-start.1 = (bf16[1024,1,128]{2,0,1:T(8,128)(2,1)}, bf16[1024,1,128]{2,0,1:T(8,128)(2,1)S(1)}, u32[]{:S(2)}, u32[]{:S(2)}) collective-permute-start(bf16[1024,1,128]{2,0,1:T(8,128)(2,1)} %copy.69), channel_id=1, source_target_pairs={{0,8},{8,16},{16,24},{24,32},{32,40},{40,48},{48,56},{56,64},{64,7... | collective-permute-start | bytes 786440 | tf_op jit(solution)/shard_map/while/body/eval_jaxpr/ppermute | solution.py:103
  205.0 14.7 %collective-permute-start.1 = (bf16[1024,1,128]{2,0,1:T(8,128)(2,1)}, bf16[1024,1,128]{2,0,1:T(8,128)(2,1)S(1)}, u32[]{:S(2)}, u32[]{:S(2)}) collective-permute-start(bf16[1024,1,128]{2,0,1:T(8,128)(2,1)} %copy.69), channel_id=1, source_target_pairs={{0,8},{8,16},{16,24},{24,32},{32,40},{40,48},{48,56},{56,64},{64,7... | collective-permute-start | bytes 786440 | tf_op jit(solution)/shard_map/while/body/eval_jaxpr/ppermute | solution.py:103
  221.2 16.2 %collective-permute-start.1 = (bf16[1024,1,128]{2,0,1:T(8,128)(2,1)}, bf16[1024,1,128]{2,0,1:T(8,128)(2,1)S(1)}, u32[]{:S(2)}, u32[]{:S(2)}) collective-permute-start(bf16[1024,1,128]{2,0,1:T(8,128)(2,1)} %copy.69), channel_id=1, source_target_pairs={{0,8},{8,16},{16,24},{24,32},{32,40},{40,48},{48,56},{56,64},{64,7... | collective-permute-start | bytes 786440 | tf_op jit(solution)/shard_map/while/body/eval_jaxpr/ppermute | solution.py:103
  238.9 15.5 %collective-permute-start.1 = (bf16[1024,1,128]{2,0,1:T(8,128)(2,1)}, bf16[1024,1,128]{2,0,1:T(8,128)(2,1)S(1)}, u32[]{:S(2)}, u32[]{:S(2)}) collective-permute-start(bf16[1024,1,128]{2,0,1:T(8,128)(2,1)} %copy.69), channel_id=1, source_target_pairs={{0,8},{8,16},{16,24},{24,32},{32,40},{40,48},{48,56},{56,64},{64,7... | collective-permute-start | bytes 786440 | tf_op jit(solution)/shard_map/while/body/eval_jaxpr/ppermute | solution.py:103
  255.9 14.7 %collective-permute-start.1 = (bf16[1024,1,128]{2,0,1:T(8,128)(2,1)}, bf16[1024,1,128]{2,0,1:T(8,128)(2,1)S(1)}, u32[]{:S(2)}, u32[]{:S(2)}) collective-permute-start(bf16[1024,1,128]{2,0,1:T(8,128)(2,1)} %copy.69), channel_id=1, source_target_pairs={{0,8},{8,16},{16,24},{24,32},{32,40},{40,48},{48,56},{56,64},{64,7... | collective-permute-start | bytes 786440 | tf_op jit(solution)/shard_map/while/body/eval_jaxpr/ppermute | solution.py:103
  272.1 14.0 %collective-permute-start.1 = (bf16[1024,1,128]{2,0,1:T(8,128)(2,1)}, bf16[1024,1,128]{2,0,1:T(8,128)(2,1)S(1)}, u32[]{:S(2)}, u32[]{:S(2)}) collective-permute-start(bf16[1024,1,128]{2,0,1:T(8,128)(2,1)} %copy.69), channel_id=1, source_target_pairs={{0,8},{8,16},{16,24},{24,32},{32,40},{40,48},{48,56},{56,64},{64,7... | collective-permute-start | bytes 786440 | tf_op jit(solution)/shard_map/while/body/eval_jaxpr/ppermute | solution.py:103
  322.9 97.7 %all-gather.11.cloned.1.call-start = ((), (), s32[]{:S(2)}) async-start(), calls=%async_computation.8 | async-start | bytes 12582912 | tf_op jit(solution)/shard_map/all_gather | solution.py:151
  401.2 146.0 %reduce-scatter.2.cloned.1.call-start = ((), (), s32[]{:S(2)}) async-start(), calls=%async_computation.7 | async-start | bytes 4718592 | tf_op jit(solution)/shard_map/reduce_scatter | solution.py:127
  466.6 63.0 %all-to-all-start.3 = ((bf16[64,16,2048]{2,1,0:T(8,128)(2,1)}), bf16[64,16,2048]{2,1,0:T(8,128)(2,1)}, u32[]{:S(2)}, u32[]{:S(2)}) async-start(bf16[64,16,2048]{2,1,0:T(8,128)(2,1)} %fusion.24), calls=%async_computation.4 | async-start | bytes 8388608 | tf_op jit(solution)/shard_map/all_to_all | solution.py:167
  (86 other events, 1051.8 us)
Sparse Core Ops, SparseCore 0:
  9.7 35.6 all-gather.6
  323.0 58.4 all-gather.8
  401.3 18.9 all-gather.10
  422.5 35.9 reduce-scatter.1

commit v5 on v3

--- a/solution.py
+++ b/solution.py
@@ -45,14 +45,8 @@
 ):
     local_rows = stream.shape[0]
     n_exp = lax.axis_size(EXP)
-    meta = jnp.stack([positions, segment_ids, cache_slots]).astype(jnp.float32)
-    meta_all = lax.all_gather(meta, ("blk",) + EXP, axis=0)
-    all_position = meta_all[:, 0, :].reshape(-1).astype(jnp.int32)
-    all_segment = meta_all[:, 1, :].reshape(-1).astype(jnp.int32)
-    meta_group = lax.dynamic_slice_in_dim(meta_all, lax.axis_index("blk") * n_exp, n_exp, 0)
-    group_position = meta_group[:, 0, :].reshape(-1).astype(jnp.int32)
-    group_segment = meta_group[:, 1, :].reshape(-1).astype(jnp.int32)
-    group_slot = meta_group[:, 2, :].reshape(-1).astype(jnp.int32)
+    meta = jnp.stack([positions, segment_ids, cache_slots]).astype(jnp.int32)
+    group_position, group_segment, group_slot = lax.all_gather(meta, EXP, axis=1, tiled=True)
     group_stream = lax.all_gather(stream, EXP, axis=0, tiled=True)
     group_size = group_stream.shape[0]
     normed = rms_norm(group_stream, norm_gain)
@@ -98,11 +92,21 @@
     key_heads = keys.reshape(group_size, local_heads, HD)
     value_heads = values.reshape(group_size, local_heads, HD)
     carry = initial
+    coded = (
+        jnp.stack([group_position // 128, group_position % 128, group_segment])
+        .astype(jnp.bfloat16)
+        .reshape(-1, width)
+    )
+    coded_rows = coded.shape[0]
+    keys_coded = lax.all_gather(
+        jnp.concatenate([keys, coded], axis=0), "blk", axis=0, tiled=True
+    ).reshape(-1, group_size + coded_rows, width)
+    coded_all = keys_coded[:, group_size:].reshape(-1, 3, group_size).astype(jnp.int32)
     piece = (
-        lax.all_gather(key_heads, "blk", axis=0, tiled=True),
+        keys_coded[:, :group_size].reshape(-1, local_heads, HD),
         lax.all_gather(value_heads, "blk", axis=0, tiled=True),
-        all_position,
-        all_segment,
+        (coded_all[:, 0] * 128 + coded_all[:, 1]).reshape(-1),
+        coded_all[:, 2].reshape(-1),
     )
     piece_rows = piece[0].shape[0]
     block = math.gcd(piece_rows, 1024)

time: 546 us -> 547 us (level)
  blocking collectives: 134 us -> 110 us
  waiting for transfers between devices: 141 us -> 158 us
  local copies, waits for them, and re-layouts: 32.9 us -> 38.8 us
    all_gather x1, waiting for transfers between devices: 5.53 us -> 47.5 us  [per_device(): lax.all_gather(value_heads, 'blk', axis=0, tiled=True)]
    all_gather x1, blocking collectives: 36.5 us -> 13.3 us  [per_device(): lax.all_gather(meta, EXP, axis=1, tiled=True)]
    all_gather x1, waiting for transfers between devices: 37.4 us -> 22.6 us  [per_device(): group_stream = lax.all_gather(stream, EXP, axis=0, tiled=True)]
    all_gather x1, waiting for transfers between devices: 53.7 us -> 42.9 us  [per_device(): lax.all_gather(jnp.concatenate([keys, coded], axis=0), 'blk', axis=0, til...]
    unnamed x35, local copies, waits for them, and re-layouts: 4.05 us -> 9.92 us
  transfers between devices with their start and end apart: 7 -> 7, of which waited for: 4 -> 4; matrix products, arithmetic and copies ran while one was open for 17% -> 18% of each run, Pallas kernels for 0% -> 0%
where the time goes in v5:
time: 547 us; the launch traced here: 536 us
  waiting for transfers between devices  158 us (29%)
  matrix products  154 us (28%)
  blocking collectives  110 us (20%)
  other arithmetic  49.2 us (9%)
  local copies, waits for them, and re-layouts  38.8 us (7%)
  between operations  14.6 us (3%)
  starting transfers between devices  10.6 us (2%)
    all_to_all x1, blocking collectives, per_device(): lax.all_to_all(outgoing, CHIPS, split_axis=0, concat_axis=0, tiled=True)  73 us
    all_gather x1, waiting for transfers between devices, per_device(): lax.all_gather(value_heads, 'blk', axis=0, tiled=True)  47.5 us
    dot_general x16, matrix products, attend(): jnp.einsum('hqk,khd->hqd', probs.astype(jnp.bfloat16), block_values, pref...  44.8 us
    all_to_all x1, waiting for transfers between devices, per_device(): lax.all_to_all(summed_halves, CHIPS, split_axis=0, concat_axis=0, tiled=T...  43.9 us
    all_gather x1, waiting for transfers between devices, per_device(): lax.all_gather(jnp.concatenate([keys, coded], axis=0), 'blk', axis=0, til...  42.9 us
    dot_general x16, matrix products, attend(): jnp.einsum('qhd,khd->hqk', query_heads, block_keys, preferred_element_typ...  38.6 us
    reduce_sum x16, other arithmetic, attend(): denom = denom * shrink + jnp.sum(probs, axis=2)  25.6 us
    all_gather x1, waiting for transfers between devices, per_device(): group_stream = lax.all_gather(stream, EXP, axis=0, tiled=True)  22.6 us
  transfers between devices with their start and end apart: 7, of which 4 were waited for; matrix products, arithmetic and copies ran while one was open for 18% of the time, Pallas kernels for 0%

profile of v5, /device:TPU:1, one launch (start us, length us, event | category | flops | bytes accessed | tf_op | source)
XLA Modules:
  0.0 536.3 jit_solution(8371172057045494344)
XLA Ops:
  8.8 13.3 %all_gather.22 = s32[3,1024]{1,0:T(4,128)S(1)} all-gather(s32[3,128]{1,0:T(4,128)S(1)} %pad_add_fusion), channel_id=1, replica_groups=mesh['blk'=16,'x'=4,'core'=2] {'x','core'}, dimensions={1}, use_global_device_ids=true | all-gather | bytes 13824 | tf_op jit(solution)/shard_map/all_gather | solution.py:49
  22.8 22.6 %all-gather.8.cloned.1.call-done = bf16[1024,2048]{1,0:T(8,128)(2,1)} async-done(((bf16[128,2048]{1,0:T(8,128)(2,1)}), bf16[1024,2048]{1,0:T(8,128)(2,1)}) %all-gather.8.cloned.1.call-update) | async-done | bytes 4194320 | tf_op jit(solution)/shard_map/all_gather | solution.py:50
  45.4 3.2 fusion.25
  54.6 4.3 convolution_convert_fusion.2
  59.0 4.1 fusion.38
  63.1 42.9 %all-gather.10.cloned.1.call-done = bf16[16768,128]{1,0:T(8,128)(2,1)} async-done(((bf16[1048,128]{1,0:T(8,128)(2,1)}), bf16[16768,128]{1,0:T(8,128)(2,1)}) %all-gather.10.cloned.1.call-update) | async-done | bytes 4292624 | tf_op jit(solution)/shard_map/all_gather | solution.py:101
  107.2 4.6 slice_bitcast_fusion
  111.8 47.5 %all-gather.14.cloned.1.call-done = bf16[16384,128]{1,0:T(8,128)(2,1)} async-done(((bf16[1024,128]{1,0:T(8,128)(2,1)}), bf16[16384,128]{1,0:T(8,128)(2,1)}) %all-gather.14.cloned.1.call-update) | async-done | bytes 4194320 | tf_op jit(solution)/shard_map/all_gather | solution.py:107
  159.3 123.4 %while.15 = (s32[]{:T(128)}, f32[1,1024]{1,0:T(1,128)S(1)}, f32[1,1024]{1,0:T(1,128)S(1)}, f32[1,1024,128]{2,1,0:T(8,128)}, s32[16,1024]{1,0:T(8,128)S(1)}, /*in...) while((s32[]{:T(128)}, f32[1,1024]{1,0:T(1,128)S(1)}, ...), condition=%wide.region_4.5_spmd.clone, body=%wide.region_1.4_spmd.clone.sunk | while | flops 560337920 | bytes 18743508 | solution.py:115
  284.0 11.5 %all_to_all.24 = bf16[8,128,128]{2,1,0:T(8,128)(2,1)} all-to-all(bf16[8,128,128]{2,1,0:T(8,128)(2,1)S(1)} %bitcast.157), channel_id=1, replica_groups=mesh['blk'=16,'x'=4,'core'=2] {'x','core'}, dimensions={0} | all-to-all | bytes 524288 | tf_op jit(solution)/shard_map/all_to_all | solution.py:119
  307.6 73.0 %all_to_all.25 = bf16[64,16,2048]{2,1,0:T(8,128)(2,1)} all-to-all(bf16[64,16,2048]{2,1,0:T(8,128)(2,1)S(1)} %bitcast.150), channel_id=1, replica_groups=mesh['blk'=16,'x'=4,'core'=2] {'blk','x'}, dimensions={0} | all-to-all | bytes 8388608 | tf_op jit(solution)/shard_map/all_to_all | solution.py:157
  381.3 3.5 fusion.52
  384.8 5.2 fusion.51
  390.0 9.8 %multiply_convert_fusion = bf16[1024,2048]{1,0:T(8,128)(2,1)} fusion(bf16[384,2048]{1,0:T(8,128)(2,1)} %param.30, f32[1024]{0:T(1024)S(1)} %add_divide_fusion, f32[1024,384]{1,0:T(8,128)} %fusion.51, bf16[1024,2048]{1,0:T(8,128)(2,1)} %all-gather.12.cloned.1.call-done, bf16[2048,384]{1,0:T(8,128)(2,1)} %param.29), kind=kOutput, calls=%fused_computation.37 | convolution fusion | flops 3227779072 | bytes 13111296 | tf_op jit(solution)/shard_map/dot_general | solution.py:136
  399.9 11.1 %fusion.32 = f32[2048,704]{0,1:T(8,128)} fusion(bf16[2048,2048]{1,0:T(8,128)(2,1)} %bitcast.181, bf16[1,2048,704]{1,2,0:T(8,128)(2,1)} %param.32), kind=kOutput, calls=%fused_computation.46 | convolution fusion | flops 5905580032 | bytes 17039360 | tf_op jit(solution)/shard_map/dot_general | solution.py:162
  411.0 19.4 %convolution_convert_fusion = bf16[2048,2048]{1,0:T(8,128)(2,1)} fusion(f32[2048,704]{0,1:T(8,128)} %fusion.32, bf16[2048,2048]{1,0:T(8,128)(2,1)} %bitcast.182, bf16[1,704,2048]{2,1,0:T(8,128)(2,1)S(1)} %copy-done, bf16[1,2048,704]{1,2,0:T(8,128)(2,1)} %param.33), kind=kOutput, calls=%fused_computation.38 | convolution fusion | flops 11824005120 | bytes 28311552 | tf_op jit(solution)/shard_map/dot_general | solution.py:166
  430.4 12.6 %all_to_all.26 = bf16[2,64,16,2048]{3,2,1,0:T(8,128)(2,1)S(1)} all-to-all(bf16[2,64,16,2048]{3,2,1,0:T(8,128)(2,1)} %bitcast.151), channel_id=1, replica_groups=mesh['blk'=16,'x'=4,'core'=2] {'core'}, dimensions={0} | all-to-all | bytes 16777216 | tf_op jit(solution)/shard_map/all_to_all | solution.py:170
  446.0 10.0 %all-to-all-start.3 = ((bf16[64,16,2048]{2,1,0:T(8,128)(2,1)}), bf16[64,16,2048]{2,1,0:T(8,128)(2,1)}, u32[]{:S(2)}, u32[]{:S(2)}) async-start(bf16[64,16,2048]{2,1,0:T(8,128)(2,1)} %fusion.28), calls=%async_computation.4 | async-start | bytes 8388608 | tf_op jit(solution)/shard_map/all_to_all | solution.py:174
  456.9 4.2 scatter_custom_fusion
  461.1 4.2 scatter_custom_fusion.1
  465.3 43.9 %all-to-all-done.3 = bf16[64,16,2048]{2,1,0:T(8,128)(2,1)} async-done(((bf16[64,16,2048]{2,1,0:T(8,128)(2,1)}), bf16[64,16,2048]{2,1,0:T(8,128)(2,1)}, u32[]{:S(2)}, u32[]{:S(2)}) %all-to-all-start.3) | async-done | bytes 4194336 | tf_op jit(solution)/shard_map/all_to_all | solution.py:174
  509.1 6.5 %convolution_multiply_fusion = f32[512,2048]{1,0:T(8,128)} fusion(bf16[1024,2048]{1,0:T(8,128)(2,1)} %bitcast.22, f32[512]{0:T(512)S(1)} %mul.141, s32[512]{0:T(512)S(1)} %multiply_add_fusion.1), kind=kOutput, calls=%fused_computation.43 | convolution fusion | flops 2149056512 | bytes 8392704 | tf_op jit(solution)/shard_map/dot_general | solution.py:176
  515.7 5.2 reshape.194
  520.9 5.8 %reduce_sum.53 = f32[128,2048]{1,0:T(8,128)} reduce(f32[128,4,2048]{2,1,0:T(4,128)} %reshape.194, f32[]{:T(128)} %constant.71.clone.1), dimensions={1}, to_apply=%region_11.12 | reduce | flops 786432 | bytes 5242884 | tf_op jit(solution)/shard_map/reduce_sum | solution.py:180
  (264 shorter events, 152.3 us)
Async XLA Ops:
  7.2 403.9 %copy-start = (bf16[1,704,2048]{2,1,0:T(8,128)(2,1)S(1)}, bf16[1,704,2048]{2,1,0:T(8,128)(2,1)}, u32[]{:S(2)}) copy-start(bf16[1,704,2048]{2,1,0:T(8,128)(2,1)} %param.34) | copy-start | bytes 8650756
  7.2 41.4 %copy-start.10 = (f32[2048]{0:T(1024)S(1)}, f32[2048]{0:T(1024)}, u32[]{:S(2)}) copy-start(f32[2048]{0:T(1024)} %param.22) | copy-start | bytes 24580
  7.2 38.2 %all-gather.8.cloned.1.call-start = ((), (), s32[]{:S(2)}) async-start(), calls=%async_computation.5 | async-start | bytes 4718592 | tf_op jit(solution)/shard_map/all_gather | solution.py:50
  7.9 98.1 %all-gather.10.cloned.1.call-start = ((), (), s32[]{:S(2)}) async-start(), calls=%async_computation.6 | async-start | bytes 4560896 | tf_op jit(solution)/shard_map/all_gather | solution.py:101
  54.5 4.5 copy-start.16
  54.5 104.8 %all-gather.14.cloned.1.call-start = ((), (), s32[]{:S(2)}) async-start(), calls=%async_computation.9 | async-start | bytes 4456448 | tf_op jit(solution)/shard_map/all_gather | solution.py:107
  58.9 322.4 %all-gather.12.cloned.1.call-start = ((), (), s32[]{:S(2)}) async-start(), calls=%async_computation.7 | async-start | bytes 4718592 | tf_op jit(solution)/shard_map/all_gather | solution.py:126
  159.3 138.0 %copy-start.5 = (bf16[128,2048]{1,0:T(8,128)(2,1)S(1)}, bf16[128,2048]{1,0:T(8,128)(2,1)}, u32[]{:S(2)}) copy-start(bf16[128,2048]{1,0:T(8,128)(2,1)} %param.21) | copy-start | bytes 1572868
  159.3 4.1 copy-start.6
  167.1 4.1 copy-start.6
  174.8 4.1 copy-start.6
  182.5 4.1 copy-start.6
  197.9 4.1 copy-start.6
  205.7 4.1 copy-start.6
  213.4 4.1 copy-start.6
  259.6 4.1 copy-start.6
  267.4 4.1 copy-start.6
  275.1 4.1 copy-start.6
  282.8 18.6 %copy-start.11 = (f32[2048]{0:T(1024)S(1)}, f32[2048]{0:T(1024)}, u32[]{:S(2)}) copy-start(f32[2048]{0:T(1024)} %param.27) | copy-start | bytes 24580
  297.3 5.5 %copy-start.12 = (s32[128,4]{0,1:T(4,128)S(1)}, s32[128,4]{0,1:T(4,128)}, u32[]{:S(2)}) copy-start(s32[128,4]{0,1:T(4,128)} %param.35) | copy-start | bytes 6148
  302.4 97.5 %all-gather.16.cloned.1.call-start = ((), (), s32[]{:S(2)}) async-start(), calls=%async_computation.10 | async-start | bytes 12582912 | tf_op jit(solution)/shard_map/all_gather | solution.py:158
  380.6 146.1 %reduce-scatter.2.cloned.1.call-start = ((), (), s32[]{:S(2)}) async-start(), calls=%async_computation.8 | async-start | bytes 4718592 | tf_op jit(solution)/shard_map/reduce_scatter | solution.py:134
  446.0 10.0 %copy-start.14 = (f32[128,4]{0,1:T(4,128)S(1)}, f32[128,4]{0,1:T(4,128)}, u32[]{:S(2)}) copy-start(f32[128,4]{0,1:T(4,128)} %param.36) | copy-start | bytes 6148
  446.0 63.2 %all-to-all-start.3 = ((bf16[64,16,2048]{2,1,0:T(8,128)(2,1)}), bf16[64,16,2048]{2,1,0:T(8,128)(2,1)}, u32[]{:S(2)}, u32[]{:S(2)}) async-start(bf16[64,16,2048]{2,1,0:T(8,128)(2,1)} %fusion.28), calls=%async_computation.4 | async-start | bytes 8388608 | tf_op jit(solution)/shard_map/all_to_all | solution.py:174
  (30 other events, 52.2 us)
Sparse Core Ops, SparseCore 0:
  9.7 35.6 all-gather.7
  54.7 51.3 all-gather.9
  108.2 51.0 all-gather.13
  302.5 57.3 all-gather.11
  380.7 18.9 all-gather.15
  402.0 35.9 reduce-scatter.1

commit v6 on v4

--- a/solution.py
+++ b/solution.py
@@ -14,6 +14,7 @@
 FLOOR_SCORE = -1e30
 EXP = ("x", "core")
 CHIPS = ("blk", "x")
+RING = [None]
 
 
 def rms_norm(rows, gain):
@@ -46,10 +47,7 @@
     local_rows = stream.shape[0]
     n_exp = lax.axis_size(EXP)
     meta = jnp.stack([positions, segment_ids, cache_slots]).astype(jnp.int32)
-    meta_group = lax.all_gather(meta, EXP, axis=0)
-    group_position = meta_group[:, 0, :].reshape(-1)
-    group_segment = meta_group[:, 1, :].reshape(-1)
-    group_slot = meta_group[:, 2, :].reshape(-1)
+    group_position, group_segment, group_slot = lax.all_gather(meta, EXP, axis=1, tiled=True)
     group_stream = lax.all_gather(stream, EXP, axis=0, tiled=True)
     group_size = group_stream.shape[0]
     normed = rms_norm(group_stream, norm_gain)
@@ -92,20 +90,39 @@
         jnp.zeros((local_heads, group_size), jnp.float32),
         jnp.zeros((local_heads, group_size, HD), jnp.float32),
     )
-    key_heads = keys.reshape(group_size, local_heads, HD)
-    value_heads = values.reshape(group_size, local_heads, HD)
     n_blk = lax.axis_size("blk")
-    ring = [(i, (i + 1) % n_blk) for i in range(n_blk)]
+    coded = (
+        jnp.stack([group_position // 128, group_position % 128, group_segment])
+        .astype(jnp.bfloat16)
+        .reshape(-1, 2 * width)
+    )
+    coded_rows = coded.shape[0]
+    padded_rows = -(-coded_rows // 16) * 16
+    block = jnp.concatenate(
+        [
+            jnp.concatenate([keys, values], axis=1),
+            jnp.pad(coded, ((0, padded_rows - coded_rows), (0, 0))),
+        ],
+        axis=0,
+    )
+
+    def unpack(block):
+        code = block[group_size : group_size + coded_rows].reshape(3, group_size).astype(jnp.int32)
+        return (
+            block[:group_size, :width].reshape(group_size, local_heads, HD),
+            block[:group_size, width:].reshape(group_size, local_heads, HD),
+            code[0] * 128 + code[1],
+            code[2],
+        )
 
     def ring_step(state, _):
         carry, block = state
-        carry, _ = attend(carry, block)
-        block = lax.ppermute(block, "blk", ring)
+        carry, _ = attend(carry, unpack(block))
+        block = lax.ppermute(block, "blk", RING[0])
         return ((carry, block), None)
 
-    block = (key_heads, value_heads, group_position, group_segment)
     (carry, block), _ = lax.scan(ring_step, (initial, block), None, length=n_blk - 1)
-    carry, _ = attend(carry, block)
+    carry, _ = attend(carry, unpack(block))
     highest, denom, summed = carry
     heads_out = (summed / denom[:, :, None]).astype(jnp.bfloat16)
     heads_out = jnp.transpose(heads_out, (1, 0, 2)).reshape(group_size, width)
@@ -175,9 +192,25 @@
     return (final, cache_keys, cache_values)
 
 
+def snake(mesh):
+    blk = mesh.shape["blk"]
+    try:
+        spots = [tuple(mesh.devices.reshape(blk, -1)[b, 0].coords) for b in range(blk)]
+        zs = sorted({s[2] for s in spots})
+        order = []
+        for i, z in enumerate(zs):
+            row = sorted((b for b in range(blk) if spots[b][2] == z), key=lambda b: spots[b][1])
+            order += row if i % 2 == 0 else row[::-1]
+        assert sorted(order) == list(range(blk))
+    except Exception:
+        order = list(range(blk))
+    return [(order[k], order[(k + 1) % blk]) for k in range(blk)]
+
+
 def solution(mesh):
     blk, exp = mesh.shape["blk"], mesh.shape["exp"]
     chip_mesh = Mesh(mesh.devices.reshape(blk, exp // 2, 2), ("blk", "x", "core"))
+    RING[0] = snake(mesh)
     rows = ("blk",) + EXP
     in_specs = (
         P(rows, None),

time: 564 us -> 537 us (0.952)
  starting transfers between devices: 48.1 us -> 11.2 us
  waiting for transfers between devices: 124 us -> 143 us
  local copies, waits for them, and re-layouts: 50.1 us -> 32.4 us
  other arithmetic: 45.4 us -> 57.6 us
    ppermute x60 -> x15, starting transfers between devices: 38.1 us -> 1.24 us  [ring_step(): block = lax.ppermute(block, 'blk', RING[0])]
    while x135 -> x120, local copies, waits for them, and re-layouts: 32.9 us -> 12.2 us
    ppermute x60 -> x15, waiting for transfers between devices: 55.5 us -> 75.4 us  [ring_step(): block = lax.ppermute(block, 'blk', RING[0])]
    convert_element_type x0 -> x16, other arithmetic: none -> 11 us  [unpack(): block[group_size:group_size + coded_rows].reshape(3, group_size)]
  transfers between devices with their start and end apart: 65 -> 20, of which waited for: 20 -> 17; matrix products, arithmetic and copies ran while one was open for 37% -> 38% of each run, Pallas kernels for 0% -> 0%
where the time goes in v6:
time: 537 us; the launch traced here: 529 us
  matrix products  149 us (28%)
  waiting for transfers between devices  143 us (27%)
  blocking collectives  120 us (22%)
  other arithmetic  57.6 us (11%)
  local copies, waits for them, and re-layouts  32.4 us (6%)
  between operations  14.6 us (3%)
  starting transfers between devices  11.2 us (2%)
    ppermute x15, waiting for transfers between devices, ring_step(): block = lax.ppermute(block, 'blk', RING[0])  75.4 us
    all_to_all x1, blocking collectives, per_device(): lax.all_to_all(outgoing, CHIPS, split_axis=0, concat_axis=0, tiled=True)  70.5 us
    dot_general x16, matrix products, attend(): jnp.einsum('hqk,khd->hqd', probs.astype(jnp.bfloat16), block_values, pref...  44.3 us
    all_to_all x1, waiting for transfers between devices, per_device(): lax.all_to_all(summed_halves, CHIPS, split_axis=0, concat_axis=0, tiled=T...  43.8 us
    dot_general x16, matrix products, attend(): jnp.einsum('qhd,khd->hqk', query_heads, block_keys, preferred_element_typ...  38.3 us
    reduce_sum x16, other arithmetic, attend(): denom = denom * shrink + jnp.sum(probs, axis=2)  25.8 us
    all_to_all x1, blocking collectives, per_device(): lax.all_to_all(heads_out, EXP, split_axis=0, concat_axis=0, tiled=True)  23.7 us
    all_gather x1, waiting for transfers between devices, per_device(): group_stream = lax.all_gather(stream, EXP, axis=0, tiled=True)  23 us
  transfers between devices with their start and end apart: 20, of which 17 were waited for; matrix products, arithmetic and copies ran while one was open for 38% of the time, Pallas kernels for 0%

profile of v6, /device:TPU:1, one launch (start us, length us, event | category | flops | bytes accessed | tf_op | source)
XLA Modules:
  0.0 529.2 jit_solution(7226522329426354823)
XLA Ops:
  8.7 13.3 %all_gather.16 = s32[3,1024]{1,0:T(4,128)S(1)} all-gather(s32[3,128]{1,0:T(4,128)S(1)} %pad_add_fusion), channel_id=1, replica_groups=mesh['blk'=16,'x'=4,'core'=2] {'x','core'}, dimensions={1}, use_global_device_ids=true | all-gather | bytes 13824 | tf_op jit(solution)/shard_map/all_gather | solution.py:50
  22.3 23.0 %all-gather.5.cloned.1.call-done = bf16[1024,2048]{1,0:T(8,128)(2,1)} async-done(((bf16[128,2048]{1,0:T(8,128)(2,1)}), bf16[1024,2048]{1,0:T(8,128)(2,1)}) %all-gather.5.cloned.1.call-update) | async-done | bytes 4194320 | tf_op jit(solution)/shard_map/all_gather | solution.py:51
  57.7 204.2 %while.17 = (s32[]{:T(128)}, f32[1,1024]{1,0:T(1,128)S(1)}, f32[1,1024]{1,0:T(1,128)S(1)}, f32[1,1024,128]{2,1,0:T(8,128)}, bf16[1040,256]{1,0:T(8,128)(2,1)S(1)...) while((s32[]{:T(128)}, f32[1,1024]{1,0:T(1,128)S(1)}, ...), condition=%wide.region_4.5_spmd.clone, body=%wide.region_1.4_spmd.clone.sunk | while | flops 560343040 | bytes 21977296 | solution.py:124
  67.6 5.9 %collective-permute-done = bf16[1040,256]{1,0:T(8,128)(2,1)S(1)} collective-permute-done((bf16[1040,256]{1,0:T(8,128)(2,1)}, bf16[1040,256]{1,0:T(8,128)(2,1)S(1)}, u32[]{:S(2)}, u32[]{:S(2)}) %collective-permute-start) | collective-permute-done | bytes 532512 | tf_op jit(solution)/shard_map/while/body/eval_jaxpr/ppermute | solution.py:121
  82.0 6.3 %collective-permute-done = bf16[1040,256]{1,0:T(8,128)(2,1)S(1)} collective-permute-done((bf16[1040,256]{1,0:T(8,128)(2,1)}, bf16[1040,256]{1,0:T(8,128)(2,1)S(1)}, u32[]{:S(2)}, u32[]{:S(2)}) %collective-permute-start) | collective-permute-done | bytes 532512 | tf_op jit(solution)/shard_map/while/body/eval_jaxpr/ppermute | solution.py:121
  96.8 5.4 %collective-permute-done = bf16[1040,256]{1,0:T(8,128)(2,1)S(1)} collective-permute-done((bf16[1040,256]{1,0:T(8,128)(2,1)}, bf16[1040,256]{1,0:T(8,128)(2,1)S(1)}, u32[]{:S(2)}, u32[]{:S(2)}) %collective-permute-start) | collective-permute-done | bytes 532512 | tf_op jit(solution)/shard_map/while/body/eval_jaxpr/ppermute | solution.py:121
  181.9 5.4 %collective-permute-done = bf16[1040,256]{1,0:T(8,128)(2,1)S(1)} collective-permute-done((bf16[1040,256]{1,0:T(8,128)(2,1)}, bf16[1040,256]{1,0:T(8,128)(2,1)S(1)}, u32[]{:S(2)}, u32[]{:S(2)}) %collective-permute-start) | collective-permute-done | bytes 532512 | tf_op jit(solution)/shard_map/while/body/eval_jaxpr/ppermute | solution.py:121
  195.7 6.5 %collective-permute-done = bf16[1040,256]{1,0:T(8,128)(2,1)S(1)} collective-permute-done((bf16[1040,256]{1,0:T(8,128)(2,1)}, bf16[1040,256]{1,0:T(8,128)(2,1)S(1)}, u32[]{:S(2)}, u32[]{:S(2)}) %collective-permute-start) | collective-permute-done | bytes 532512 | tf_op jit(solution)/shard_map/while/body/eval_jaxpr/ppermute | solution.py:121
  210.7 7.7 %collective-permute-done = bf16[1040,256]{1,0:T(8,128)(2,1)S(1)} collective-permute-done((bf16[1040,256]{1,0:T(8,128)(2,1)}, bf16[1040,256]{1,0:T(8,128)(2,1)S(1)}, u32[]{:S(2)}, u32[]{:S(2)}) %collective-permute-start) | collective-permute-done | bytes 532512 | tf_op jit(solution)/shard_map/while/body/eval_jaxpr/ppermute | solution.py:121
  226.9 6.9 %collective-permute-done = bf16[1040,256]{1,0:T(8,128)(2,1)S(1)} collective-permute-done((bf16[1040,256]{1,0:T(8,128)(2,1)}, bf16[1040,256]{1,0:T(8,128)(2,1)S(1)}, u32[]{:S(2)}, u32[]{:S(2)}) %collective-permute-start) | collective-permute-done | bytes 532512 | tf_op jit(solution)/shard_map/while/body/eval_jaxpr/ppermute | solution.py:121
  242.3 6.0 %collective-permute-done = bf16[1040,256]{1,0:T(8,128)(2,1)S(1)} collective-permute-done((bf16[1040,256]{1,0:T(8,128)(2,1)}, bf16[1040,256]{1,0:T(8,128)(2,1)S(1)}, u32[]{:S(2)}, u32[]{:S(2)}) %collective-permute-start) | collective-permute-done | bytes 532512 | tf_op jit(solution)/shard_map/while/body/eval_jaxpr/ppermute | solution.py:121
  256.8 5.2 collective-permute-done
  269.3 23.7 %all_to_all.24 = bf16[8,128,128]{1,2,0:T(8,128)(2,1)S(1)} all-to-all(bf16[8,128,128]{1,2,0:T(8,128)(2,1)S(1)} %copy.61), channel_id=1, replica_groups=mesh['blk'=16,'x'=4,'core'=2] {'x','core'}, dimensions={0} | all-to-all | bytes 524288 | tf_op jit(solution)/shard_map/all_to_all | solution.py:129
  303.0 70.5 %all_to_all.25 = bf16[64,16,2048]{2,1,0:T(8,128)(2,1)} all-to-all(bf16[64,16,2048]{2,1,0:T(8,128)(2,1)S(1)} %bitcast.132), channel_id=1, replica_groups=mesh['blk'=16,'x'=4,'core'=2] {'blk','x'}, dimensions={0} | all-to-all | bytes 8388608 | tf_op jit(solution)/shard_map/all_to_all | solution.py:167
  377.8 5.2 fusion.73
  383.0 9.9 %multiply_convert_fusion = bf16[1024,2048]{1,0:T(8,128)(2,1)} fusion(bf16[384,2048]{1,0:T(8,128)(2,1)} %param.30, f32[1024]{0:T(1024)S(1)} %add_divide_fusion, f32[1024,384]{1,0:T(8,128)} %fusion.73, bf16[1024,2048]{1,0:T(8,128)(2,1)} %all-gather.7.cloned.1.call-done, bf16[2048,384]{1,0:T(8,128)(2,1)} %param.29), kind=kOutput, calls=%fused_computation.36 | convolution fusion | flops 3227779072 | bytes 13111296 | tf_op jit(solution)/shard_map/dot_general | solution.py:146
  393.0 11.2 %fusion.30 = f32[2048,704]{0,1:T(8,128)} fusion(bf16[2048,2048]{1,0:T(8,128)(2,1)} %bitcast.177, bf16[1,2048,704]{1,2,0:T(8,128)(2,1)} %param.32), kind=kOutput, calls=%fused_computation.48 | convolution fusion | flops 5905580032 | bytes 17039360 | tf_op jit(solution)/shard_map/dot_general | solution.py:172
  404.1 19.2 %convolution_convert_fusion = bf16[2048,2048]{1,0:T(8,128)(2,1)} fusion(f32[2048,704]{0,1:T(8,128)} %fusion.30, bf16[2048,2048]{1,0:T(8,128)(2,1)} %bitcast.178, bf16[1,704,2048]{2,1,0:T(8,128)(2,1)S(1)} %copy-done, bf16[1,2048,704]{1,2,0:T(8,128)(2,1)} %param.33), kind=kOutput, calls=%fused_computation.37 | convolution fusion | flops 11824005120 | bytes 28311552 | tf_op jit(solution)/shard_map/dot_general | solution.py:176
  423.4 12.8 %all_to_all.26 = bf16[2,64,16,2048]{3,2,1,0:T(8,128)(2,1)S(1)} all-to-all(bf16[2,64,16,2048]{3,2,1,0:T(8,128)(2,1)} %bitcast.133), channel_id=1, replica_groups=mesh['blk'=16,'x'=4,'core'=2] {'core'}, dimensions={0} | all-to-all | bytes 16777216 | tf_op jit(solution)/shard_map/all_to_all | solution.py:180
  439.1 9.8 %all-to-all-start.3 = ((bf16[64,16,2048]{2,1,0:T(8,128)(2,1)}), bf16[64,16,2048]{2,1,0:T(8,128)(2,1)}, u32[]{:S(2)}, u32[]{:S(2)}) async-start(bf16[64,16,2048]{2,1,0:T(8,128)(2,1)} %fusion.25), calls=%async_computation.4 | async-start | bytes 8388608 | tf_op jit(solution)/shard_map/all_to_all | solution.py:184
  458.2 43.8 %all-to-all-done.3 = bf16[64,16,2048]{2,1,0:T(8,128)(2,1)} async-done(((bf16[64,16,2048]{2,1,0:T(8,128)(2,1)}), bf16[64,16,2048]{2,1,0:T(8,128)(2,1)}, u32[]{:S(2)}, u32[]{:S(2)}) %all-to-all-start.3) | async-done | bytes 4194336 | tf_op jit(solution)/shard_map/all_to_all | solution.py:184
  502.0 6.5 %convolution_multiply_fusion = f32[512,2048]{1,0:T(8,128)} fusion(bf16[1024,2048]{1,0:T(8,128)(2,1)} %bitcast.24, f32[512]{0:T(512)S(1)} %mul.162, s32[512]{0:T(512)S(1)} %multiply_add_fusion.2), kind=kOutput, calls=%fused_computation.45 | convolution fusion | flops 2149056512 | bytes 8392704 | tf_op jit(solution)/shard_map/dot_general | solution.py:186
  508.6 5.2 reshape.222
  513.7 5.8 %reduce_sum.66 = f32[128,2048]{1,0:T(8,128)} reduce(f32[128,4,2048]{2,1,0:T(4,128)} %reshape.222, f32[]{:T(128)} %constant.47.clone.1), dimensions={1}, to_apply=%region_13.14 | reduce | flops 786432 | bytes 5242884 | tf_op jit(solution)/shard_map/reduce_sum | solution.py:190
  (348 shorter events, 198.0 us)
Async XLA Ops:
  7.2 397.0 %copy-start = (bf16[1,704,2048]{2,1,0:T(8,128)(2,1)S(1)}, bf16[1,704,2048]{2,1,0:T(8,128)(2,1)}, u32[]{:S(2)}) copy-start(bf16[1,704,2048]{2,1,0:T(8,128)(2,1)} %param.34) | copy-start | bytes 8650756
  7.2 41.4 %copy-start.10 = (f32[2048]{0:T(1024)S(1)}, f32[2048]{0:T(1024)}, u32[]{:S(2)}) copy-start(f32[2048]{0:T(1024)} %param.22) | copy-start | bytes 24580
  7.2 38.2 %all-gather.5.cloned.1.call-start = ((), (), s32[]{:S(2)}) async-start(), calls=%async_computation.5 | async-start | bytes 4718592 | tf_op jit(solution)/shard_map/all_gather | solution.py:51
  7.9 366.3 %all-gather.7.cloned.1.call-start = ((), (), s32[]{:S(2)}) async-start(), calls=%async_computation.6 | async-start | bytes 4718592 | tf_op jit(solution)/shard_map/all_gather | solution.py:136
  58.7 14.8 %collective-permute-start = (bf16[1040,256]{1,0:T(8,128)(2,1)}, bf16[1040,256]{1,0:T(8,128)(2,1)S(1)}, u32[]{:S(2)}, u32[]{:S(2)}) collective-permute-start(bf16[1040,256]{1,0:T(8,128)(2,1)} %copy.88), channel_id=1, source_target_pairs={{0,8},{8,16},{16,24},{24,56},{56,48},{48,40},{40,32},{32,64},{64,7... | collective-permute-start | bytes 1597448 | tf_op jit(solution)/shard_map/while/body/eval_jaxpr/ppermute | solution.py:121
  74.3 14.0 %collective-permute-start = (bf16[1040,256]{1,0:T(8,128)(2,1)}, bf16[1040,256]{1,0:T(8,128)(2,1)S(1)}, u32[]{:S(2)}, u32[]{:S(2)}) collective-permute-start(bf16[1040,256]{1,0:T(8,128)(2,1)} %copy.88), channel_id=1, source_target_pairs={{0,8},{8,16},{16,24},{24,56},{56,48},{48,40},{40,32},{32,64},{64,7... | collective-permute-start | bytes 1597448 | tf_op jit(solution)/shard_map/while/body/eval_jaxpr/ppermute | solution.py:121
  89.1 13.1 %collective-permute-start = (bf16[1040,256]{1,0:T(8,128)(2,1)}, bf16[1040,256]{1,0:T(8,128)(2,1)S(1)}, u32[]{:S(2)}, u32[]{:S(2)}) collective-permute-start(bf16[1040,256]{1,0:T(8,128)(2,1)} %copy.88), channel_id=1, source_target_pairs={{0,8},{8,16},{16,24},{24,56},{56,48},{48,40},{40,32},{32,64},{64,7... | collective-permute-start | bytes 1597448 | tf_op jit(solution)/shard_map/while/body/eval_jaxpr/ppermute | solution.py:121
  102.9 12.2 %collective-permute-start = (bf16[1040,256]{1,0:T(8,128)(2,1)}, bf16[1040,256]{1,0:T(8,128)(2,1)S(1)}, u32[]{:S(2)}, u32[]{:S(2)}) collective-permute-start(bf16[1040,256]{1,0:T(8,128)(2,1)} %copy.88), channel_id=1, source_target_pairs={{0,8},{8,16},{16,24},{24,56},{56,48},{48,40},{40,32},{32,64},{64,7... | collective-permute-start | bytes 1597448 | tf_op jit(solution)/shard_map/while/body/eval_jaxpr/ppermute | solution.py:121
  116.0 11.4 %collective-permute-start = (bf16[1040,256]{1,0:T(8,128)(2,1)}, bf16[1040,256]{1,0:T(8,128)(2,1)S(1)}, u32[]{:S(2)}, u32[]{:S(2)}) collective-permute-start(bf16[1040,256]{1,0:T(8,128)(2,1)} %copy.88), channel_id=1, source_target_pairs={{0,8},{8,16},{16,24},{24,56},{56,48},{48,40},{40,32},{32,64},{64,7... | collective-permute-start | bytes 1597448 | tf_op jit(solution)/shard_map/while/body/eval_jaxpr/ppermute | solution.py:121
  128.2 10.5 %collective-permute-start = (bf16[1040,256]{1,0:T(8,128)(2,1)}, bf16[1040,256]{1,0:T(8,128)(2,1)S(1)}, u32[]{:S(2)}, u32[]{:S(2)}) collective-permute-start(bf16[1040,256]{1,0:T(8,128)(2,1)} %copy.88), channel_id=1, source_target_pairs={{0,8},{8,16},{16,24},{24,56},{56,48},{48,40},{40,32},{32,64},{64,7... | collective-permute-start | bytes 1597448 | tf_op jit(solution)/shard_map/while/body/eval_jaxpr/ppermute | solution.py:121
  139.5 9.6 %collective-permute-start = (bf16[1040,256]{1,0:T(8,128)(2,1)}, bf16[1040,256]{1,0:T(8,128)(2,1)S(1)}, u32[]{:S(2)}, u32[]{:S(2)}) collective-permute-start(bf16[1040,256]{1,0:T(8,128)(2,1)} %copy.88), channel_id=1, source_target_pairs={{0,8},{8,16},{16,24},{24,56},{56,48},{48,40},{40,32},{32,64},{64,7... | collective-permute-start | bytes 1597448 | tf_op jit(solution)/shard_map/while/body/eval_jaxpr/ppermute | solution.py:121
  149.9 10.8 %collective-permute-start = (bf16[1040,256]{1,0:T(8,128)(2,1)}, bf16[1040,256]{1,0:T(8,128)(2,1)S(1)}, u32[]{:S(2)}, u32[]{:S(2)}) collective-permute-start(bf16[1040,256]{1,0:T(8,128)(2,1)} %copy.88), channel_id=1, source_target_pairs={{0,8},{8,16},{16,24},{24,56},{56,48},{48,40},{40,32},{32,64},{64,7... | collective-permute-start | bytes 1597448 | tf_op jit(solution)/shard_map/while/body/eval_jaxpr/ppermute | solution.py:121
  161.5 11.9 %collective-permute-start = (bf16[1040,256]{1,0:T(8,128)(2,1)}, bf16[1040,256]{1,0:T(8,128)(2,1)S(1)}, u32[]{:S(2)}, u32[]{:S(2)}) collective-permute-start(bf16[1040,256]{1,0:T(8,128)(2,1)} %copy.88), channel_id=1, source_target_pairs={{0,8},{8,16},{16,24},{24,56},{56,48},{48,40},{40,32},{32,64},{64,7... | collective-permute-start | bytes 1597448 | tf_op jit(solution)/shard_map/while/body/eval_jaxpr/ppermute | solution.py:121
  174.2 13.1 %collective-permute-start = (bf16[1040,256]{1,0:T(8,128)(2,1)}, bf16[1040,256]{1,0:T(8,128)(2,1)S(1)}, u32[]{:S(2)}, u32[]{:S(2)}) collective-permute-start(bf16[1040,256]{1,0:T(8,128)(2,1)} %copy.88), channel_id=1, source_target_pairs={{0,8},{8,16},{16,24},{24,56},{56,48},{48,40},{40,32},{32,64},{64,7... | collective-permute-start | bytes 1597448 | tf_op jit(solution)/shard_map/while/body/eval_jaxpr/ppermute | solution.py:121
  188.0 14.2 %collective-permute-start = (bf16[1040,256]{1,0:T(8,128)(2,1)}, bf16[1040,256]{1,0:T(8,128)(2,1)S(1)}, u32[]{:S(2)}, u32[]{:S(2)}) collective-permute-start(bf16[1040,256]{1,0:T(8,128)(2,1)} %copy.88), channel_id=1, source_target_pairs={{0,8},{8,16},{16,24},{24,56},{56,48},{48,40},{40,32},{32,64},{64,7... | collective-permute-start | bytes 1597448 | tf_op jit(solution)/shard_map/while/body/eval_jaxpr/ppermute | solution.py:121
  203.0 15.4 %collective-permute-start = (bf16[1040,256]{1,0:T(8,128)(2,1)}, bf16[1040,256]{1,0:T(8,128)(2,1)S(1)}, u32[]{:S(2)}, u32[]{:S(2)}) collective-permute-start(bf16[1040,256]{1,0:T(8,128)(2,1)} %copy.88), channel_id=1, source_target_pairs={{0,8},{8,16},{16,24},{24,56},{56,48},{48,40},{40,32},{32,64},{64,7... | collective-permute-start | bytes 1597448 | tf_op jit(solution)/shard_map/while/body/eval_jaxpr/ppermute | solution.py:121
  219.2 14.6 %collective-permute-start = (bf16[1040,256]{1,0:T(8,128)(2,1)}, bf16[1040,256]{1,0:T(8,128)(2,1)S(1)}, u32[]{:S(2)}, u32[]{:S(2)}) collective-permute-start(bf16[1040,256]{1,0:T(8,128)(2,1)} %copy.88), channel_id=1, source_target_pairs={{0,8},{8,16},{16,24},{24,56},{56,48},{48,40},{40,32},{32,64},{64,7... | collective-permute-start | bytes 1597448 | tf_op jit(solution)/shard_map/while/body/eval_jaxpr/ppermute | solution.py:121
  234.6 13.7 %collective-permute-start = (bf16[1040,256]{1,0:T(8,128)(2,1)}, bf16[1040,256]{1,0:T(8,128)(2,1)S(1)}, u32[]{:S(2)}, u32[]{:S(2)}) collective-permute-start(bf16[1040,256]{1,0:T(8,128)(2,1)} %copy.88), channel_id=1, source_target_pairs={{0,8},{8,16},{16,24},{24,56},{56,48},{48,40},{40,32},{32,64},{64,7... | collective-permute-start | bytes 1597448 | tf_op jit(solution)/shard_map/while/body/eval_jaxpr/ppermute | solution.py:121
  249.1 12.9 %collective-permute-start = (bf16[1040,256]{1,0:T(8,128)(2,1)}, bf16[1040,256]{1,0:T(8,128)(2,1)S(1)}, u32[]{:S(2)}, u32[]{:S(2)}) collective-permute-start(bf16[1040,256]{1,0:T(8,128)(2,1)} %copy.88), channel_id=1, source_target_pairs={{0,8},{8,16},{16,24},{24,56},{56,48},{48,40},{40,32},{32,64},{64,7... | collective-permute-start | bytes 1597448 | tf_op jit(solution)/shard_map/while/body/eval_jaxpr/ppermute | solution.py:121
  268.2 29.0 %copy-start.11 = (f32[2048]{0:T(1024)S(1)}, f32[2048]{0:T(1024)}, u32[]{:S(2)}) copy-start(f32[2048]{0:T(1024)} %param.27) | copy-start | bytes 24580
  298.2 94.8 %all-gather.9.cloned.1.call-start = ((), (), s32[]{:S(2)}) async-start(), calls=%async_computation.8 | async-start | bytes 12582912 | tf_op jit(solution)/shard_map/all_gather | solution.py:168
  373.6 146.0 %reduce-scatter.2.cloned.1.call-start = ((), (), s32[]{:S(2)}) async-start(), calls=%async_computation.7 | async-start | bytes 4718592 | tf_op jit(solution)/shard_map/reduce_scatter | solution.py:144
  439.1 10.9 %copy-start.5 = (bf16[1024,128]{0,1:T(8,128)(2,1)S(1)}, bf16[1024,128]{0,1:T(8,128)(2,1)}, u32[]{:S(2)}) copy-start(bf16[1024,128]{0,1:T(8,128)(2,1)} %copy-done.4) | copy-start | bytes 786436
  439.1 62.9 %all-to-all-start.3 = ((bf16[64,16,2048]{2,1,0:T(8,128)(2,1)}), bf16[64,16,2048]{2,1,0:T(8,128)(2,1)}, u32[]{:S(2)}, u32[]{:S(2)}) async-start(bf16[64,16,2048]{2,1,0:T(8,128)(2,1)} %fusion.25), calls=%async_computation.4 | async-start | bytes 8388608 | tf_op jit(solution)/shard_map/all_to_all | solution.py:184
  (43 other events, 183.6 us)
Sparse Core Ops, SparseCore 0:
  9.7 35.6 all-gather.4
  298.3 53.7 all-gather.6
  373.7 18.8 all-gather.8
  394.8 35.9 reduce-scatter.1

commit v7 on v6

--- a/solution.py
+++ b/solution.py
@@ -115,14 +115,27 @@
             code[2],
         )
 
+    forward = RING[0]
+    backward = [(b, a) for a, b in forward]
+
     def ring_step(state, _):
-        carry, block = state
-        carry, _ = attend(carry, unpack(block))
-        block = lax.ppermute(block, "blk", RING[0])
-        return ((carry, block), None)
-
-    (carry, block), _ = lax.scan(ring_step, (initial, block), None, length=n_blk - 1)
-    carry, _ = attend(carry, unpack(block))
+        carry, ahead, behind = state
+        carry, _ = attend(carry, unpack(ahead))
+        carry, _ = attend(carry, unpack(behind))
+        ahead = lax.ppermute(ahead, "blk", forward)
+        behind = lax.ppermute(behind, "blk", backward)
+        return ((carry, ahead, behind), None)
+
+    carry, _ = attend(initial, unpack(block))
+    ahead = lax.ppermute(block, "blk", forward)
+    behind = lax.ppermute(block, "blk", backward)
+    (carry, ahead, behind), _ = lax.scan(
+        ring_step, (carry, ahead, behind), None, length=n_blk // 2 - 2
+    )
+    opposite = lax.ppermute(ahead, "blk", forward)
+    carry, _ = attend(carry, unpack(ahead))
+    carry, _ = attend(carry, unpack(behind))
+    carry, _ = attend(carry, unpack(opposite))
     highest, denom, summed = carry
     heads_out = (summed / denom[:, :, None]).astype(jnp.bfloat16)
     heads_out = jnp.transpose(heads_out, (1, 0, 2)).reshape(group_size, width)

time: 537 us -> 471 us (0.88)
  waiting for transfers between devices: 143 us -> 76.7 us
  starting transfers between devices: 11.2 us -> 29.5 us
  other arithmetic: 57.6 us -> 40.2 us
  blocking collectives: 120 us -> 111 us
  local copies, waits for them, and re-layouts: 32.4 us -> 38.9 us
    ppermute x15, waiting for transfers between devices: 75.4 us -> 10.2 us  [the longest x1 4.64 us: per_device(): opposite = lax.ppermute(ahead, 'blk', forward)]
    ppermute x15, starting transfers between devices: 1.24 us -> 19.3 us  [the longest x6 16 us: ring_step(): behind = lax.ppermute(behind, 'blk', backward)]
    another operation x1 -> x13, local copies, waits for them, and re-layouts: 0.01 us -> 17.5 us
    while x120 -> x54, local copies, waits for them, and re-layouts: 12.2 us -> 0.17 us
    reduce_sum x16 -> x8, other arithmetic: 25.8 us -> 14.6 us  [attend(): denom = denom * shrink + jnp.sum(probs, axis=2)]
    all_to_all x1, blocking collectives: 23.7 us -> 15.4 us  [per_device(): lax.all_to_all(heads_out, EXP, split_axis=0, concat_axis=0, tiled=True)]
    convert_element_type x16 -> x9, other arithmetic: 11 us -> 5.17 us  [unpack(): block[group_size:group_size + coded_rows].reshape(3, group_size)]
    dot_general x16, matrix products: 38.3 us -> 43.9 us  [attend(): jnp.einsum('qhd,khd->hqk', query_heads, block_keys, preferred_element_typ...]
  transfers between devices with their start and end apart: 20 -> 20, of which waited for: 17 -> 5; matrix products, arithmetic and copies ran while one was open for 38% -> 41% of each run, Pallas kernels for 0% -> 0%
where the time goes in v7:
time: 471 us; the launch traced here: 464 us
  matrix products  152 us (32%)
  blocking collectives  111 us (24%)
  waiting for transfers between devices  76.7 us (16%)
  other arithmetic  40.2 us (9%)
  local copies, waits for them, and re-layouts  38.9 us (8%)
  starting transfers between devices  29.5 us (6%)
  between operations  14.5 us (3%)
    all_to_all x1, blocking collectives, per_device(): lax.all_to_all(outgoing, CHIPS, split_axis=0, concat_axis=0, tiled=True)  69.9 us
    dot_general x16, matrix products, attend(): jnp.einsum('qhd,khd->hqk', query_heads, block_keys, preferred_element_typ...  43.9 us
    all_to_all x1, waiting for transfers between devices, per_device(): lax.all_to_all(summed_halves, CHIPS, split_axis=0, concat_axis=0, tiled=T...  43.2 us
    dot_general x16, matrix products, attend(): jnp.einsum('hqk,khd->hqd', probs.astype(jnp.bfloat16), block_values, pref...  40.5 us
    all_gather x1, waiting for transfers between devices, per_device(): group_stream = lax.all_gather(stream, EXP, axis=0, tiled=True)  22.5 us
    dot_general x1, matrix products, per_device(): jnp.dot(hidden, expert_down[0], preferred_element_type=jnp.float32)  19.4 us
    another operation x13, local copies, waits for them, and re-layouts  17.5 us
    ppermute x6, starting transfers between devices, ring_step(): behind = lax.ppermute(behind, 'blk', backward)  16 us
  transfers between devices with their start and end apart: 20, of which 5 were waited for; matrix products, arithmetic and copies ran while one was open for 41% of the time, Pallas kernels for 0%

profile of v7, /device:TPU:1, one launch (start us, length us, event | category | flops | bytes accessed | tf_op | source)
XLA Modules:
  0.0 463.6 jit_solution(15056188511793702772)
XLA Ops:
  8.8 13.3 %all_gather.15 = s32[3,1024]{1,0:T(4,128)S(1)} all-gather(s32[3,128]{1,0:T(4,128)S(1)} %pad_add_fusion), channel_id=1, replica_groups=mesh['blk'=16,'x'=4,'core'=2] {'x','core'}, dimensions={1}, use_global_device_ids=true | all-gather | bytes 13824 | tf_op jit(solution)/shard_map/all_gather | solution.py:50
  22.9 22.5 %all-gather.5.cloned.1.call-done = bf16[1024,2048]{1,0:T(8,128)(2,1)} async-done(((bf16[128,2048]{1,0:T(8,128)(2,1)}), bf16[1024,2048]{1,0:T(8,128)(2,1)}) %all-gather.5.cloned.1.call-update) | async-done | bytes 4194320 | tf_op jit(solution)/shard_map/all_gather | solution.py:51
  72.2 114.0 %while.18 = (s32[]{:T(128)}, f32[1,1024]{1,0:T(1,128)S(1)}, f32[1,1024]{1,0:T(1,128)S(1)}, f32[1,1024,128]{2,1,0:T(8,128)}, bf16[1040,256]{1,0:T(8,128)(2,1)}, /...) while((s32[]{:T(128)}, f32[1,1024]{1,0:T(1,128)S(1)}, ...), condition=%wide.region_8.9_spmd, body=%wide.region_3.8_spmd.sunk | while | flops 1120417792 | bytes 38682860 | solution.py:132
  99.7 3.7 fusion.185
  118.7 3.7 fusion.185
  137.7 3.7 fusion.185
  156.7 3.7 fusion.185
  175.7 3.7 fusion.185
  192.3 4.6 %collective-permute-done.4 = bf16[1040,256]{1,0:T(8,128)(2,1)S(1)} collective-permute-done((bf16[1040,256]{1,0:T(8,128)(2,1)}, bf16[1040,256]{1,0:T(8,128)(2,1)S(1)}, u32[]{:S(2)}, u32[]{:S(2)}) %collective-permute-start.4) | collective-permute-done | bytes 532512 | tf_op jit(solution)/shard_map/ppermute | solution.py:135
  197.7 4.9 %fusion.59 = (f32[1024]{0:T(1024)S(1)}, f32[1024]{0:T(1024)S(1)}, f32[1024]{0:T(1024)S(1)}, f32[1024,1024]{0,1:T(8,128)S(1)}) fusion(f32[1024,1024]{0,1:T(8,128)S(1)} %get-tuple-element.139, f32[1024]{0:T(1024)S(1)} %bitcast.274, s32[1024]{0:T(1024)S(1)} %bitcast.254, s32[1024]{0:T(1024)S(1)} %bitcast.235, s32[1024]{0:T(1024)S(1)} %bitcast.310, ...), kind=kOutput, calls=%fused_computation.86 | convolution fusion | flops 289403904 | bytes 13156352 | tf_op jit(solution)/shard_map/qhd,khd->hqk/dot_general | solution.py:68
  212.9 15.4 %all_to_all.24 = bf16[8,128,128]{1,2,0:T(8,128)(2,1)S(1)} all-to-all(bf16[8,128,128]{1,2,0:T(8,128)(2,1)} %copy.66), channel_id=1, replica_groups=mesh['blk'=16,'x'=4,'core'=2] {'x','core'}, dimensions={0} | all-to-all | bytes 524288 | tf_op jit(solution)/shard_map/all_to_all | solution.py:142
  238.4 69.9 %all_to_all.25 = bf16[64,16,2048]{2,1,0:T(8,128)(2,1)} all-to-all(bf16[64,16,2048]{2,1,0:T(8,128)(2,1)S(1)} %bitcast.209), channel_id=1, replica_groups=mesh['blk'=16,'x'=4,'core'=2] {'blk','x'}, dimensions={0} | all-to-all | bytes 8388608 | tf_op jit(solution)/shard_map/all_to_all | solution.py:180
  312.6 5.2 %fusion.143 = f32[1024,384]{1,0:T(8,128)} fusion(bf16[1024,2048]{1,0:T(8,128)(2,1)S(1)} %copy-done.4, bf16[2048,384]{1,0:T(8,128)(2,1)} %param.28), kind=kOutput, calls=%fused_computation.196 | convolution fusion | flops 1610612736 | bytes 7340032 | tf_op jit(solution)/shard_map/dot_general | solution.py:151
  317.7 9.8 %multiply_convert_fusion = bf16[1024,2048]{1,0:T(8,128)(2,1)} fusion(bf16[384,2048]{1,0:T(8,128)(2,1)} %param.30, f32[1024]{0:T(1024)S(1)} %add_divide_fusion, f32[1024,384]{1,0:T(8,128)} %fusion.143, bf16[1024,2048]{1,0:T(8,128)(2,1)} %all-gather.7.cloned.1.call-done, bf16[2048,384]{1,0:T(8,128)(2,1)} %param.29), kind=kOutput, calls=%fused_computation.54 | convolution fusion | flops 3227779072 | bytes 13111296 | tf_op jit(solution)/shard_map/dot_general | solution.py:159
  327.6 11.0 %fusion.52 = f32[2048,704]{0,1:T(8,128)} fusion(bf16[2048,2048]{1,0:T(8,128)(2,1)} %bitcast.316, bf16[1,2048,704]{1,2,0:T(8,128)(2,1)} %param.32), kind=kOutput, calls=%fused_computation.78 | convolution fusion | flops 5905580032 | bytes 17039360 | tf_op jit(solution)/shard_map/dot_general | solution.py:185
  338.6 19.4 %convolution_convert_fusion = bf16[2048,2048]{1,0:T(8,128)(2,1)} fusion(f32[2048,704]{0,1:T(8,128)} %fusion.52, bf16[2048,2048]{1,0:T(8,128)(2,1)} %bitcast.317, bf16[1,704,2048]{2,1,0:T(8,128)(2,1)S(1)} %copy-done, bf16[1,2048,704]{1,2,0:T(8,128)(2,1)} %param.33), kind=kOutput, calls=%fused_computation.55 | convolution fusion | flops 11824005120 | bytes 28311552 | tf_op jit(solution)/shard_map/dot_general | solution.py:189
  358.0 12.6 %all_to_all.26 = bf16[2,64,16,2048]{3,2,1,0:T(8,128)(2,1)S(1)} all-to-all(bf16[2,64,16,2048]{3,2,1,0:T(8,128)(2,1)} %bitcast.210), channel_id=1, replica_groups=mesh['blk'=16,'x'=4,'core'=2] {'core'}, dimensions={0} | all-to-all | bytes 16777216 | tf_op jit(solution)/shard_map/all_to_all | solution.py:193
  373.6 9.9 %all-to-all-start.3 = ((bf16[64,16,2048]{2,1,0:T(8,128)(2,1)}), bf16[64,16,2048]{2,1,0:T(8,128)(2,1)}, u32[]{:S(2)}, u32[]{:S(2)}) async-start(bf16[64,16,2048]{2,1,0:T(8,128)(2,1)} %fusion.44), calls=%async_computation.4 | async-start | bytes 8388608 | tf_op jit(solution)/shard_map/all_to_all | solution.py:197
  385.5 4.2 scatter_custom_fusion
  389.7 3.8 scatter_custom_fusion.1
  393.5 43.2 %all-to-all-done.3 = bf16[64,16,2048]{2,1,0:T(8,128)(2,1)} async-done(((bf16[64,16,2048]{2,1,0:T(8,128)(2,1)}), bf16[64,16,2048]{2,1,0:T(8,128)(2,1)}, u32[]{:S(2)}, u32[]{:S(2)}) %all-to-all-start.3) | async-done | bytes 4194336 | tf_op jit(solution)/shard_map/all_to_all | solution.py:197
  436.6 6.5 %convolution_multiply_fusion = f32[512,2048]{1,0:T(8,128)} fusion(bf16[1024,2048]{1,0:T(8,128)(2,1)} %bitcast.52, f32[512]{0:T(512)S(1)} %mul.256, s32[512]{0:T(512)S(1)} %multiply_add_fusion.4), kind=kOutput, calls=%fused_computation.75 | convolution fusion | flops 2149056512 | bytes 8392704 | tf_op jit(solution)/shard_map/dot_general | solution.py:199
  443.2 5.2 %reshape.404 = f32[128,4,2048]{2,1,0:T(4,128)} reshape(f32[512,2048]{1,0:T(8,128)} %convolution_multiply_fusion) | data formatting | bytes 8388608 | tf_op jit(solution)/shard_map/reshape | solution.py:203
  448.3 5.8 %reduce_sum.116 = f32[128,2048]{1,0:T(8,128)} reduce(f32[128,4,2048]{2,1,0:T(4,128)} %reshape.404, f32[]{:T(128)} %constant.74.clone.1), dimensions={1}, to_apply=%region_21.22 | reduce | flops 786432 | bytes 5242884 | tf_op jit(solution)/shard_map/reduce_sum | solution.py:203
  (282 shorter events, 162.3 us)
Async XLA Ops:
  7.2 331.5 %copy-start = (bf16[1,704,2048]{2,1,0:T(8,128)(2,1)S(1)}, bf16[1,704,2048]{2,1,0:T(8,128)(2,1)}, u32[]{:S(2)}) copy-start(bf16[1,704,2048]{2,1,0:T(8,128)(2,1)} %param.34) | copy-start | bytes 8650756
  7.2 41.4 %copy-start.18 = (f32[2048]{0:T(1024)S(1)}, f32[2048]{0:T(1024)}, u32[]{:S(2)}) copy-start(f32[2048]{0:T(1024)} %param.22) | copy-start | bytes 24580
  7.2 38.2 %all-gather.5.cloned.1.call-start = ((), (), s32[]{:S(2)}) async-start(), calls=%async_computation.5 | async-start | bytes 4718592 | tf_op jit(solution)/shard_map/all_gather | solution.py:51
  7.9 301.1 %all-gather.7.cloned.1.call-start = ((), (), s32[]{:S(2)}) async-start(), calls=%async_computation.6 | async-start | bytes 4718592 | tf_op jit(solution)/shard_map/all_gather | solution.py:149
  54.8 14.2 %collective-permute-start.3 = (bf16[1040,256]{1,0:T(8,128)(2,1)}, bf16[1040,256]{1,0:T(8,128)(2,1)}, u32[]{:S(2)}, u32[]{:S(2)}) collective-permute-start(bf16[1040,256]{1,0:T(8,128)(2,1)} %copy.64), channel_id=1, source_target_pairs={{8,0},{16,8},{24,16},{56,24},{48,56},{40,48},{32,40},{64,32},{72,6... | collective-permute-start | bytes 1597448 | tf_op jit(solution)/shard_map/ppermute | solution.py:131
  57.4 14.8 %collective-permute-start.2 = (bf16[1040,256]{1,0:T(8,128)(2,1)}, bf16[1040,256]{1,0:T(8,128)(2,1)}, u32[]{:S(2)}, u32[]{:S(2)}) collective-permute-start(bf16[1040,256]{1,0:T(8,128)(2,1)} %copy.64), channel_id=1, source_target_pairs={{0,8},{8,16},{16,24},{24,56},{56,48},{48,40},{40,32},{32,64},{64,7... | collective-permute-start | bytes 1597448 | tf_op jit(solution)/shard_map/ppermute | solution.py:130
  73.3 18.0 %collective-permute-start = (bf16[1040,256]{1,0:T(8,128)(2,1)S(1)}, bf16[1040,256]{1,0:T(8,128)(2,1)}, u32[]{:S(2)}, u32[]{:S(2)}) collective-permute-start(bf16[1040,256]{1,0:T(8,128)(2,1)S(1)} %copy.104), channel_id=1, source_target_pairs={{0,8},{8,16},{16,24},{24,56},{56,48},{48,40},{40,32},{32,64},{64,7... | collective-permute-start | bytes 1597448 | tf_op jit(solution)/shard_map/while/body/eval_jaxpr/ppermute | solution.py:125
  75.1 16.1 %collective-permute-start.1 = (bf16[1040,256]{1,0:T(8,128)(2,1)}, bf16[1040,256]{1,0:T(8,128)(2,1)}, u32[]{:S(2)}, u32[]{:S(2)}) collective-permute-start(bf16[1040,256]{1,0:T(8,128)(2,1)} %copy.105), channel_id=1, source_target_pairs={{8,0},{16,8},{24,16},{56,24},{48,56},{40,48},{32,40},{64,32},{72,6... | collective-permute-start | bytes 1597448 | tf_op jit(solution)/shard_map/while/body/eval_jaxpr/ppermute | solution.py:126
  92.3 17.9 %collective-permute-start = (bf16[1040,256]{1,0:T(8,128)(2,1)S(1)}, bf16[1040,256]{1,0:T(8,128)(2,1)}, u32[]{:S(2)}, u32[]{:S(2)}) collective-permute-start(bf16[1040,256]{1,0:T(8,128)(2,1)S(1)} %copy.104), channel_id=1, source_target_pairs={{0,8},{8,16},{16,24},{24,56},{56,48},{48,40},{40,32},{32,64},{64,7... | collective-permute-start | bytes 1597448 | tf_op jit(solution)/shard_map/while/body/eval_jaxpr/ppermute | solution.py:125
  94.1 16.1 %collective-permute-start.1 = (bf16[1040,256]{1,0:T(8,128)(2,1)}, bf16[1040,256]{1,0:T(8,128)(2,1)}, u32[]{:S(2)}, u32[]{:S(2)}) collective-permute-start(bf16[1040,256]{1,0:T(8,128)(2,1)} %copy.105), channel_id=1, source_target_pairs={{8,0},{16,8},{24,16},{56,24},{48,56},{40,48},{32,40},{64,32},{72,6... | collective-permute-start | bytes 1597448 | tf_op jit(solution)/shard_map/while/body/eval_jaxpr/ppermute | solution.py:126
  111.3 17.9 %collective-permute-start = (bf16[1040,256]{1,0:T(8,128)(2,1)S(1)}, bf16[1040,256]{1,0:T(8,128)(2,1)}, u32[]{:S(2)}, u32[]{:S(2)}) collective-permute-start(bf16[1040,256]{1,0:T(8,128)(2,1)S(1)} %copy.104), channel_id=1, source_target_pairs={{0,8},{8,16},{16,24},{24,56},{56,48},{48,40},{40,32},{32,64},{64,7... | collective-permute-start | bytes 1597448 | tf_op jit(solution)/shard_map/while/body/eval_jaxpr/ppermute | solution.py:125
  113.1 16.1 %collective-permute-start.1 = (bf16[1040,256]{1,0:T(8,128)(2,1)}, bf16[1040,256]{1,0:T(8,128)(2,1)}, u32[]{:S(2)}, u32[]{:S(2)}) collective-permute-start(bf16[1040,256]{1,0:T(8,128)(2,1)} %copy.105), channel_id=1, source_target_pairs={{8,0},{16,8},{24,16},{56,24},{48,56},{40,48},{32,40},{64,32},{72,6... | collective-permute-start | bytes 1597448 | tf_op jit(solution)/shard_map/while/body/eval_jaxpr/ppermute | solution.py:126
  130.3 17.9 %collective-permute-start = (bf16[1040,256]{1,0:T(8,128)(2,1)S(1)}, bf16[1040,256]{1,0:T(8,128)(2,1)}, u32[]{:S(2)}, u32[]{:S(2)}) collective-permute-start(bf16[1040,256]{1,0:T(8,128)(2,1)S(1)} %copy.104), channel_id=1, source_target_pairs={{0,8},{8,16},{16,24},{24,56},{56,48},{48,40},{40,32},{32,64},{64,7... | collective-permute-start | bytes 1597448 | tf_op jit(solution)/shard_map/while/body/eval_jaxpr/ppermute | solution.py:125
  132.1 16.1 %collective-permute-start.1 = (bf16[1040,256]{1,0:T(8,128)(2,1)}, bf16[1040,256]{1,0:T(8,128)(2,1)}, u32[]{:S(2)}, u32[]{:S(2)}) collective-permute-start(bf16[1040,256]{1,0:T(8,128)(2,1)} %copy.105), channel_id=1, source_target_pairs={{8,0},{16,8},{24,16},{56,24},{48,56},{40,48},{32,40},{64,32},{72,6... | collective-permute-start | bytes 1597448 | tf_op jit(solution)/shard_map/while/body/eval_jaxpr/ppermute | solution.py:126
  149.3 17.9 %collective-permute-start = (bf16[1040,256]{1,0:T(8,128)(2,1)S(1)}, bf16[1040,256]{1,0:T(8,128)(2,1)}, u32[]{:S(2)}, u32[]{:S(2)}) collective-permute-start(bf16[1040,256]{1,0:T(8,128)(2,1)S(1)} %copy.104), channel_id=1, source_target_pairs={{0,8},{8,16},{16,24},{24,56},{56,48},{48,40},{40,32},{32,64},{64,7... | collective-permute-start | bytes 1597448 | tf_op jit(solution)/shard_map/while/body/eval_jaxpr/ppermute | solution.py:125
  151.1 16.1 %collective-permute-start.1 = (bf16[1040,256]{1,0:T(8,128)(2,1)}, bf16[1040,256]{1,0:T(8,128)(2,1)}, u32[]{:S(2)}, u32[]{:S(2)}) collective-permute-start(bf16[1040,256]{1,0:T(8,128)(2,1)} %copy.105), channel_id=1, source_target_pairs={{8,0},{16,8},{24,16},{56,24},{48,56},{40,48},{32,40},{64,32},{72,6... | collective-permute-start | bytes 1597448 | tf_op jit(solution)/shard_map/while/body/eval_jaxpr/ppermute | solution.py:126
  168.3 17.9 %collective-permute-start = (bf16[1040,256]{1,0:T(8,128)(2,1)S(1)}, bf16[1040,256]{1,0:T(8,128)(2,1)}, u32[]{:S(2)}, u32[]{:S(2)}) collective-permute-start(bf16[1040,256]{1,0:T(8,128)(2,1)S(1)} %copy.104), channel_id=1, source_target_pairs={{0,8},{8,16},{16,24},{24,56},{56,48},{48,40},{40,32},{32,64},{64,7... | collective-permute-start | bytes 1597448 | tf_op jit(solution)/shard_map/while/body/eval_jaxpr/ppermute | solution.py:125
  170.1 16.1 %collective-permute-start.1 = (bf16[1040,256]{1,0:T(8,128)(2,1)}, bf16[1040,256]{1,0:T(8,128)(2,1)}, u32[]{:S(2)}, u32[]{:S(2)}) collective-permute-start(bf16[1040,256]{1,0:T(8,128)(2,1)} %copy.105), channel_id=1, source_target_pairs={{8,0},{16,8},{24,16},{56,24},{48,56},{40,48},{32,40},{64,32},{72,6... | collective-permute-start | bytes 1597448 | tf_op jit(solution)/shard_map/while/body/eval_jaxpr/ppermute | solution.py:126
  186.2 10.7 %collective-permute-start.4 = (bf16[1040,256]{1,0:T(8,128)(2,1)}, bf16[1040,256]{1,0:T(8,128)(2,1)S(1)}, u32[]{:S(2)}, u32[]{:S(2)}) collective-permute-start(bf16[1040,256]{1,0:T(8,128)(2,1)} %get-tuple-element.56), channel_id=1, source_target_pairs={{0,8},{8,16},{16,24},{24,56},{56,48},{48,40},{40,32},{32,64},{64,7... | collective-permute-start | bytes 1597448 | tf_op jit(solution)/shard_map/ppermute | solution.py:135
  208.8 19.5 %copy-start.11 = (bf16[128,2048]{1,0:T(8,128)(2,1)S(1)}, bf16[128,2048]{1,0:T(8,128)(2,1)}, u32[]{:S(2)}) copy-start(bf16[128,2048]{1,0:T(8,128)(2,1)} %param.21) | copy-start | bytes 1572868
  211.1 21.2 %copy-start.19 = (f32[2048]{0:T(1024)S(1)}, f32[2048]{0:T(1024)}, u32[]{:S(2)}) copy-start(f32[2048]{0:T(1024)} %param.27) | copy-start | bytes 24580
  233.3 94.2 %all-gather.9.cloned.1.call-start = ((), (), s32[]{:S(2)}) async-start(), calls=%async_computation.8 | async-start | bytes 12582912 | tf_op jit(solution)/shard_map/all_gather | solution.py:181
  308.3 145.8 %reduce-scatter.2.cloned.1.call-start = ((), (), s32[]{:S(2)}) async-start(), calls=%async_computation.7 | async-start | bytes 4718592 | tf_op jit(solution)/shard_map/reduce_scatter | solution.py:157
  373.6 63.1 %all-to-all-start.3 = ((bf16[64,16,2048]{2,1,0:T(8,128)(2,1)}), bf16[64,16,2048]{2,1,0:T(8,128)(2,1)}, u32[]{:S(2)}, u32[]{:S(2)}) async-start(bf16[64,16,2048]{2,1,0:T(8,128)(2,1)} %fusion.44), calls=%async_computation.4 | async-start | bytes 8388608 | tf_op jit(solution)/shard_map/all_to_all | solution.py:197
  (31 other events, 100.8 us)
Sparse Core Ops, SparseCore 0:
  9.7 35.6 all-gather.4
  233.4 51.9 all-gather.6
  308.4 18.8 all-gather.8
  329.6 35.9 reduce-scatter.1

commit v8 on v7

--- a/solution.py
+++ b/solution.py
@@ -195,12 +195,20 @@
         both_halves[0].astype(jnp.float32) + both_halves[1].astype(jnp.float32)
     ).astype(jnp.bfloat16)
     returned = lax.all_to_all(summed_halves, CHIPS, split_axis=0, concat_axis=0, tiled=True)
-    gather_pick = (target[:, None] == slot_ids[None, :]).astype(jnp.bfloat16)
-    picked = jnp.dot(
-        gather_pick, returned.reshape(-1, D), preferred_element_type=jnp.float32
-    ) * route_weights.reshape(-1)[:, None]
-    routed = jnp.sum(picked.reshape(local_rows, TOP, D), axis=1)
-    routed = jnp.sum(picked.reshape(local_rows, TOP, D), axis=1)
+    choice_weights = jnp.sum(
+        jnp.where(
+            target.reshape(local_rows, TOP, 1) == slot_ids[None, None, :],
+            route_weights[:, :, None],
+            0.0,
+        ),
+        axis=1,
+    )
+    routed = jnp.dot(
+        choice_weights,
+        returned.reshape(-1, D).astype(jnp.float32),
+        precision=lax.Precision.HIGHEST,
+        preferred_element_type=jnp.float32,
+    )
     final = (resid_local.astype(jnp.float32) + shared_local + routed).astype(jnp.bfloat16)
     return (final, cache_keys, cache_values)
 

time: 471 us -> 483 us (1.025)
  matrix products: 152 us -> 167 us
  other arithmetic: 40.2 us -> 32.8 us
  local copies, waits for them, and re-layouts: 38.9 us -> 45.8 us
    dot_general x16, matrix products: 40.5 us -> 55.7 us  [attend(): jnp.einsum('hqk,khd->hqd', probs.astype(jnp.bfloat16), block_values, pref...]
    while x54 -> x78, local copies, waits for them, and re-layouts: 0.17 us -> 11.8 us
    reshape x2 -> x0, local copies, waits for them, and re-layouts: 5.28 us -> none  [the longest x1 5.17 us: per_device(): routed = jnp.sum(picked.reshape(local_rows, TOP, D), axis=1)]
  transfers between devices with their start and end apart: 20 -> 20, of which waited for: 5 -> 4; matrix products, arithmetic and copies ran while one was open for 41% -> 40% of each run, Pallas kernels for 0% -> 0%
where the time goes in v8:
time: 483 us; the launch traced here: 475 us
  matrix products  167 us (35%)
  blocking collectives  111 us (23%)
  waiting for transfers between devices  73.3 us (15%)
  local copies, waits for them, and re-layouts  45.8 us (9%)
  other arithmetic  32.8 us (7%)
  starting transfers between devices  29.3 us (6%)
  between operations  14.5 us (3%)
    all_to_all x1, blocking collectives, per_device(): lax.all_to_all(outgoing, CHIPS, split_axis=0, concat_axis=0, tiled=True)  70.1 us
    dot_general x16, matrix products, attend(): jnp.einsum('hqk,khd->hqd', probs.astype(jnp.bfloat16), block_values, pref...  55.7 us
    dot_general x16, matrix products, attend(): jnp.einsum('qhd,khd->hqk', query_heads, block_keys, preferred_element_typ...  45.2 us
    all_to_all x1, waiting for transfers between devices, per_device(): lax.all_to_all(summed_halves, CHIPS, split_axis=0, concat_axis=0, tiled=T...  42.2 us
    all_gather x1, waiting for transfers between devices, per_device(): group_stream = lax.all_gather(stream, EXP, axis=0, tiled=True)  22.5 us
    dot_general x1, matrix products, per_device(): jnp.dot(hidden, expert_down[0], preferred_element_type=jnp.float32)  19.3 us
    another operation x13, local copies, waits for them, and re-layouts  18.1 us
    all_to_all x1, blocking collectives, per_device(): lax.all_to_all(heads_out, EXP, split_axis=0, concat_axis=0, tiled=True)  15.3 us
  transfers between devices with their start and end apart: 20, of which 4 were waited for; matrix products, arithmetic and copies ran while one was open for 40% of the time, Pallas kernels for 0%

profile of v8, /device:TPU:1, one launch (start us, length us, event | category | flops | bytes accessed | tf_op | source)
XLA Modules:
  0.0 475.2 jit_solution(7983810710825959676)
XLA Ops:
  8.8 13.3 %all_gather.15 = s32[3,1024]{1,0:T(4,128)S(1)} all-gather(s32[3,128]{1,0:T(4,128)S(1)} %pad_add_fusion), channel_id=1, replica_groups=mesh['blk'=16,'x'=4,'core'=2] {'x','core'}, dimensions={1}, use_global_device_ids=true | all-gather | bytes 13824 | tf_op jit(solution)/shard_map/all_gather | solution.py:50
  22.9 22.5 %all-gather.5.cloned.1.call-done = bf16[1024,2048]{1,0:T(8,128)(2,1)} async-done(((bf16[128,2048]{1,0:T(8,128)(2,1)}), bf16[1024,2048]{1,0:T(8,128)(2,1)}) %all-gather.5.cloned.1.call-update) | async-done | bytes 4194320 | tf_op jit(solution)/shard_map/all_gather | solution.py:51
  69.7 142.8 %while.18 = (s32[]{:T(128)}, f32[1,1024]{1,0:T(1,128)S(1)}, f32[1,1024]{1,0:T(1,128)S(1)}, f32[1,1024,128]{2,1,0:T(8,128)}, bf16[1040,256]{1,0:T(8,128)(2,1)}, /...) while((s32[]{:T(128)}, f32[1,1024]{1,0:T(1,128)S(1)}, ...), condition=%wide.region_8.9_spmd, body=%wide.region_3.8_spmd.sunk | while | flops 1120417792 | bytes 86917408 | solution.py:132
  85.8 4.2 fusion.188
  109.6 4.2 fusion.188
  125.8 3.9 fusion.186
  133.4 4.2 fusion.188
  157.2 4.2 fusion.188
  181.0 4.2 fusion.188
  197.3 3.9 fusion.186
  204.9 4.2 fusion.188
  218.6 4.7 collective-permute-done.4
  224.1 4.9 %fusion.60 = (f32[1024]{0:T(1024)S(1)}, f32[1024]{0:T(1024)S(1)}, f32[1024]{0:T(1024)S(1)}, f32[1024,1024]{0,1:T(8,128)S(1)}) fusion(f32[1024,1024]{0,1:T(8,128)S(1)} %get-tuple-element.139, f32[1024]{0:T(1024)S(1)} %bitcast.273, s32[1024]{0:T(1024)S(1)} %bitcast.253, s32[1024]{0:T(1024)S(1)} %bitcast.234, s32[1024]{0:T(1024)S(1)} %bitcast.309, ...), kind=kOutput, calls=%fused_computation.87 | convolution fusion | flops 289403904 | bytes 13156352 | tf_op jit(solution)/shard_map/qhd,khd->hqk/dot_general | solution.py:68
  239.4 15.3 %all_to_all.24 = bf16[8,128,128]{1,2,0:T(8,128)(2,1)S(1)} all-to-all(bf16[8,128,128]{1,2,0:T(8,128)(2,1)} %copy.68), channel_id=1, replica_groups=mesh['blk'=16,'x'=4,'core'=2] {'x','core'}, dimensions={0} | all-to-all | bytes 524288 | tf_op jit(solution)/shard_map/all_to_all | solution.py:142
  264.5 70.1 %all_to_all.25 = bf16[64,16,2048]{2,1,0:T(8,128)(2,1)} all-to-all(bf16[64,16,2048]{2,1,0:T(8,128)(2,1)S(1)} %bitcast.208), channel_id=1, replica_groups=mesh['blk'=16,'x'=4,'core'=2] {'blk','x'}, dimensions={0} | all-to-all | bytes 8388608 | tf_op jit(solution)/shard_map/all_to_all | solution.py:180
  338.9 5.2 %fusion.143 = f32[1024,384]{1,0:T(8,128)} fusion(bf16[1024,2048]{1,0:T(8,128)(2,1)S(1)} %copy-done.6, bf16[2048,384]{1,0:T(8,128)(2,1)} %param.28), kind=kOutput, calls=%fused_computation.195 | convolution fusion | flops 1610612736 | bytes 7340032 | tf_op jit(solution)/shard_map/dot_general | solution.py:151
  344.1 9.9 %multiply_convert_fusion = bf16[1024,2048]{1,0:T(8,128)(2,1)} fusion(bf16[384,2048]{1,0:T(8,128)(2,1)} %param.30, f32[1024]{0:T(1024)S(1)} %add_divide_fusion, f32[1024,384]{1,0:T(8,128)} %fusion.143, bf16[1024,2048]{1,0:T(8,128)(2,1)} %all-gather.7.cloned.1.call-done, bf16[2048,384]{1,0:T(8,128)(2,1)} %param.29), kind=kOutput, calls=%fused_computation.54 | convolution fusion | flops 3227779072 | bytes 13111296 | tf_op jit(solution)/shard_map/dot_general | solution.py:159
  354.0 11.1 %fusion.52 = f32[2048,704]{0,1:T(8,128)} fusion(bf16[2048,2048]{1,0:T(8,128)(2,1)} %bitcast.315, bf16[1,2048,704]{1,2,0:T(8,128)(2,1)} %param.32), kind=kOutput, calls=%fused_computation.77 | convolution fusion | flops 5905580032 | bytes 17039360 | tf_op jit(solution)/shard_map/dot_general | solution.py:185
  365.1 19.3 %convolution_convert_fusion = bf16[2048,2048]{1,0:T(8,128)(2,1)} fusion(f32[2048,704]{0,1:T(8,128)} %fusion.52, bf16[2048,2048]{1,0:T(8,128)(2,1)} %bitcast.316, bf16[1,704,2048]{2,1,0:T(8,128)(2,1)S(1)} %copy-done, bf16[1,2048,704]{1,2,0:T(8,128)(2,1)} %param.33), kind=kOutput, calls=%fused_computation.55 | convolution fusion | flops 11824005120 | bytes 28311552 | tf_op jit(solution)/shard_map/dot_general | solution.py:189
  384.4 12.8 %all_to_all.26 = bf16[2,64,16,2048]{3,2,1,0:T(8,128)(2,1)S(1)} all-to-all(bf16[2,64,16,2048]{3,2,1,0:T(8,128)(2,1)} %bitcast.209), channel_id=1, replica_groups=mesh['blk'=16,'x'=4,'core'=2] {'core'}, dimensions={0} | all-to-all | bytes 16777216 | tf_op jit(solution)/shard_map/all_to_all | solution.py:193
  400.1 9.8 %all-to-all-start.3 = ((bf16[64,16,2048]{2,1,0:T(8,128)(2,1)}), bf16[64,16,2048]{2,1,0:T(8,128)(2,1)}, u32[]{:S(2)}, u32[]{:S(2)}) async-start(bf16[64,16,2048]{2,1,0:T(8,128)(2,1)} %fusion.44), calls=%async_computation.4 | async-start | bytes 8388608 | tf_op jit(solution)/shard_map/all_to_all | solution.py:197
  412.8 4.2 scatter_custom_fusion
  420.8 42.2 %all-to-all-done.3 = bf16[64,16,2048]{2,1,0:T(8,128)(2,1)} async-done(((bf16[64,16,2048]{2,1,0:T(8,128)(2,1)}), bf16[64,16,2048]{2,1,0:T(8,128)(2,1)}, u32[]{:S(2)}, u32[]{:S(2)}) %all-to-all-start.3) | async-done | bytes 4194336 | tf_op jit(solution)/shard_map/all_to_all | solution.py:197
  463.0 5.4 %fusion.57 = bf16[128,2048]{1,0:T(8,128)(2,1)} fusion(f32[128,1024]{1,0:T(8,128)} %select_reduce_fusion, bf16[1024,2048]{1,0:T(8,128)(2,1)} %bitcast.52, f32[128,2048]{1,0:T(8,128)} %copy-done.5, bf16[128,2048]{1,0:T(8,128)(2,1)} %reduce-scatter.2.cloned.1.call-done), kind=kOutput, calls=%fused_computation.84 | convolution fusion | flops 3222274048 | bytes 6815744 | tf_op jit(solution)/shard_map/dot_general | solution.py:206
  (301 shorter events, 176.0 us)
Async XLA Ops:
  7.2 357.9 %copy-start = (bf16[1,704,2048]{2,1,0:T(8,128)(2,1)S(1)}, bf16[1,704,2048]{2,1,0:T(8,128)(2,1)}, u32[]{:S(2)}) copy-start(bf16[1,704,2048]{2,1,0:T(8,128)(2,1)} %param.34) | copy-start | bytes 8650756
  7.2 41.4 %copy-start.20 = (f32[2048]{0:T(1024)S(1)}, f32[2048]{0:T(1024)}, u32[]{:S(2)}) copy-start(f32[2048]{0:T(1024)} %param.22) | copy-start | bytes 24580
  7.2 38.2 %all-gather.5.cloned.1.call-start = ((), (), s32[]{:S(2)}) async-start(), calls=%async_computation.5 | async-start | bytes 4718592 | tf_op jit(solution)/shard_map/all_gather | solution.py:51
  7.9 327.4 %all-gather.7.cloned.1.call-start = ((), (), s32[]{:S(2)}) async-start(), calls=%async_computation.6 | async-start | bytes 4718592 | tf_op jit(solution)/shard_map/all_gather | solution.py:149
  54.7 14.9 %collective-permute-start.2 = (bf16[1040,256]{1,0:T(8,128)(2,1)}, bf16[1040,256]{1,0:T(8,128)(2,1)}, u32[]{:S(2)}, u32[]{:S(2)}) collective-permute-start(bf16[1040,256]{1,0:T(8,128)(2,1)} %copy.66), channel_id=1, source_target_pairs={{0,8},{8,16},{16,24},{24,56},{56,48},{48,40},{40,32},{32,64},{64,7... | collective-permute-start | bytes 1597448 | tf_op jit(solution)/shard_map/ppermute | solution.py:130
  55.9 13.7 %collective-permute-start.3 = (bf16[1040,256]{1,0:T(8,128)(2,1)}, bf16[1040,256]{1,0:T(8,128)(2,1)}, u32[]{:S(2)}, u32[]{:S(2)}) collective-permute-start(bf16[1040,256]{1,0:T(8,128)(2,1)} %copy.66), channel_id=1, source_target_pairs={{8,0},{16,8},{24,16},{56,24},{48,56},{40,48},{32,40},{64,32},{72,6... | collective-permute-start | bytes 1597448 | tf_op jit(solution)/shard_map/ppermute | solution.py:131
  70.7 22.8 %collective-permute-start = (bf16[1040,256]{1,0:T(8,128)(2,1)S(1)}, bf16[1040,256]{1,0:T(8,128)(2,1)}, u32[]{:S(2)}, u32[]{:S(2)}) collective-permute-start(bf16[1040,256]{1,0:T(8,128)(2,1)S(1)} %copy.105), channel_id=1, source_target_pairs={{0,8},{8,16},{16,24},{24,56},{56,48},{48,40},{40,32},{32,64},{64,7... | collective-permute-start | bytes 1597448 | tf_op jit(solution)/shard_map/while/body/eval_jaxpr/ppermute | solution.py:125
  73.8 19.7 %collective-permute-start.1 = (bf16[1040,256]{1,0:T(8,128)(2,1)}, bf16[1040,256]{1,0:T(8,128)(2,1)}, u32[]{:S(2)}, u32[]{:S(2)}) collective-permute-start(bf16[1040,256]{1,0:T(8,128)(2,1)} %copy.106), channel_id=1, source_target_pairs={{8,0},{16,8},{24,16},{56,24},{48,56},{40,48},{32,40},{64,32},{72,6... | collective-permute-start | bytes 1597448 | tf_op jit(solution)/shard_map/while/body/eval_jaxpr/ppermute | solution.py:126
  94.5 22.8 %collective-permute-start = (bf16[1040,256]{1,0:T(8,128)(2,1)S(1)}, bf16[1040,256]{1,0:T(8,128)(2,1)}, u32[]{:S(2)}, u32[]{:S(2)}) collective-permute-start(bf16[1040,256]{1,0:T(8,128)(2,1)S(1)} %copy.105), channel_id=1, source_target_pairs={{0,8},{8,16},{16,24},{24,56},{56,48},{48,40},{40,32},{32,64},{64,7... | collective-permute-start | bytes 1597448 | tf_op jit(solution)/shard_map/while/body/eval_jaxpr/ppermute | solution.py:125
  96.5 20.8 %collective-permute-start.1 = (bf16[1040,256]{1,0:T(8,128)(2,1)}, bf16[1040,256]{1,0:T(8,128)(2,1)}, u32[]{:S(2)}, u32[]{:S(2)}) collective-permute-start(bf16[1040,256]{1,0:T(8,128)(2,1)} %copy.106), channel_id=1, source_target_pairs={{8,0},{16,8},{24,16},{56,24},{48,56},{40,48},{32,40},{64,32},{72,6... | collective-permute-start | bytes 1597448 | tf_op jit(solution)/shard_map/while/body/eval_jaxpr/ppermute | solution.py:126
  118.3 22.8 %collective-permute-start = (bf16[1040,256]{1,0:T(8,128)(2,1)S(1)}, bf16[1040,256]{1,0:T(8,128)(2,1)}, u32[]{:S(2)}, u32[]{:S(2)}) collective-permute-start(bf16[1040,256]{1,0:T(8,128)(2,1)S(1)} %copy.105), channel_id=1, source_target_pairs={{0,8},{8,16},{16,24},{24,56},{56,48},{48,40},{40,32},{32,64},{64,7... | collective-permute-start | bytes 1597448 | tf_op jit(solution)/shard_map/while/body/eval_jaxpr/ppermute | solution.py:125
  120.3 20.8 %collective-permute-start.1 = (bf16[1040,256]{1,0:T(8,128)(2,1)}, bf16[1040,256]{1,0:T(8,128)(2,1)}, u32[]{:S(2)}, u32[]{:S(2)}) collective-permute-start(bf16[1040,256]{1,0:T(8,128)(2,1)} %copy.106), channel_id=1, source_target_pairs={{8,0},{16,8},{24,16},{56,24},{48,56},{40,48},{32,40},{64,32},{72,6... | collective-permute-start | bytes 1597448 | tf_op jit(solution)/shard_map/while/body/eval_jaxpr/ppermute | solution.py:126
  142.1 22.8 %collective-permute-start = (bf16[1040,256]{1,0:T(8,128)(2,1)S(1)}, bf16[1040,256]{1,0:T(8,128)(2,1)}, u32[]{:S(2)}, u32[]{:S(2)}) collective-permute-start(bf16[1040,256]{1,0:T(8,128)(2,1)S(1)} %copy.105), channel_id=1, source_target_pairs={{0,8},{8,16},{16,24},{24,56},{56,48},{48,40},{40,32},{32,64},{64,7... | collective-permute-start | bytes 1597448 | tf_op jit(solution)/shard_map/while/body/eval_jaxpr/ppermute | solution.py:125
  144.1 20.8 %collective-permute-start.1 = (bf16[1040,256]{1,0:T(8,128)(2,1)}, bf16[1040,256]{1,0:T(8,128)(2,1)}, u32[]{:S(2)}, u32[]{:S(2)}) collective-permute-start(bf16[1040,256]{1,0:T(8,128)(2,1)} %copy.106), channel_id=1, source_target_pairs={{8,0},{16,8},{24,16},{56,24},{48,56},{40,48},{32,40},{64,32},{72,6... | collective-permute-start | bytes 1597448 | tf_op jit(solution)/shard_map/while/body/eval_jaxpr/ppermute | solution.py:126
  165.9 22.8 %collective-permute-start = (bf16[1040,256]{1,0:T(8,128)(2,1)S(1)}, bf16[1040,256]{1,0:T(8,128)(2,1)}, u32[]{:S(2)}, u32[]{:S(2)}) collective-permute-start(bf16[1040,256]{1,0:T(8,128)(2,1)S(1)} %copy.105), channel_id=1, source_target_pairs={{0,8},{8,16},{16,24},{24,56},{56,48},{48,40},{40,32},{32,64},{64,7... | collective-permute-start | bytes 1597448 | tf_op jit(solution)/shard_map/while/body/eval_jaxpr/ppermute | solution.py:125
  167.9 20.8 %collective-permute-start.1 = (bf16[1040,256]{1,0:T(8,128)(2,1)}, bf16[1040,256]{1,0:T(8,128)(2,1)}, u32[]{:S(2)}, u32[]{:S(2)}) collective-permute-start(bf16[1040,256]{1,0:T(8,128)(2,1)} %copy.106), channel_id=1, source_target_pairs={{8,0},{16,8},{24,16},{56,24},{48,56},{40,48},{32,40},{64,32},{72,6... | collective-permute-start | bytes 1597448 | tf_op jit(solution)/shard_map/while/body/eval_jaxpr/ppermute | solution.py:126
  189.7 22.8 %collective-permute-start = (bf16[1040,256]{1,0:T(8,128)(2,1)S(1)}, bf16[1040,256]{1,0:T(8,128)(2,1)}, u32[]{:S(2)}, u32[]{:S(2)}) collective-permute-start(bf16[1040,256]{1,0:T(8,128)(2,1)S(1)} %copy.105), channel_id=1, source_target_pairs={{0,8},{8,16},{16,24},{24,56},{56,48},{48,40},{40,32},{32,64},{64,7... | collective-permute-start | bytes 1597448 | tf_op jit(solution)/shard_map/while/body/eval_jaxpr/ppermute | solution.py:125
  191.7 20.8 %collective-permute-start.1 = (bf16[1040,256]{1,0:T(8,128)(2,1)}, bf16[1040,256]{1,0:T(8,128)(2,1)}, u32[]{:S(2)}, u32[]{:S(2)}) collective-permute-start(bf16[1040,256]{1,0:T(8,128)(2,1)} %copy.106), channel_id=1, source_target_pairs={{8,0},{16,8},{24,16},{56,24},{48,56},{40,48},{32,40},{64,32},{72,6... | collective-permute-start | bytes 1597448 | tf_op jit(solution)/shard_map/while/body/eval_jaxpr/ppermute | solution.py:126
  212.5 10.9 %collective-permute-start.4 = (bf16[1040,256]{1,0:T(8,128)(2,1)}, bf16[1040,256]{1,0:T(8,128)(2,1)S(1)}, u32[]{:S(2)}, u32[]{:S(2)}) collective-permute-start(bf16[1040,256]{1,0:T(8,128)(2,1)} %get-tuple-element.56), channel_id=1, source_target_pairs={{0,8},{8,16},{16,24},{24,56},{56,48},{48,40},{40,32},{32,64},{64,7... | collective-permute-start | bytes 1597448 | tf_op jit(solution)/shard_map/ppermute | solution.py:135
  235.2 19.4 %copy-start.13 = (bf16[128,2048]{1,0:T(8,128)(2,1)S(1)}, bf16[128,2048]{1,0:T(8,128)(2,1)}, u32[]{:S(2)}) copy-start(bf16[128,2048]{1,0:T(8,128)(2,1)} %param.21) | copy-start | bytes 1572868
  237.6 21.1 %copy-start.21 = (f32[2048]{0:T(1024)S(1)}, f32[2048]{0:T(1024)}, u32[]{:S(2)}) copy-start(f32[2048]{0:T(1024)} %param.27) | copy-start | bytes 24580
  259.7 94.4 %all-gather.9.cloned.1.call-start = ((), (), s32[]{:S(2)}) async-start(), calls=%async_computation.8 | async-start | bytes 12582912 | tf_op jit(solution)/shard_map/all_gather | solution.py:181
  334.7 86.1 %reduce-scatter.2.cloned.1.call-start = ((), (), s32[]{:S(2)}) async-start(), calls=%async_computation.7 | async-start | bytes 4718592 | tf_op jit(solution)/shard_map/reduce_scatter | solution.py:157
  400.1 62.9 %all-to-all-start.3 = ((bf16[64,16,2048]{2,1,0:T(8,128)(2,1)}), bf16[64,16,2048]{2,1,0:T(8,128)(2,1)}, u32[]{:S(2)}, u32[]{:S(2)}) async-start(bf16[64,16,2048]{2,1,0:T(8,128)(2,1)} %fusion.44), calls=%async_computation.4 | async-start | bytes 8388608 | tf_op jit(solution)/shard_map/all_to_all | solution.py:197
  (43 other events, 184.5 us)
Sparse Core Ops, SparseCore 0:
  9.7 35.6 all-gather.4
  259.8 52.3 all-gather.6
  334.8 18.8 all-gather.8
  355.9 35.9 reduce-scatter.1

commit v9 on v8

--- a/solution.py
+++ b/solution.py
@@ -129,9 +129,10 @@
     carry, _ = attend(initial, unpack(block))
     ahead = lax.ppermute(block, "blk", forward)
     behind = lax.ppermute(block, "blk", backward)
-    (carry, ahead, behind), _ = lax.scan(
-        ring_step, (carry, ahead, behind), None, length=n_blk // 2 - 2
-    )
+    state = (carry, ahead, behind)
+    for _ in range(n_blk // 2 - 2):
+        state, _ = ring_step(state, None)
+    carry, ahead, behind = state
     opposite = lax.ppermute(ahead, "blk", forward)
     carry, _ = attend(carry, unpack(ahead))
     carry, _ = attend(carry, unpack(behind))

time: 483 us -> 482 us (level)
  waiting for transfers between devices: 73.3 us -> 120 us
  local copies, waits for them, and re-layouts: 45.8 us -> 17 us
  matrix products: 167 us -> 147 us
    ppermute x6, waiting for transfers between devices: 0.02 us -> 30.5 us  [ring_step(): behind = lax.ppermute(behind, 'blk', backward)]
    another operation x13 -> x1, local copies, waits for them, and re-layouts: 18.1 us -> 0.01 us
    dot_general x16, matrix products: 55.7 us -> 41.6 us  [attend(): jnp.einsum('hqk,khd->hqd', probs.astype(jnp.bfloat16), block_values, pref...]
    while x78 -> x0, local copies, waits for them, and re-layouts: 11.8 us -> none
    ppermute x6, starting transfers between devices: 14.9 us -> 6.62 us  [ring_step(): behind = lax.ppermute(behind, 'blk', backward)]
    reduce_sum x8 -> x3, other arithmetic: 14.6 us -> 22.7 us  [attend(): denom = denom * shrink + jnp.sum(probs, axis=2)]
    ppermute x6, waiting for transfers between devices: 0.02 us -> 7.7 us  [ring_step(): ahead = lax.ppermute(ahead, 'blk', forward)]
    ppermute x1, waiting for transfers between devices: 0.01 us -> 6.63 us  [per_device(): behind = lax.ppermute(block, 'blk', backward)]
  transfers between devices with their start and end apart: 20 -> 20, of which waited for: 4 -> 12; matrix products, arithmetic and copies ran while one was open for 40% -> 21% of each run, Pallas kernels for 0% -> 0%
where the time goes in v9:
time: 482 us; the launch traced here: 473 us
  matrix products  147 us (30%)
  waiting for transfers between devices  120 us (25%)
  blocking collectives  114 us (24%)
  other arithmetic  36.3 us (8%)
  starting transfers between devices  24.7 us (5%)
  local copies, waits for them, and re-layouts  17 us (4%)
  between operations  15.2 us (3%)
    all_to_all x1, blocking collectives, per_device(): lax.all_to_all(outgoing, CHIPS, split_axis=0, concat_axis=0, tiled=True)  70.9 us
    all_to_all x1, waiting for transfers between devices, per_device(): lax.all_to_all(summed_halves, CHIPS, split_axis=0, concat_axis=0, tiled=T...  42.3 us
    dot_general x16, matrix products, attend(): jnp.einsum('hqk,khd->hqd', probs.astype(jnp.bfloat16), block_values, pref...  41.6 us
    dot_general x16, matrix products, attend(): jnp.einsum('qhd,khd->hqk', query_heads, block_keys, preferred_element_typ...  38.6 us
    ppermute x6, waiting for transfers between devices, ring_step(): behind = lax.ppermute(behind, 'blk', backward)  30.5 us
    reduce_sum x3, other arithmetic, attend(): denom = denom * shrink + jnp.sum(probs, axis=2)  22.7 us
    all_gather x1, waiting for transfers between devices, per_device(): group_stream = lax.all_gather(stream, EXP, axis=0, tiled=True)  22.4 us
    dot_general x1, matrix products, per_device(): jnp.dot(hidden, expert_down[0], preferred_element_type=jnp.float32)  19.3 us
  transfers between devices with their start and end apart: 20, of which 12 were waited for; matrix products, arithmetic and copies ran while one was open for 21% of the time, Pallas kernels for 0%

profile of v9, /device:TPU:1, one launch (start us, length us, event | category | flops | bytes accessed | tf_op | source)
XLA Modules:
  0.0 473.2 jit_solution(16588118848990602344)
XLA Ops:
  8.8 13.3 %all_gather.15 = s32[3,1024]{1,0:T(4,128)S(1)} all-gather(s32[3,128]{1,0:T(4,128)S(1)} %pad_add_fusion), channel_id=1, replica_groups=mesh['blk'=16,'x'=4,'core'=2] {'x','core'}, dimensions={1}, use_global_device_ids=true | all-gather | bytes 13824 | tf_op jit(solution)/shard_map/all_gather | solution.py:50
  22.9 22.4 %all-gather.5.cloned.1.call-done = bf16[1024,2048]{1,0:T(8,128)(2,1)} async-done(((bf16[128,2048]{1,0:T(8,128)(2,1)}), bf16[1024,2048]{1,0:T(8,128)(2,1)}) %all-gather.5.cloned.1.call-update) | async-done | bytes 4194320 | tf_op jit(solution)/shard_map/all_gather | solution.py:51
  62.3 6.6 %collective-permute-done.1 = bf16[1040,256]{1,0:T(8,128)(2,1)S(1)} collective-permute-done((bf16[1040,256]{1,0:T(8,128)(2,1)}, bf16[1040,256]{1,0:T(8,128)(2,1)S(1)}, u32[]{:S(2)}, u32[]{:S(2)}) %collective-permute-start.1) | collective-permute-done | bytes 532512 | tf_op jit(solution)/shard_map/ppermute | solution.py:131
  73.3 9.2 %collective-permute-done.3 = bf16[1040,256]{1,0:T(8,128)(2,1)S(1)} collective-permute-done((bf16[1040,256]{1,0:T(8,128)(2,1)S(1)}, bf16[1040,256]{1,0:T(8,128)(2,1)S(1)}, u32[]{:S(2)}, u32[]{:S(2)}) %collective-permute-start.3) | collective-permute-done | bytes 532512 | tf_op jit(solution)/shard_map/ppermute | solution.py:126
  87.5 6.0 %fusion.29 = (f32[1024]{0:T(1024)S(1)}, f32[1024]{0:T(1024)S(1)}, f32[1024]{0:T(1024)S(1)}, f32[1024]{0:T(1024)S(1)}, f32[1024]{0:T(1024)S(1)}, /*index=5*/f32[1024,1024]{0,1:T(8,128)S(1)}) fusion(f32[1024,1024]{0,1:T(8,128)S(1)} %get-tuple-element.105, f32[1024]{0:T(1024)S(1)} %broadcast_maximum_fusion, s32[1024]{0:T(1024)S(1)} %bitcast.208, ...), kind=kOutput, calls=%fused_computation.87 | convolution fusion | flops 301984768 | bytes 21569536 | tf_op jit(solution)/shard_map/qhd,khd->hqk/dot_general | solution.py:68
  99.8 5.2 %collective-permute-done.5 = bf16[1040,256]{1,0:T(8,128)(2,1)S(1)} collective-permute-done((bf16[1040,256]{1,0:T(8,128)(2,1)S(1)}, bf16[1040,256]{1,0:T(8,128)(2,1)S(1)}, u32[]{:S(2)}, u32[]{:S(2)}) %collective-permute-start.5) | collective-permute-done | bytes 532512 | tf_op jit(solution)/shard_map/ppermute | solution.py:126
  107.6 7.9 %collective-permute-done.7 = bf16[1040,256]{1,0:T(8,128)(2,1)S(1)} collective-permute-done((bf16[1040,256]{1,0:T(8,128)(2,1)S(1)}, bf16[1040,256]{1,0:T(8,128)(2,1)S(1)}, u32[]{:S(2)}, u32[]{:S(2)}) %collective-permute-start.7) | collective-permute-done | bytes 532512 | tf_op jit(solution)/shard_map/ppermute | solution.py:126
  121.6 7.3 %fusion.31 = (f32[1024]{0:T(1024)S(1)}, f32[1024]{0:T(1024)S(1)}, f32[1024]{0:T(1024)S(1)}, f32[1024]{0:T(1024)S(1)}, f32[1024]{0:T(1024)S(1)}, /*index=5*/f32[1024,1024]{0,1:T(8,128)}) fusion(f32[1024,1024]{0,1:T(8,128)S(1)} %get-tuple-element.106, f32[1024]{0:T(1024)S(1)} %get-tuple-element.64, s32[1024]{0:T(1024)S(1)} %bitcast.211, ...), kind=kOutput, calls=%fused_computation.89 | convolution fusion | flops 301984768 | bytes 21569536 | tf_op jit(solution)/shard_map/qhd,khd->hqk/dot_general | solution.py:68
  131.2 8.2 %collective-permute-done.11 = bf16[1040,256]{1,0:T(8,128)(2,1)S(1)} collective-permute-done((bf16[1040,256]{1,0:T(8,128)(2,1)S(1)}, bf16[1040,256]{1,0:T(8,128)(2,1)S(1)}, u32[]{:S(2)}, u32[]{:S(2)}) %collective-permute-start.11) | collective-permute-done | bytes 532512 | tf_op jit(solution)/shard_map/ppermute | solution.py:126
  143.6 7.3 %fusion.33 = (f32[1024]{0:T(1024)S(1)}, f32[1024]{0:T(1024)S(1)}, f32[1024]{0:T(1024)S(1)}, f32[1024]{0:T(1024)S(1)}, f32[1024]{0:T(1024)S(1)}, /*index=5*/f32[1024,1024]{0,1:T(8,128)}) fusion(f32[1024,1024]{0,1:T(8,128)S(1)} %fusion.235, f32[1024]{0:T(1024)S(1)} %get-tuple-element.63, s32[1024]{0:T(1024)S(1)} %bitcast.212, s32[1024]{0:T(1024)S(1)} %bitcast.188, ...), kind=kOutput, calls=%fused_computation.91 | convolution fusion | flops 301984768 | bytes 21569536 | tf_op jit(solution)/shard_map/qhd,khd->hqk/dot_general | solution.py:68
  153.2 9.3 %collective-permute-done.14 = bf16[1040,256]{1,0:T(8,128)(2,1)S(1)} collective-permute-done((bf16[1040,256]{1,0:T(8,128)(2,1)}, bf16[1040,256]{1,0:T(8,128)(2,1)S(1)}, u32[]{:S(2)}, u32[]{:S(2)}) %collective-permute-start.14) | collective-permute-done | bytes 532512 | tf_op jit(solution)/shard_map/ppermute | solution.py:136
  164.0 9.0 %fusion.35 = (f32[1024]{0:T(1024)S(1)}, f32[1024]{0:T(1024)S(1)}, f32[1024]{0:T(1024)S(1)}, f32[1024]{0:T(1024)S(1)}, f32[1024]{0:T(1024)S(1)}, /*index=5*/f32[1024,1024]{0,1:T(8,128)}) fusion(f32[1024,1024]{0,1:T(8,128)S(1)} %fusion.232, f32[1024]{0:T(1024)S(1)} %get-tuple-element.62, s32[1024]{0:T(1024)S(1)} %bitcast.213, s32[1024]{0:T(1024)S(1)} %bitcast.189, ...), kind=kOutput, calls=%fused_computation.93 | convolution fusion | flops 304081920 | bytes 21573632 | tf_op jit(solution)/shard_map/qhd,khd->hqk/dot_general | solution.py:68
  173.1 6.4 %fusion.55 = (f32[1024]{0:T(1024)S(1)}, f32[1024]{0:T(1024)S(1)}, f32[1024]{0:T(1024)S(1)}) fusion(f32[1024,1024]{0,1:T(8,128)} %get-tuple-element.107, f32[1024]{0:T(1024)S(1)} %get-tuple-element.52, s32[1024]{0:T(1024)S(1)} %bitcast.214, s32[1024]{0:T(1024)S(1)} %bitcast.190, s32[1024]{0:T(1024)S(1)} %bitcast.239, s32[1024]{0:T(1024)S(1)} %bitcast.233, ...), kind=kLoop, calls=%fused_computation.113 | loop fusion | flops 25162752 | bytes 12640256 | tf_op jit(solution)/shard_map/reduce_sum | solution.py:79
  179.5 7.3 %fusion.39 = (f32[1024]{0:T(1024)S(1)}, f32[1024]{0:T(1024)S(1)}, f32[1024]{0:T(1024)S(1)}, f32[1024]{0:T(1024)S(1)}) fusion(f32[1024,1024]{0,1:T(8,128)S(1)} %copy-done.7, f32[1024]{0:T(1024)S(1)} %get-tuple-element.60, s32[1024]{0:T(1024)S(1)} %bitcast.215, s32[1024]{0:T(1024)S(1)} %bitcast.191, s32[1024]{0:T(1024)S(1)} %bitcast.254, ...), kind=kLoop, calls=%fused_computation.97 | loop fusion | flops 33550336 | bytes 16850944 | tf_op jit(solution)/shard_map/reduce_sum | solution.py:79
  186.9 8.9 %fusion.47 = (f32[1024]{0:T(1024)S(1)}, f32[1024]{0:T(1024)S(1)}, f32[1024]{0:T(1024)S(1)}, f32[1024]{0:T(1024)S(1)}) fusion(f32[1024,1024]{0,1:T(8,128)} %get-tuple-element.108, f32[1024]{0:T(1024)S(1)} %get-tuple-element.56, s32[1024]{0:T(1024)S(1)} %bitcast.216, s32[1024]{0:T(1024)S(1)} %bitcast.192, s32[1024]{0:T(1024)S(1)} %bitcast.278, ...), kind=kLoop, calls=%fused_computation.105 | loop fusion | flops 33550336 | bytes 16850944 | tf_op jit(solution)/shard_map/reduce_sum | solution.py:79
  235.0 16.8 %all_to_all.24 = bf16[8,128,128]{1,2,0:T(8,128)(2,1)S(1)} all-to-all(bf16[8,128,128]{1,2,0:T(8,128)(2,1)S(1)} %copy.93), channel_id=1, replica_groups=mesh['blk'=16,'x'=4,'core'=2] {'x','core'}, dimensions={0} | all-to-all | bytes 524288 | tf_op jit(solution)/shard_map/all_to_all | solution.py:143
  261.8 70.9 %all_to_all.25 = bf16[64,16,2048]{2,1,0:T(8,128)(2,1)} all-to-all(bf16[64,16,2048]{2,1,0:T(8,128)(2,1)S(1)} %bitcast.179), channel_id=1, replica_groups=mesh['blk'=16,'x'=4,'core'=2] {'blk','x'}, dimensions={0} | all-to-all | bytes 8388608 | tf_op jit(solution)/shard_map/all_to_all | solution.py:181
  342.1 9.9 %multiply_convert_fusion = bf16[1024,2048]{1,0:T(8,128)(2,1)} fusion(bf16[384,2048]{1,0:T(8,128)(2,1)} %param.28, f32[1024]{0:T(1024)S(1)} %add_divide_fusion, f32[1024,384]{1,0:T(8,128)} %fusion.318, bf16[1024,2048]{1,0:T(8,128)(2,1)} %all-gather.7.cloned.1.call-done, bf16[2048,384]{1,0:T(8,128)(2,1)} %param.27), kind=kOutput, calls=%fused_computation.8 | convolution fusion | flops 3227779072 | bytes 13111296 | tf_op jit(solution)/shard_map/dot_general | solution.py:160
  352.0 11.0 %fusion.23 = f32[2048,704]{0,1:T(8,128)} fusion(bf16[2048,2048]{1,0:T(8,128)(2,1)} %bitcast.333, bf16[1,2048,704]{1,2,0:T(8,128)(2,1)} %param.30), kind=kOutput, calls=%fused_computation.79 | convolution fusion | flops 5905580032 | bytes 17039360 | tf_op jit(solution)/shard_map/dot_general | solution.py:186
  363.1 19.3 %convolution_convert_fusion = bf16[2048,2048]{1,0:T(8,128)(2,1)} fusion(f32[2048,704]{0,1:T(8,128)} %fusion.23, bf16[2048,2048]{1,0:T(8,128)(2,1)} %bitcast.334, bf16[1,704,2048]{2,1,0:T(8,128)(2,1)S(1)} %copy-done, bf16[1,2048,704]{1,2,0:T(8,128)(2,1)} %param.31), kind=kOutput, calls=%fused_computation.9 | convolution fusion | flops 11824005120 | bytes 28311552 | tf_op jit(solution)/shard_map/dot_general | solution.py:190
  382.4 12.7 %all_to_all.26 = bf16[2,64,16,2048]{3,2,1,0:T(8,128)(2,1)S(1)} all-to-all(bf16[2,64,16,2048]{3,2,1,0:T(8,128)(2,1)} %bitcast.180), channel_id=1, replica_groups=mesh['blk'=16,'x'=4,'core'=2] {'core'}, dimensions={0} | all-to-all | bytes 16777216 | tf_op jit(solution)/shard_map/all_to_all | solution.py:194
  398.1 9.8 %all-to-all-start.3 = ((bf16[64,16,2048]{2,1,0:T(8,128)(2,1)}), bf16[64,16,2048]{2,1,0:T(8,128)(2,1)}, u32[]{:S(2)}, u32[]{:S(2)}) async-start(bf16[64,16,2048]{2,1,0:T(8,128)(2,1)} %fusion.3), calls=%async_computation.4 | async-start | bytes 8388608 | tf_op jit(solution)/shard_map/all_to_all | solution.py:198
  418.8 42.3 %all-to-all-done.3 = bf16[64,16,2048]{2,1,0:T(8,128)(2,1)} async-done(((bf16[64,16,2048]{2,1,0:T(8,128)(2,1)}), bf16[64,16,2048]{2,1,0:T(8,128)(2,1)}, u32[]{:S(2)}, u32[]{:S(2)}) %all-to-all-start.3) | async-done | bytes 4194336 | tf_op jit(solution)/shard_map/all_to_all | solution.py:198
  461.0 5.4 %fusion.28 = bf16[128,2048]{1,0:T(8,128)(2,1)} fusion(f32[128,1024]{1,0:T(8,128)} %select_reduce_fusion, bf16[1024,2048]{1,0:T(8,128)(2,1)} %bitcast.19, f32[128,2048]{1,0:T(8,128)} %copy-done.3, bf16[128,2048]{1,0:T(8,128)(2,1)} %reduce-scatter.2.cloned.1.call-done), kind=kOutput, calls=%fused_computation.86 | convolution fusion | flops 3222274048 | bytes 6815744 | tf_op jit(solution)/shard_map/dot_general | solution.py:207
  (265 shorter events, 125.4 us)
Async XLA Ops:
  7.2 355.9 %copy-start = (bf16[1,704,2048]{2,1,0:T(8,128)(2,1)S(1)}, bf16[1,704,2048]{2,1,0:T(8,128)(2,1)}, u32[]{:S(2)}) copy-start(bf16[1,704,2048]{2,1,0:T(8,128)(2,1)} %param.32) | copy-start | bytes 8650756
  7.2 38.2 %all-gather.5.cloned.1.call-start = ((), (), s32[]{:S(2)}) async-start(), calls=%async_computation.5 | async-start | bytes 4718592 | tf_op jit(solution)/shard_map/all_gather | solution.py:51
  7.9 325.5 %all-gather.7.cloned.1.call-start = ((), (), s32[]{:S(2)}) async-start(), calls=%async_computation.6 | async-start | bytes 4718592 | tf_op jit(solution)/shard_map/all_gather | solution.py:150
  54.7 14.2 %collective-permute-start.1 = (bf16[1040,256]{1,0:T(8,128)(2,1)}, bf16[1040,256]{1,0:T(8,128)(2,1)S(1)}, u32[]{:S(2)}, u32[]{:S(2)}) collective-permute-start(bf16[1040,256]{1,0:T(8,128)(2,1)} %copy.91), channel_id=1, source_target_pairs={{8,0},{16,8},{24,16},{56,24},{48,56},{40,48},{32,40},{64,32},{72,6... | collective-permute-start | bytes 1597448 | tf_op jit(solution)/shard_map/ppermute | solution.py:131
  57.4 14.8 %collective-permute-start = (bf16[1040,256]{1,0:T(8,128)(2,1)}, bf16[1040,256]{1,0:T(8,128)(2,1)S(1)}, u32[]{:S(2)}, u32[]{:S(2)}) collective-permute-start(bf16[1040,256]{1,0:T(8,128)(2,1)} %copy.91), channel_id=1, source_target_pairs={{0,8},{8,16},{16,24},{24,56},{56,48},{48,40},{40,32},{32,64},{64,7... | collective-permute-start | bytes 1597448 | tf_op jit(solution)/shard_map/ppermute | solution.py:130
  68.9 13.6 %collective-permute-start.3 = (bf16[1040,256]{1,0:T(8,128)(2,1)S(1)}, bf16[1040,256]{1,0:T(8,128)(2,1)S(1)}, u32[]{:S(2)}, u32[]{:S(2)}) collective-permute-start(bf16[1040,256]{1,0:T(8,128)(2,1)S(1)} %collective-permute-done.1), channel_id=1, source_target_pairs={{8,0},{16,8},{24,16},{56,24},{48,56},{40,48},{32,40},{64,32},{72,6... | collective-permute-start | bytes 1597448 | tf_op jit(solution)/shard_map/ppermute | solution.py:126
  72.2 13.7 %collective-permute-start.2 = (bf16[1040,256]{1,0:T(8,128)(2,1)S(1)}, bf16[1040,256]{1,0:T(8,128)(2,1)S(1)}, u32[]{:S(2)}, u32[]{:S(2)}) collective-permute-start(bf16[1040,256]{1,0:T(8,128)(2,1)S(1)} %collective-permute-done), channel_id=1, source_target_pairs={{0,8},{8,16},{16,24},{24,56},{56,48},{48,40},{40,32},{32,64},{64,7... | collective-permute-start | bytes 1597448 | tf_op jit(solution)/shard_map/ppermute | solution.py:125
  73.3 48.3 %copy-start.28 = (s32[1,2,4,128]{3,1,2,0:T(2,128)}, s32[1,2,4,128]{3,1,2,0:T(2,128)S(1)}, u32[]{:S(2)}) copy-start(s32[1,2,4,128]{3,1,2,0:T(2,128)S(1)} %copy.101) | copy-start | bytes 12292
  86.0 78.0 %copy-start.34 = (s32[1,2,4,128]{3,1,2,0:T(2,128)}, s32[1,2,4,128]{3,1,2,0:T(2,128)S(1)}, u32[]{:S(2)}) copy-start(s32[1,2,4,128]{3,1,2,0:T(2,128)S(1)} %copy.105) | copy-start | bytes 12292
  86.0 78.0 %copy-start.36 = (s32[1,2,4,128]{3,1,2,0:T(2,128)}, s32[1,2,4,128]{3,1,2,0:T(2,128)S(1)}, u32[]{:S(2)}) copy-start(s32[1,2,4,128]{3,1,2,0:T(2,128)S(1)} %copy.106) | copy-start | bytes 12292
  93.5 11.5 %collective-permute-start.5 = (bf16[1040,256]{1,0:T(8,128)(2,1)S(1)}, bf16[1040,256]{1,0:T(8,128)(2,1)S(1)}, u32[]{:S(2)}, u32[]{:S(2)}) collective-permute-start(bf16[1040,256]{1,0:T(8,128)(2,1)S(1)} %collective-permute-done.3), channel_id=1, source_target_pairs={{8,0},{16,8},{24,16},{56,24},{48,56},{40,48},{32,40},{64,32},{72,6... | collective-permute-start | bytes 1597448 | tf_op jit(solution)/shard_map/ppermute | solution.py:126
  93.6 12.9 %collective-permute-start.4 = (bf16[1040,256]{1,0:T(8,128)(2,1)S(1)}, bf16[1040,256]{1,0:T(8,128)(2,1)S(1)}, u32[]{:S(2)}, u32[]{:S(2)}) collective-permute-start(bf16[1040,256]{1,0:T(8,128)(2,1)S(1)} %collective-permute-done.2), channel_id=1, source_target_pairs={{0,8},{8,16},{16,24},{24,56},{56,48},{48,40},{40,32},{32,64},{64,7... | collective-permute-start | bytes 1597448 | tf_op jit(solution)/shard_map/ppermute | solution.py:125
  105.0 10.6 %collective-permute-start.7 = (bf16[1040,256]{1,0:T(8,128)(2,1)S(1)}, bf16[1040,256]{1,0:T(8,128)(2,1)S(1)}, u32[]{:S(2)}, u32[]{:S(2)}) collective-permute-start(bf16[1040,256]{1,0:T(8,128)(2,1)S(1)} %collective-permute-done.5), channel_id=1, source_target_pairs={{8,0},{16,8},{24,16},{56,24},{48,56},{40,48},{32,40},{64,32},{72,6... | collective-permute-start | bytes 1597448 | tf_op jit(solution)/shard_map/ppermute | solution.py:126
  106.6 12.0 %collective-permute-start.6 = (bf16[1040,256]{1,0:T(8,128)(2,1)S(1)}, bf16[1040,256]{1,0:T(8,128)(2,1)S(1)}, u32[]{:S(2)}, u32[]{:S(2)}) collective-permute-start(bf16[1040,256]{1,0:T(8,128)(2,1)S(1)} %collective-permute-done.4), channel_id=1, source_target_pairs={{0,8},{8,16},{16,24},{24,56},{56,48},{48,40},{40,32},{32,64},{64,7... | collective-permute-start | bytes 1597448 | tf_op jit(solution)/shard_map/ppermute | solution.py:125
  118.6 10.3 %collective-permute-start.9 = (bf16[1040,256]{1,0:T(8,128)(2,1)S(1)}, bf16[1040,256]{1,0:T(8,128)(2,1)S(1)}, u32[]{:S(2)}, u32[]{:S(2)}) collective-permute-start(bf16[1040,256]{1,0:T(8,128)(2,1)S(1)} %collective-permute-done.7), channel_id=1, source_target_pairs={{8,0},{16,8},{24,16},{56,24},{48,56},{40,48},{32,40},{64,32},{72,6... | collective-permute-start | bytes 1597448 | tf_op jit(solution)/shard_map/ppermute | solution.py:126
  118.7 11.5 %collective-permute-start.8 = (bf16[1040,256]{1,0:T(8,128)(2,1)S(1)}, bf16[1040,256]{1,0:T(8,128)(2,1)S(1)}, u32[]{:S(2)}, u32[]{:S(2)}) collective-permute-start(bf16[1040,256]{1,0:T(8,128)(2,1)S(1)} %collective-permute-done.6), channel_id=1, source_target_pairs={{0,8},{8,16},{16,24},{24,56},{56,48},{48,40},{40,32},{32,64},{64,7... | collective-permute-start | bytes 1597448 | tf_op jit(solution)/shard_map/ppermute | solution.py:125
  128.9 10.5 %collective-permute-start.11 = (bf16[1040,256]{1,0:T(8,128)(2,1)S(1)}, bf16[1040,256]{1,0:T(8,128)(2,1)S(1)}, u32[]{:S(2)}, u32[]{:S(2)}) collective-permute-start(bf16[1040,256]{1,0:T(8,128)(2,1)S(1)} %collective-permute-done.9), channel_id=1, source_target_pairs={{8,0},{16,8},{24,16},{56,24},{48,56},{40,48},{32,40},{64,32},{72,6... | collective-permute-start | bytes 1597448 | tf_op jit(solution)/shard_map/ppermute | solution.py:126
  130.2 10.4 %collective-permute-start.10 = (bf16[1040,256]{1,0:T(8,128)(2,1)S(1)}, bf16[1040,256]{1,0:T(8,128)(2,1)S(1)}, u32[]{:S(2)}, u32[]{:S(2)}) collective-permute-start(bf16[1040,256]{1,0:T(8,128)(2,1)S(1)} %collective-permute-done.8), channel_id=1, source_target_pairs={{0,8},{8,16},{16,24},{24,56},{56,48},{48,40},{40,32},{32,64},{64,7... | collective-permute-start | bytes 1597448 | tf_op jit(solution)/shard_map/ppermute | solution.py:125
  140.7 10.3 %collective-permute-start.13 = (bf16[1040,256]{1,0:T(8,128)(2,1)S(1)}, bf16[1040,256]{1,0:T(8,128)(2,1)S(1)}, u32[]{:S(2)}, u32[]{:S(2)}) collective-permute-start(bf16[1040,256]{1,0:T(8,128)(2,1)S(1)} %collective-permute-done.11), channel_id=1, source_target_pairs={{8,0},{16,8},{24,16},{56,24},{48,56},{40,48},{32,40},{64,32},{72,6... | collective-permute-start | bytes 1597448 | tf_op jit(solution)/shard_map/ppermute | solution.py:126
  141.0 10.2 %collective-permute-start.12 = (bf16[1040,256]{1,0:T(8,128)(2,1)S(1)}, bf16[1040,256]{1,0:T(8,128)(2,1)}, u32[]{:S(2)}, u32[]{:S(2)}) collective-permute-start(bf16[1040,256]{1,0:T(8,128)(2,1)S(1)} %collective-permute-done.10), channel_id=1, source_target_pairs={{0,8},{8,16},{16,24},{24,56},{56,48},{48,40},{40,32},{32,64},{64,7... | collective-permute-start | bytes 1597448 | tf_op jit(solution)/shard_map/ppermute | solution.py:125
  151.8 10.7 %collective-permute-start.14 = (bf16[1040,256]{1,0:T(8,128)(2,1)}, bf16[1040,256]{1,0:T(8,128)(2,1)S(1)}, u32[]{:S(2)}, u32[]{:S(2)}) collective-permute-start(bf16[1040,256]{1,0:T(8,128)(2,1)} %collective-permute-done.12), channel_id=1, source_target_pairs={{0,8},{8,16},{16,24},{24,56},{56,48},{48,40},{40,32},{32,64},{64,7... | collective-permute-start | bytes 1597448 | tf_op jit(solution)/shard_map/ppermute | solution.py:136
  256.9 95.1 %all-gather.9.cloned.1.call-start = ((), (), s32[]{:S(2)}) async-start(), calls=%async_computation.8 | async-start | bytes 12582912 | tf_op jit(solution)/shard_map/all_gather | solution.py:182
  332.7 86.1 %reduce-scatter.2.cloned.1.call-start = ((), (), s32[]{:S(2)}) async-start(), calls=%async_computation.7 | async-start | bytes 4718592 | tf_op jit(solution)/shard_map/reduce_scatter | solution.py:158
  398.1 62.9 %all-to-all-start.3 = ((bf16[64,16,2048]{2,1,0:T(8,128)(2,1)}), bf16[64,16,2048]{2,1,0:T(8,128)(2,1)}, u32[]{:S(2)}, u32[]{:S(2)}) async-start(bf16[64,16,2048]{2,1,0:T(8,128)(2,1)} %fusion.3), calls=%async_computation.4 | async-start | bytes 8388608 | tf_op jit(solution)/shard_map/all_to_all | solution.py:198
  (43 other events, 383.8 us)
Sparse Core Ops, SparseCore 0:
  9.7 35.6 all-gather.4
  257.0 54.5 all-gather.6
  332.8 18.7 all-gather.8
  353.9 35.9 reduce-scatter.1

commit v10 on v7

--- a/solution.py
+++ b/solution.py
@@ -195,12 +195,12 @@
         both_halves[0].astype(jnp.float32) + both_halves[1].astype(jnp.float32)
     ).astype(jnp.bfloat16)
     returned = lax.all_to_all(summed_halves, CHIPS, split_axis=0, concat_axis=0, tiled=True)
-    gather_pick = (target[:, None] == slot_ids[None, :]).astype(jnp.bfloat16)
+    target_by_choice = target.reshape(local_rows, TOP).T.reshape(-1)
+    gather_pick = (target_by_choice[:, None] == slot_ids[None, :]).astype(jnp.bfloat16)
     picked = jnp.dot(
         gather_pick, returned.reshape(-1, D), preferred_element_type=jnp.float32
-    ) * route_weights.reshape(-1)[:, None]
-    routed = jnp.sum(picked.reshape(local_rows, TOP, D), axis=1)
-    routed = jnp.sum(picked.reshape(local_rows, TOP, D), axis=1)
+    ) * route_weights.T.reshape(-1)[:, None]
+    routed = jnp.sum(picked.reshape(TOP, local_rows, D), axis=0)
     final = (resid_local.astype(jnp.float32) + shared_local + routed).astype(jnp.bfloat16)
     return (final, cache_keys, cache_values)
 

time: 471 us -> 464 us (0.985)
  local copies, waits for them, and re-layouts: 38.9 us -> 33.5 us
    reshape x2 -> x0, local copies, waits for them, and re-layouts: 5.28 us -> none  [the longest x1 5.17 us: per_device(): routed = jnp.sum(picked.reshape(local_rows, TOP, D), axis=1)]
  transfers between devices with their start and end apart: 20 -> 20, of which waited for: 5 -> 5; matrix products, arithmetic and copies ran while one was open for 41% -> 40% of each run, Pallas kernels for 0% -> 0%
where the time goes in v10:
time: 464 us; the launch traced here: 456 us
  matrix products  152 us (33%)
  blocking collectives  111 us (24%)
  waiting for transfers between devices  76.9 us (17%)
  other arithmetic  38 us (8%)
  local copies, waits for them, and re-layouts  33.5 us (7%)
  starting transfers between devices  29.5 us (6%)
  between operations  14.5 us (3%)
    all_to_all x1, blocking collectives, per_device(): lax.all_to_all(outgoing, CHIPS, split_axis=0, concat_axis=0, tiled=True)  69.9 us
    dot_general x16, matrix products, attend(): jnp.einsum('qhd,khd->hqk', query_heads, block_keys, preferred_element_typ...  43.9 us
    all_to_all x1, waiting for transfers between devices, per_device(): lax.all_to_all(summed_halves, CHIPS, split_axis=0, concat_axis=0, tiled=T...  43.4 us
    dot_general x16, matrix products, attend(): jnp.einsum('hqk,khd->hqd', probs.astype(jnp.bfloat16), block_values, pref...  40.5 us
    all_gather x1, waiting for transfers between devices, per_device(): group_stream = lax.all_gather(stream, EXP, axis=0, tiled=True)  22.5 us
    dot_general x1, matrix products, per_device(): jnp.dot(hidden, expert_down[0], preferred_element_type=jnp.float32)  19.4 us
    another operation x13, local copies, waits for them, and re-layouts  17.5 us
    ppermute x6, starting transfers between devices, ring_step(): behind = lax.ppermute(behind, 'blk', backward)  16 us
  transfers between devices with their start and end apart: 20, of which 5 were waited for; matrix products, arithmetic and copies ran while one was open for 40% of the time, Pallas kernels for 0%

profile of v10, /device:TPU:1, one launch (start us, length us, event | category | flops | bytes accessed | tf_op | source)
XLA Modules:
  0.0 456.2 jit_solution(14096025891108505901)
XLA Ops:
  8.8 13.3 %all_gather.15 = s32[3,1024]{1,0:T(4,128)S(1)} all-gather(s32[3,128]{1,0:T(4,128)S(1)} %pad_add_fusion), channel_id=1, replica_groups=mesh['blk'=16,'x'=4,'core'=2] {'x','core'}, dimensions={1}, use_global_device_ids=true | all-gather | bytes 13824 | tf_op jit(solution)/shard_map/all_gather | solution.py:50
  22.9 22.5 %all-gather.5.cloned.1.call-done = bf16[1024,2048]{1,0:T(8,128)(2,1)} async-done(((bf16[128,2048]{1,0:T(8,128)(2,1)}), bf16[1024,2048]{1,0:T(8,128)(2,1)}) %all-gather.5.cloned.1.call-update) | async-done | bytes 4194320 | tf_op jit(solution)/shard_map/all_gather | solution.py:51
  72.2 114.0 %while.18 = (s32[]{:T(128)}, f32[1,1024]{1,0:T(1,128)S(1)}, f32[1,1024]{1,0:T(1,128)S(1)}, f32[1,1024,128]{2,1,0:T(8,128)}, bf16[1040,256]{1,0:T(8,128)(2,1)}, /...) while((s32[]{:T(128)}, f32[1,1024]{1,0:T(1,128)S(1)}, ...), condition=%wide.region_8.9_spmd, body=%wide.region_3.8_spmd.sunk | while | flops 1120417792 | bytes 38682860 | solution.py:132
  80.7 3.7 fusion.185
  99.7 3.7 fusion.185
  118.7 3.7 fusion.185
  137.7 3.7 fusion.185
  156.7 3.7 fusion.185
  175.7 3.7 fusion.185
  192.3 4.6 %collective-permute-done.4 = bf16[1040,256]{1,0:T(8,128)(2,1)S(1)} collective-permute-done((bf16[1040,256]{1,0:T(8,128)(2,1)}, bf16[1040,256]{1,0:T(8,128)(2,1)S(1)}, u32[]{:S(2)}, u32[]{:S(2)}) %collective-permute-start.4) | collective-permute-done | bytes 532512 | tf_op jit(solution)/shard_map/ppermute | solution.py:135
  197.7 4.9 %fusion.59 = (f32[1024]{0:T(1024)S(1)}, f32[1024]{0:T(1024)S(1)}, f32[1024]{0:T(1024)S(1)}, f32[1024,1024]{0,1:T(8,128)S(1)}) fusion(f32[1024,1024]{0,1:T(8,128)S(1)} %get-tuple-element.148, f32[1024]{0:T(1024)S(1)} %bitcast.282, s32[1024]{0:T(1024)S(1)} %bitcast.262, s32[1024]{0:T(1024)S(1)} %bitcast.243, s32[1024]{0:T(1024)S(1)} %bitcast.319, ...), kind=kOutput, calls=%fused_computation.86 | convolution fusion | flops 289403904 | bytes 13156352 | tf_op jit(solution)/shard_map/qhd,khd->hqk/dot_general | solution.py:68
  212.9 15.4 %all_to_all.24 = bf16[8,128,128]{1,2,0:T(8,128)(2,1)S(1)} all-to-all(bf16[8,128,128]{1,2,0:T(8,128)(2,1)} %copy.77), channel_id=1, replica_groups=mesh['blk'=16,'x'=4,'core'=2] {'x','core'}, dimensions={0} | all-to-all | bytes 524288 | tf_op jit(solution)/shard_map/all_to_all | solution.py:142
  238.4 69.9 %all_to_all.25 = bf16[64,16,2048]{2,1,0:T(8,128)(2,1)} all-to-all(bf16[64,16,2048]{2,1,0:T(8,128)(2,1)S(1)} %bitcast.216), channel_id=1, replica_groups=mesh['blk'=16,'x'=4,'core'=2] {'blk','x'}, dimensions={0} | all-to-all | bytes 8388608 | tf_op jit(solution)/shard_map/all_to_all | solution.py:180
  312.6 5.2 %fusion.143 = f32[1024,384]{1,0:T(8,128)} fusion(bf16[1024,2048]{1,0:T(8,128)(2,1)S(1)} %copy-done.4, bf16[2048,384]{1,0:T(8,128)(2,1)} %param.28), kind=kOutput, calls=%fused_computation.195 | convolution fusion | flops 1610612736 | bytes 7340032 | tf_op jit(solution)/shard_map/dot_general | solution.py:151
  317.7 9.8 %multiply_convert_fusion = bf16[1024,2048]{1,0:T(8,128)(2,1)} fusion(bf16[384,2048]{1,0:T(8,128)(2,1)} %param.30, f32[1024]{0:T(1024)S(1)} %add_divide_fusion, f32[1024,384]{1,0:T(8,128)} %fusion.143, bf16[1024,2048]{1,0:T(8,128)(2,1)} %all-gather.7.cloned.1.call-done, bf16[2048,384]{1,0:T(8,128)(2,1)} %param.29), kind=kOutput, calls=%fused_computation.54 | convolution fusion | flops 3227779072 | bytes 13111296 | tf_op jit(solution)/shard_map/dot_general | solution.py:159
  327.6 11.0 %fusion.52 = f32[2048,704]{0,1:T(8,128)} fusion(bf16[2048,2048]{1,0:T(8,128)(2,1)} %bitcast.325, bf16[1,2048,704]{1,2,0:T(8,128)(2,1)} %param.32), kind=kOutput, calls=%fused_computation.78 | convolution fusion | flops 5905580032 | bytes 17039360 | tf_op jit(solution)/shard_map/dot_general | solution.py:185
  338.6 19.4 %convolution_convert_fusion = bf16[2048,2048]{1,0:T(8,128)(2,1)} fusion(f32[2048,704]{0,1:T(8,128)} %fusion.52, bf16[2048,2048]{1,0:T(8,128)(2,1)} %bitcast.326, bf16[1,704,2048]{2,1,0:T(8,128)(2,1)S(1)} %copy-done, bf16[1,2048,704]{1,2,0:T(8,128)(2,1)} %param.33), kind=kOutput, calls=%fused_computation.55 | convolution fusion | flops 11824005120 | bytes 28311552 | tf_op jit(solution)/shard_map/dot_general | solution.py:189
  358.0 12.6 %all_to_all.26 = bf16[2,64,16,2048]{3,2,1,0:T(8,128)(2,1)S(1)} all-to-all(bf16[2,64,16,2048]{3,2,1,0:T(8,128)(2,1)} %bitcast.217), channel_id=1, replica_groups=mesh['blk'=16,'x'=4,'core'=2] {'core'}, dimensions={0} | all-to-all | bytes 16777216 | tf_op jit(solution)/shard_map/all_to_all | solution.py:193
  373.6 9.9 %all-to-all-start.3 = ((bf16[64,16,2048]{2,1,0:T(8,128)(2,1)}), bf16[64,16,2048]{2,1,0:T(8,128)(2,1)}, u32[]{:S(2)}, u32[]{:S(2)}) async-start(bf16[64,16,2048]{2,1,0:T(8,128)(2,1)} %fusion.44), calls=%async_computation.4 | async-start | bytes 8388608 | tf_op jit(solution)/shard_map/all_to_all | solution.py:197
  385.2 4.2 scatter_custom_fusion
  389.4 3.8 scatter_custom_fusion.1
  393.2 43.4 %all-to-all-done.3 = bf16[64,16,2048]{2,1,0:T(8,128)(2,1)} async-done(((bf16[64,16,2048]{2,1,0:T(8,128)(2,1)}), bf16[64,16,2048]{2,1,0:T(8,128)(2,1)}, u32[]{:S(2)}, u32[]{:S(2)}) %all-to-all-start.3) | async-done | bytes 4194336 | tf_op jit(solution)/shard_map/all_to_all | solution.py:197
  436.6 6.5 %convolution_multiply_fusion = f32[512,2048]{1,0:T(8,128)} fusion(bf16[1024,2048]{1,0:T(8,128)(2,1)} %bitcast.54, f32[512]{0:T(512)S(1)} %bitcast.327, s32[512]{0:T(512)S(1)} %bitcast.305), kind=kOutput, calls=%fused_computation.75 | convolution fusion | flops 2149056512 | bytes 8392704 | tf_op jit(solution)/shard_map/dot_general | solution.py:200
  443.2 3.6 reduce_sum.116
  (278 shorter events, 158.4 us)
Async XLA Ops:
  7.2 331.4 %copy-start = (bf16[1,704,2048]{2,1,0:T(8,128)(2,1)S(1)}, bf16[1,704,2048]{2,1,0:T(8,128)(2,1)}, u32[]{:S(2)}) copy-start(bf16[1,704,2048]{2,1,0:T(8,128)(2,1)} %param.34) | copy-start | bytes 8650756
  7.2 41.4 %copy-start.18 = (f32[2048]{0:T(1024)S(1)}, f32[2048]{0:T(1024)}, u32[]{:S(2)}) copy-start(f32[2048]{0:T(1024)} %param.22) | copy-start | bytes 24580
  7.2 38.2 %all-gather.5.cloned.1.call-start = ((), (), s32[]{:S(2)}) async-start(), calls=%async_computation.5 | async-start | bytes 4718592 | tf_op jit(solution)/shard_map/all_gather | solution.py:51
  7.9 301.1 %all-gather.7.cloned.1.call-start = ((), (), s32[]{:S(2)}) async-start(), calls=%async_computation.6 | async-start | bytes 4718592 | tf_op jit(solution)/shard_map/all_gather | solution.py:149
  54.8 14.2 %collective-permute-start.3 = (bf16[1040,256]{1,0:T(8,128)(2,1)}, bf16[1040,256]{1,0:T(8,128)(2,1)}, u32[]{:S(2)}, u32[]{:S(2)}) collective-permute-start(bf16[1040,256]{1,0:T(8,128)(2,1)} %copy.75), channel_id=1, source_target_pairs={{8,0},{16,8},{24,16},{56,24},{48,56},{40,48},{32,40},{64,32},{72,6... | collective-permute-start | bytes 1597448 | tf_op jit(solution)/shard_map/ppermute | solution.py:131
  57.4 14.8 %collective-permute-start.2 = (bf16[1040,256]{1,0:T(8,128)(2,1)}, bf16[1040,256]{1,0:T(8,128)(2,1)}, u32[]{:S(2)}, u32[]{:S(2)}) collective-permute-start(bf16[1040,256]{1,0:T(8,128)(2,1)} %copy.75), channel_id=1, source_target_pairs={{0,8},{8,16},{16,24},{24,56},{56,48},{48,40},{40,32},{32,64},{64,7... | collective-permute-start | bytes 1597448 | tf_op jit(solution)/shard_map/ppermute | solution.py:130
  73.3 18.0 %collective-permute-start = (bf16[1040,256]{1,0:T(8,128)(2,1)S(1)}, bf16[1040,256]{1,0:T(8,128)(2,1)}, u32[]{:S(2)}, u32[]{:S(2)}) collective-permute-start(bf16[1040,256]{1,0:T(8,128)(2,1)S(1)} %copy.114), channel_id=1, source_target_pairs={{0,8},{8,16},{16,24},{24,56},{56,48},{48,40},{40,32},{32,64},{64,7... | collective-permute-start | bytes 1597448 | tf_op jit(solution)/shard_map/while/body/eval_jaxpr/ppermute | solution.py:125
  75.1 16.1 %collective-permute-start.1 = (bf16[1040,256]{1,0:T(8,128)(2,1)}, bf16[1040,256]{1,0:T(8,128)(2,1)}, u32[]{:S(2)}, u32[]{:S(2)}) collective-permute-start(bf16[1040,256]{1,0:T(8,128)(2,1)} %copy.115), channel_id=1, source_target_pairs={{8,0},{16,8},{24,16},{56,24},{48,56},{40,48},{32,40},{64,32},{72,6... | collective-permute-start | bytes 1597448 | tf_op jit(solution)/shard_map/while/body/eval_jaxpr/ppermute | solution.py:126
  92.3 17.9 %collective-permute-start = (bf16[1040,256]{1,0:T(8,128)(2,1)S(1)}, bf16[1040,256]{1,0:T(8,128)(2,1)}, u32[]{:S(2)}, u32[]{:S(2)}) collective-permute-start(bf16[1040,256]{1,0:T(8,128)(2,1)S(1)} %copy.114), channel_id=1, source_target_pairs={{0,8},{8,16},{16,24},{24,56},{56,48},{48,40},{40,32},{32,64},{64,7... | collective-permute-start | bytes 1597448 | tf_op jit(solution)/shard_map/while/body/eval_jaxpr/ppermute | solution.py:125
  94.1 16.1 %collective-permute-start.1 = (bf16[1040,256]{1,0:T(8,128)(2,1)}, bf16[1040,256]{1,0:T(8,128)(2,1)}, u32[]{:S(2)}, u32[]{:S(2)}) collective-permute-start(bf16[1040,256]{1,0:T(8,128)(2,1)} %copy.115), channel_id=1, source_target_pairs={{8,0},{16,8},{24,16},{56,24},{48,56},{40,48},{32,40},{64,32},{72,6... | collective-permute-start | bytes 1597448 | tf_op jit(solution)/shard_map/while/body/eval_jaxpr/ppermute | solution.py:126
  111.3 17.9 %collective-permute-start = (bf16[1040,256]{1,0:T(8,128)(2,1)S(1)}, bf16[1040,256]{1,0:T(8,128)(2,1)}, u32[]{:S(2)}, u32[]{:S(2)}) collective-permute-start(bf16[1040,256]{1,0:T(8,128)(2,1)S(1)} %copy.114), channel_id=1, source_target_pairs={{0,8},{8,16},{16,24},{24,56},{56,48},{48,40},{40,32},{32,64},{64,7... | collective-permute-start | bytes 1597448 | tf_op jit(solution)/shard_map/while/body/eval_jaxpr/ppermute | solution.py:125
  113.1 16.1 %collective-permute-start.1 = (bf16[1040,256]{1,0:T(8,128)(2,1)}, bf16[1040,256]{1,0:T(8,128)(2,1)}, u32[]{:S(2)}, u32[]{:S(2)}) collective-permute-start(bf16[1040,256]{1,0:T(8,128)(2,1)} %copy.115), channel_id=1, source_target_pairs={{8,0},{16,8},{24,16},{56,24},{48,56},{40,48},{32,40},{64,32},{72,6... | collective-permute-start | bytes 1597448 | tf_op jit(solution)/shard_map/while/body/eval_jaxpr/ppermute | solution.py:126
  130.3 17.9 %collective-permute-start = (bf16[1040,256]{1,0:T(8,128)(2,1)S(1)}, bf16[1040,256]{1,0:T(8,128)(2,1)}, u32[]{:S(2)}, u32[]{:S(2)}) collective-permute-start(bf16[1040,256]{1,0:T(8,128)(2,1)S(1)} %copy.114), channel_id=1, source_target_pairs={{0,8},{8,16},{16,24},{24,56},{56,48},{48,40},{40,32},{32,64},{64,7... | collective-permute-start | bytes 1597448 | tf_op jit(solution)/shard_map/while/body/eval_jaxpr/ppermute | solution.py:125
  132.1 16.1 %collective-permute-start.1 = (bf16[1040,256]{1,0:T(8,128)(2,1)}, bf16[1040,256]{1,0:T(8,128)(2,1)}, u32[]{:S(2)}, u32[]{:S(2)}) collective-permute-start(bf16[1040,256]{1,0:T(8,128)(2,1)} %copy.115), channel_id=1, source_target_pairs={{8,0},{16,8},{24,16},{56,24},{48,56},{40,48},{32,40},{64,32},{72,6... | collective-permute-start | bytes 1597448 | tf_op jit(solution)/shard_map/while/body/eval_jaxpr/ppermute | solution.py:126
  149.3 17.9 %collective-permute-start = (bf16[1040,256]{1,0:T(8,128)(2,1)S(1)}, bf16[1040,256]{1,0:T(8,128)(2,1)}, u32[]{:S(2)}, u32[]{:S(2)}) collective-permute-start(bf16[1040,256]{1,0:T(8,128)(2,1)S(1)} %copy.114), channel_id=1, source_target_pairs={{0,8},{8,16},{16,24},{24,56},{56,48},{48,40},{40,32},{32,64},{64,7... | collective-permute-start | bytes 1597448 | tf_op jit(solution)/shard_map/while/body/eval_jaxpr/ppermute | solution.py:125
  151.1 16.1 %collective-permute-start.1 = (bf16[1040,256]{1,0:T(8,128)(2,1)}, bf16[1040,256]{1,0:T(8,128)(2,1)}, u32[]{:S(2)}, u32[]{:S(2)}) collective-permute-start(bf16[1040,256]{1,0:T(8,128)(2,1)} %copy.115), channel_id=1, source_target_pairs={{8,0},{16,8},{24,16},{56,24},{48,56},{40,48},{32,40},{64,32},{72,6... | collective-permute-start | bytes 1597448 | tf_op jit(solution)/shard_map/while/body/eval_jaxpr/ppermute | solution.py:126
  168.3 17.9 %collective-permute-start = (bf16[1040,256]{1,0:T(8,128)(2,1)S(1)}, bf16[1040,256]{1,0:T(8,128)(2,1)}, u32[]{:S(2)}, u32[]{:S(2)}) collective-permute-start(bf16[1040,256]{1,0:T(8,128)(2,1)S(1)} %copy.114), channel_id=1, source_target_pairs={{0,8},{8,16},{16,24},{24,56},{56,48},{48,40},{40,32},{32,64},{64,7... | collective-permute-start | bytes 1597448 | tf_op jit(solution)/shard_map/while/body/eval_jaxpr/ppermute | solution.py:125
  170.1 16.1 %collective-permute-start.1 = (bf16[1040,256]{1,0:T(8,128)(2,1)}, bf16[1040,256]{1,0:T(8,128)(2,1)}, u32[]{:S(2)}, u32[]{:S(2)}) collective-permute-start(bf16[1040,256]{1,0:T(8,128)(2,1)} %copy.115), channel_id=1, source_target_pairs={{8,0},{16,8},{24,16},{56,24},{48,56},{40,48},{32,40},{64,32},{72,6... | collective-permute-start | bytes 1597448 | tf_op jit(solution)/shard_map/while/body/eval_jaxpr/ppermute | solution.py:126
  186.2 10.7 %collective-permute-start.4 = (bf16[1040,256]{1,0:T(8,128)(2,1)}, bf16[1040,256]{1,0:T(8,128)(2,1)S(1)}, u32[]{:S(2)}, u32[]{:S(2)}) collective-permute-start(bf16[1040,256]{1,0:T(8,128)(2,1)} %get-tuple-element.56), channel_id=1, source_target_pairs={{0,8},{8,16},{16,24},{24,56},{56,48},{48,40},{40,32},{32,64},{64,7... | collective-permute-start | bytes 1597448 | tf_op jit(solution)/shard_map/ppermute | solution.py:135
  211.1 21.2 %copy-start.19 = (f32[2048]{0:T(1024)S(1)}, f32[2048]{0:T(1024)}, u32[]{:S(2)}) copy-start(f32[2048]{0:T(1024)} %param.27) | copy-start | bytes 24580
  233.3 94.2 %all-gather.9.cloned.1.call-start = ((), (), s32[]{:S(2)}) async-start(), calls=%async_computation.8 | async-start | bytes 12582912 | tf_op jit(solution)/shard_map/all_gather | solution.py:181
  308.3 138.5 %reduce-scatter.2.cloned.1.call-start = ((), (), s32[]{:S(2)}) async-start(), calls=%async_computation.7 | async-start | bytes 4718592 | tf_op jit(solution)/shard_map/reduce_scatter | solution.py:157
  373.6 63.1 %copy-start.22 = (f32[128,4]{0,1:T(4,128)S(1)}, f32[128,4]{0,1:T(4,128)}, u32[]{:S(2)}) copy-start(f32[128,4]{0,1:T(4,128)} %param.36) | copy-start | bytes 6148
  373.6 63.1 %all-to-all-start.3 = ((bf16[64,16,2048]{2,1,0:T(8,128)(2,1)}), bf16[64,16,2048]{2,1,0:T(8,128)(2,1)}, u32[]{:S(2)}, u32[]{:S(2)}) async-start(bf16[64,16,2048]{2,1,0:T(8,128)(2,1)} %fusion.44), calls=%async_computation.4 | async-start | bytes 8388608 | tf_op jit(solution)/shard_map/all_to_all | solution.py:197
  (31 other events, 109.9 us)
Sparse Core Ops, SparseCore 0:
  9.7 35.6 all-gather.4
  233.4 51.9 all-gather.6
  308.4 18.8 all-gather.8
  329.5 35.9 reduce-scatter.1

commit v11 on v10

--- a/solution.py
+++ b/solution.py
@@ -190,10 +190,14 @@
         .astype(jnp.bfloat16)
         .reshape(leading + (D,))
     )
-    both_halves = lax.all_to_all(half_out, "core", split_axis=0, concat_axis=0, tiled=True)
-    summed_halves = (
-        both_halves[0].astype(jnp.float32) + both_halves[1].astype(jnp.float32)
-    ).astype(jnp.bfloat16)
+    core = lax.axis_index("core")
+    own_half = lax.dynamic_index_in_dim(half_out, core, 0, keepdims=False)
+    other_half = lax.ppermute(
+        lax.dynamic_index_in_dim(half_out, 1 - core, 0, keepdims=False), "core", [(0, 1), (1, 0)]
+    )
+    summed_halves = (own_half.astype(jnp.float32) + other_half.astype(jnp.float32)).astype(
+        jnp.bfloat16
+    )
     returned = lax.all_to_all(summed_halves, CHIPS, split_axis=0, concat_axis=0, tiled=True)
     target_by_choice = target.reshape(local_rows, TOP).T.reshape(-1)
     gather_pick = (target_by_choice[:, None] == slot_ids[None, :]).astype(jnp.bfloat16)

time: 464 us -> 481 us (1.037)
  waiting for transfers between devices: 76.9 us -> 98.6 us
  blocking collectives: 111 us -> 98.6 us
    all_to_all x1 -> x0, blocking collectives: 12.6 us -> none  [per_device(): lax.all_to_all(half_out, 'core', split_axis=0, concat_axis=0, tiled=True)]
    all_to_all x1, waiting for transfers between devices: 43.4 us -> 55.6 us  [per_device(): lax.all_to_all(summed_halves, CHIPS, split_axis=0, concat_axis=0, tiled=T...]
    all_gather x1, waiting for transfers between devices: 0.02 us -> 9.61 us  [per_device(): arrived = lax.all_gather(arrived, 'core', axis=0)]
  transfers between devices with their start and end apart: 20 -> 21, of which waited for: 5 -> 6; matrix products, arithmetic and copies ran while one was open for 40% -> 33% of each run, Pallas kernels for 0% -> 0%
where the time goes in v11:
time: 481 us; the launch traced here: 474 us
  matrix products  150 us (31%)
  waiting for transfers between devices  98.6 us (20%)
  blocking collectives  98.6 us (20%)
  other arithmetic  42.7 us (9%)
  local copies, waits for them, and re-layouts  38.2 us (8%)
  starting transfers between devices  30.5 us (6%)
  between operations  14.5 us (3%)
    all_to_all x1, blocking collectives, per_device(): lax.all_to_all(outgoing, CHIPS, split_axis=0, concat_axis=0, tiled=True)  69.9 us
    all_to_all x1, waiting for transfers between devices, per_device(): lax.all_to_all(summed_halves, CHIPS, split_axis=0, concat_axis=0, tiled=T...  55.6 us
    dot_general x16, matrix products, attend(): jnp.einsum('qhd,khd->hqk', query_heads, block_keys, preferred_element_typ...  43.9 us
    dot_general x16, matrix products, attend(): jnp.einsum('hqk,khd->hqd', probs.astype(jnp.bfloat16), block_values, pref...  40.5 us
    all_gather x1, waiting for transfers between devices, per_device(): group_stream = lax.all_gather(stream, EXP, axis=0, tiled=True)  22.5 us
    dot_general x1, matrix products, per_device(): jnp.dot(hidden, expert_down[0], preferred_element_type=jnp.float32)  19.1 us
    another operation x13, local copies, waits for them, and re-layouts  17.5 us
    ppermute x6, starting transfers between devices, ring_step(): behind = lax.ppermute(behind, 'blk', backward)  16 us
  transfers between devices with their start and end apart: 21, of which 6 were waited for; matrix products, arithmetic and copies ran while one was open for 33% of the time, Pallas kernels for 0%

profile of v11, /device:TPU:1, one launch (start us, length us, event | category | flops | bytes accessed | tf_op | source)
XLA Modules:
  0.0 474.5 jit_solution(15631455821458677582)
XLA Ops:
  8.8 13.3 %all_gather.15 = s32[3,1024]{1,0:T(4,128)S(1)} all-gather(s32[3,128]{1,0:T(4,128)S(1)} %pad_add_fusion), channel_id=1, replica_groups=mesh['blk'=16,'x'=4,'core'=2] {'x','core'}, dimensions={1}, use_global_device_ids=true | all-gather | bytes 13824 | tf_op jit(solution)/shard_map/all_gather | solution.py:50
  22.9 22.5 %all-gather.5.cloned.1.call-done = bf16[1024,2048]{1,0:T(8,128)(2,1)} async-done(((bf16[128,2048]{1,0:T(8,128)(2,1)}), bf16[1024,2048]{1,0:T(8,128)(2,1)}) %all-gather.5.cloned.1.call-update) | async-done | bytes 4194320 | tf_op jit(solution)/shard_map/all_gather | solution.py:51
  72.2 114.0 %while.18 = (s32[]{:T(128)}, f32[1,1024]{1,0:T(1,128)S(1)}, f32[1,1024]{1,0:T(1,128)S(1)}, f32[1,1024,128]{2,1,0:T(8,128)}, bf16[1040,256]{1,0:T(8,128)(2,1)}, /...) while((s32[]{:T(128)}, f32[1,1024]{1,0:T(1,128)S(1)}, ...), condition=%wide.region_8.9_spmd, body=%wide.region_3.8_spmd.sunk | while | flops 1120417792 | bytes 38682860 | solution.py:132
  99.7 3.7 fusion.185
  118.7 3.7 fusion.185
  137.7 3.7 fusion.185
  156.7 3.7 fusion.185
  175.7 3.7 fusion.185
  192.3 4.6 collective-permute-done.4
  197.7 4.9 %fusion.59 = (f32[1024]{0:T(1024)S(1)}, f32[1024]{0:T(1024)S(1)}, f32[1024]{0:T(1024)S(1)}, f32[1024,1024]{0,1:T(8,128)S(1)}) fusion(f32[1024,1024]{0,1:T(8,128)S(1)} %get-tuple-element.148, f32[1024]{0:T(1024)S(1)} %bitcast.286, s32[1024]{0:T(1024)S(1)} %bitcast.266, s32[1024]{0:T(1024)S(1)} %bitcast.247, s32[1024]{0:T(1024)S(1)} %bitcast.323, ...), kind=kOutput, calls=%fused_computation.87 | convolution fusion | flops 289403904 | bytes 13156352 | tf_op jit(solution)/shard_map/qhd,khd->hqk/dot_general | solution.py:68
  212.9 15.4 %all_to_all.19 = bf16[8,128,128]{1,2,0:T(8,128)(2,1)S(1)} all-to-all(bf16[8,128,128]{1,2,0:T(8,128)(2,1)} %copy.77), channel_id=1, replica_groups=mesh['blk'=16,'x'=4,'core'=2] {'x','core'}, dimensions={0} | all-to-all | bytes 524288 | tf_op jit(solution)/shard_map/all_to_all | solution.py:142
  238.3 69.9 %all_to_all.20 = bf16[64,16,2048]{2,1,0:T(8,128)(2,1)} all-to-all(bf16[64,16,2048]{2,1,0:T(8,128)(2,1)S(1)} %bitcast.219), channel_id=1, replica_groups=mesh['blk'=16,'x'=4,'core'=2] {'blk','x'}, dimensions={0} | all-to-all | bytes 8388608 | tf_op jit(solution)/shard_map/all_to_all | solution.py:180
  312.5 5.2 %fusion.143 = f32[1024,384]{1,0:T(8,128)} fusion(bf16[1024,2048]{1,0:T(8,128)(2,1)S(1)} %copy-done.4, bf16[2048,384]{1,0:T(8,128)(2,1)} %param.28), kind=kOutput, calls=%fused_computation.196 | convolution fusion | flops 1610612736 | bytes 7340032 | tf_op jit(solution)/shard_map/dot_general | solution.py:151
  317.6 9.6 %all-gather.9.cloned.1.call-done = bf16[128,16,2048]{2,1,0:T(8,128)(2,1)} async-done(((bf16[64,16,2048]{2,1,0:T(8,128)(2,1)}), bf16[128,16,2048]{2,1,0:T(8,128)(2,1)}) %all-gather.9.cloned.1.call-update) | async-done | bytes 8388624 | tf_op jit(solution)/shard_map/all_gather | solution.py:181
  327.3 11.1 %fusion.52 = f32[2048,704]{0,1:T(8,128)} fusion(bf16[2048,2048]{1,0:T(8,128)(2,1)} %bitcast.329, bf16[1,2048,704]{1,2,0:T(8,128)(2,1)} %param.32), kind=kOutput, calls=%fused_computation.79 | convolution fusion | flops 5905580032 | bytes 17039360 | tf_op jit(solution)/shard_map/dot_general | solution.py:185
  338.4 19.1 %convolution_convert_fusion = bf16[2048,2048]{1,0:T(8,128)(2,1)} fusion(f32[2048,704]{0,1:T(8,128)} %fusion.52, bf16[2048,2048]{1,0:T(8,128)(2,1)} %bitcast.330, bf16[1,704,2048]{2,1,0:T(8,128)(2,1)S(1)} %copy-done, bf16[1,2048,704]{1,2,0:T(8,128)(2,1)} %param.33), kind=kOutput, calls=%fused_computation.56 | convolution fusion | flops 11824005120 | bytes 28311552 | tf_op jit(solution)/shard_map/dot_general | solution.py:189
  357.5 4.7 dynamic-slice_bitcast_fusion
  362.6 8.8 %multiply_convert_fusion = bf16[1024,2048]{1,0:T(8,128)(2,1)} fusion(bf16[384,2048]{1,0:T(8,128)(2,1)} %param.30, f32[1024]{0:T(1024)S(1)} %add_divide_fusion, f32[1024,384]{1,0:T(8,128)} %fusion.143, bf16[1024,2048]{1,0:T(8,128)(2,1)} %all-gather.7.cloned.1.call-done, bf16[2048,384]{1,0:T(8,128)(2,1)} %param.29), kind=kOutput, calls=%fused_computation.55 | convolution fusion | flops 3227779072 | bytes 13111296 | tf_op jit(solution)/shard_map/dot_general | solution.py:159
  371.4 7.7 %fusion.44 = bf16[64,16,2048]{2,1,0:T(8,128)(2,1)} fusion(bf16[64,16,2048]{2,1,0:T(8,128)(2,1)} %collective-permute-done.5, bf16[2,64,16,2048]{3,2,1,0:T(8,128)(2,1)} %bitcast.221, s32[]{:T(128)S(6)} %select_n.91), kind=kLoop, calls=%fused_computation.54 | loop fusion | flops 8388608 | bytes 12582916 | tf_op jit(solution)/shard_map/convert_element_type | solution.py:198
  379.1 10.5 %all-to-all-start.2 = ((bf16[64,16,2048]{2,1,0:T(8,128)(2,1)}), bf16[64,16,2048]{2,1,0:T(8,128)(2,1)}, u32[]{:S(2)}, u32[]{:S(2)}) async-start(bf16[64,16,2048]{2,1,0:T(8,128)(2,1)} %fusion.44), calls=%async_computation.3 | async-start | bytes 8388608 | tf_op jit(solution)/shard_map/all_to_all | solution.py:201
  391.4 4.2 scatter_custom_fusion
  395.6 3.8 scatter_custom_fusion.1
  399.4 55.6 %all-to-all-done.2 = bf16[64,16,2048]{2,1,0:T(8,128)(2,1)} async-done(((bf16[64,16,2048]{2,1,0:T(8,128)(2,1)}), bf16[64,16,2048]{2,1,0:T(8,128)(2,1)}, u32[]{:S(2)}, u32[]{:S(2)}) %all-to-all-start.2) | async-done | bytes 4194336 | tf_op jit(solution)/shard_map/all_to_all | solution.py:201
  455.0 6.5 %convolution_multiply_fusion = f32[512,2048]{1,0:T(8,128)} fusion(bf16[1024,2048]{1,0:T(8,128)(2,1)} %bitcast.55, f32[512]{0:T(512)S(1)} %bitcast.331, s32[512]{0:T(512)S(1)} %bitcast.309), kind=kOutput, calls=%fused_computation.76 | convolution fusion | flops 2149056512 | bytes 8392704 | tf_op jit(solution)/shard_map/dot_general | solution.py:204
  (280 shorter events, 163.1 us)
Async XLA Ops:
  7.2 331.2 %copy-start = (bf16[1,704,2048]{2,1,0:T(8,128)(2,1)S(1)}, bf16[1,704,2048]{2,1,0:T(8,128)(2,1)}, u32[]{:S(2)}) copy-start(bf16[1,704,2048]{2,1,0:T(8,128)(2,1)} %param.34) | copy-start | bytes 8650756
  7.2 41.4 %copy-start.18 = (f32[2048]{0:T(1024)S(1)}, f32[2048]{0:T(1024)}, u32[]{:S(2)}) copy-start(f32[2048]{0:T(1024)} %param.22) | copy-start | bytes 24580
  7.2 38.2 %all-gather.5.cloned.1.call-start = ((), (), s32[]{:S(2)}) async-start(), calls=%async_computation.4 | async-start | bytes 4718592 | tf_op jit(solution)/shard_map/all_gather | solution.py:51
  7.9 301.0 %all-gather.7.cloned.1.call-start = ((), (), s32[]{:S(2)}) async-start(), calls=%async_computation.5 | async-start | bytes 4718592 | tf_op jit(solution)/shard_map/all_gather | solution.py:149
  54.8 14.2 %collective-permute-start.3 = (bf16[1040,256]{1,0:T(8,128)(2,1)}, bf16[1040,256]{1,0:T(8,128)(2,1)}, u32[]{:S(2)}, u32[]{:S(2)}) collective-permute-start(bf16[1040,256]{1,0:T(8,128)(2,1)} %copy.75), channel_id=1, source_target_pairs={{8,0},{16,8},{24,16},{56,24},{48,56},{40,48},{32,40},{64,32},{72,6... | collective-permute-start | bytes 1597448 | tf_op jit(solution)/shard_map/ppermute | solution.py:131
  57.4 14.8 %collective-permute-start.2 = (bf16[1040,256]{1,0:T(8,128)(2,1)}, bf16[1040,256]{1,0:T(8,128)(2,1)}, u32[]{:S(2)}, u32[]{:S(2)}) collective-permute-start(bf16[1040,256]{1,0:T(8,128)(2,1)} %copy.75), channel_id=1, source_target_pairs={{0,8},{8,16},{16,24},{24,56},{56,48},{48,40},{40,32},{32,64},{64,7... | collective-permute-start | bytes 1597448 | tf_op jit(solution)/shard_map/ppermute | solution.py:130
  73.3 17.9 %collective-permute-start = (bf16[1040,256]{1,0:T(8,128)(2,1)S(1)}, bf16[1040,256]{1,0:T(8,128)(2,1)}, u32[]{:S(2)}, u32[]{:S(2)}) collective-permute-start(bf16[1040,256]{1,0:T(8,128)(2,1)S(1)} %copy.114), channel_id=1, source_target_pairs={{0,8},{8,16},{16,24},{24,56},{56,48},{48,40},{40,32},{32,64},{64,7... | collective-permute-start | bytes 1597448 | tf_op jit(solution)/shard_map/while/body/eval_jaxpr/ppermute | solution.py:125
  75.1 16.1 %collective-permute-start.1 = (bf16[1040,256]{1,0:T(8,128)(2,1)}, bf16[1040,256]{1,0:T(8,128)(2,1)}, u32[]{:S(2)}, u32[]{:S(2)}) collective-permute-start(bf16[1040,256]{1,0:T(8,128)(2,1)} %copy.115), channel_id=1, source_target_pairs={{8,0},{16,8},{24,16},{56,24},{48,56},{40,48},{32,40},{64,32},{72,6... | collective-permute-start | bytes 1597448 | tf_op jit(solution)/shard_map/while/body/eval_jaxpr/ppermute | solution.py:126
  92.3 17.9 %collective-permute-start = (bf16[1040,256]{1,0:T(8,128)(2,1)S(1)}, bf16[1040,256]{1,0:T(8,128)(2,1)}, u32[]{:S(2)}, u32[]{:S(2)}) collective-permute-start(bf16[1040,256]{1,0:T(8,128)(2,1)S(1)} %copy.114), channel_id=1, source_target_pairs={{0,8},{8,16},{16,24},{24,56},{56,48},{48,40},{40,32},{32,64},{64,7... | collective-permute-start | bytes 1597448 | tf_op jit(solution)/shard_map/while/body/eval_jaxpr/ppermute | solution.py:125
  94.1 16.1 %collective-permute-start.1 = (bf16[1040,256]{1,0:T(8,128)(2,1)}, bf16[1040,256]{1,0:T(8,128)(2,1)}, u32[]{:S(2)}, u32[]{:S(2)}) collective-permute-start(bf16[1040,256]{1,0:T(8,128)(2,1)} %copy.115), channel_id=1, source_target_pairs={{8,0},{16,8},{24,16},{56,24},{48,56},{40,48},{32,40},{64,32},{72,6... | collective-permute-start | bytes 1597448 | tf_op jit(solution)/shard_map/while/body/eval_jaxpr/ppermute | solution.py:126
  111.3 17.9 %collective-permute-start = (bf16[1040,256]{1,0:T(8,128)(2,1)S(1)}, bf16[1040,256]{1,0:T(8,128)(2,1)}, u32[]{:S(2)}, u32[]{:S(2)}) collective-permute-start(bf16[1040,256]{1,0:T(8,128)(2,1)S(1)} %copy.114), channel_id=1, source_target_pairs={{0,8},{8,16},{16,24},{24,56},{56,48},{48,40},{40,32},{32,64},{64,7... | collective-permute-start | bytes 1597448 | tf_op jit(solution)/shard_map/while/body/eval_jaxpr/ppermute | solution.py:125
  113.1 16.1 %collective-permute-start.1 = (bf16[1040,256]{1,0:T(8,128)(2,1)}, bf16[1040,256]{1,0:T(8,128)(2,1)}, u32[]{:S(2)}, u32[]{:S(2)}) collective-permute-start(bf16[1040,256]{1,0:T(8,128)(2,1)} %copy.115), channel_id=1, source_target_pairs={{8,0},{16,8},{24,16},{56,24},{48,56},{40,48},{32,40},{64,32},{72,6... | collective-permute-start | bytes 1597448 | tf_op jit(solution)/shard_map/while/body/eval_jaxpr/ppermute | solution.py:126
  130.3 17.9 %collective-permute-start = (bf16[1040,256]{1,0:T(8,128)(2,1)S(1)}, bf16[1040,256]{1,0:T(8,128)(2,1)}, u32[]{:S(2)}, u32[]{:S(2)}) collective-permute-start(bf16[1040,256]{1,0:T(8,128)(2,1)S(1)} %copy.114), channel_id=1, source_target_pairs={{0,8},{8,16},{16,24},{24,56},{56,48},{48,40},{40,32},{32,64},{64,7... | collective-permute-start | bytes 1597448 | tf_op jit(solution)/shard_map/while/body/eval_jaxpr/ppermute | solution.py:125
  132.1 16.1 %collective-permute-start.1 = (bf16[1040,256]{1,0:T(8,128)(2,1)}, bf16[1040,256]{1,0:T(8,128)(2,1)}, u32[]{:S(2)}, u32[]{:S(2)}) collective-permute-start(bf16[1040,256]{1,0:T(8,128)(2,1)} %copy.115), channel_id=1, source_target_pairs={{8,0},{16,8},{24,16},{56,24},{48,56},{40,48},{32,40},{64,32},{72,6... | collective-permute-start | bytes 1597448 | tf_op jit(solution)/shard_map/while/body/eval_jaxpr/ppermute | solution.py:126
  149.2 17.9 %collective-permute-start = (bf16[1040,256]{1,0:T(8,128)(2,1)S(1)}, bf16[1040,256]{1,0:T(8,128)(2,1)}, u32[]{:S(2)}, u32[]{:S(2)}) collective-permute-start(bf16[1040,256]{1,0:T(8,128)(2,1)S(1)} %copy.114), channel_id=1, source_target_pairs={{0,8},{8,16},{16,24},{24,56},{56,48},{48,40},{40,32},{32,64},{64,7... | collective-permute-start | bytes 1597448 | tf_op jit(solution)/shard_map/while/body/eval_jaxpr/ppermute | solution.py:125
  151.1 16.1 %collective-permute-start.1 = (bf16[1040,256]{1,0:T(8,128)(2,1)}, bf16[1040,256]{1,0:T(8,128)(2,1)}, u32[]{:S(2)}, u32[]{:S(2)}) collective-permute-start(bf16[1040,256]{1,0:T(8,128)(2,1)} %copy.115), channel_id=1, source_target_pairs={{8,0},{16,8},{24,16},{56,24},{48,56},{40,48},{32,40},{64,32},{72,6... | collective-permute-start | bytes 1597448 | tf_op jit(solution)/shard_map/while/body/eval_jaxpr/ppermute | solution.py:126
  168.2 17.9 %collective-permute-start = (bf16[1040,256]{1,0:T(8,128)(2,1)S(1)}, bf16[1040,256]{1,0:T(8,128)(2,1)}, u32[]{:S(2)}, u32[]{:S(2)}) collective-permute-start(bf16[1040,256]{1,0:T(8,128)(2,1)S(1)} %copy.114), channel_id=1, source_target_pairs={{0,8},{8,16},{16,24},{24,56},{56,48},{48,40},{40,32},{32,64},{64,7... | collective-permute-start | bytes 1597448 | tf_op jit(solution)/shard_map/while/body/eval_jaxpr/ppermute | solution.py:125
  170.1 16.1 %collective-permute-start.1 = (bf16[1040,256]{1,0:T(8,128)(2,1)}, bf16[1040,256]{1,0:T(8,128)(2,1)}, u32[]{:S(2)}, u32[]{:S(2)}) collective-permute-start(bf16[1040,256]{1,0:T(8,128)(2,1)} %copy.115), channel_id=1, source_target_pairs={{8,0},{16,8},{24,16},{56,24},{48,56},{40,48},{32,40},{64,32},{72,6... | collective-permute-start | bytes 1597448 | tf_op jit(solution)/shard_map/while/body/eval_jaxpr/ppermute | solution.py:126
  186.2 10.7 %collective-permute-start.4 = (bf16[1040,256]{1,0:T(8,128)(2,1)}, bf16[1040,256]{1,0:T(8,128)(2,1)S(1)}, u32[]{:S(2)}, u32[]{:S(2)}) collective-permute-start(bf16[1040,256]{1,0:T(8,128)(2,1)} %get-tuple-element.56), channel_id=1, source_target_pairs={{0,8},{8,16},{16,24},{24,56},{56,48},{48,40},{40,32},{32,64},{64,7... | collective-permute-start | bytes 1597448 | tf_op jit(solution)/shard_map/ppermute | solution.py:135
  233.3 94.0 %all-gather.9.cloned.1.call-start = ((), (), s32[]{:S(2)}) async-start(), calls=%async_computation.7 | async-start | bytes 12582912 | tf_op jit(solution)/shard_map/all_gather | solution.py:181
  308.3 156.8 %reduce-scatter.2.cloned.1.call-start = ((), (), s32[]{:S(2)}) async-start(), calls=%async_computation.6 | async-start | bytes 4718592 | tf_op jit(solution)/shard_map/reduce_scatter | solution.py:157
  362.2 9.2 %collective-permute-start.5 = (bf16[64,16,2048]{2,1,0:T(8,128)(2,1)}, bf16[64,16,2048]{2,1,0:T(8,128)(2,1)}, u32[]{:S(2)}, u32[]{:S(2)}) collective-permute-start(bf16[64,16,2048]{2,1,0:T(8,128)(2,1)} %dynamic-slice_bitcast_fusion), channel_id=1, source_target_pairs={{0,1},{1,0},{2,3},{3,2},{4,5},{5,4},{6,7},{7,6},{8,9},{9,8},{10,11... | collective-permute-start | bytes 12582920 | tf_op jit(solution)/shard_map/ppermute | solution.py:195
  379.1 75.8 %copy-start.22 = (f32[128,4]{0,1:T(4,128)S(1)}, f32[128,4]{0,1:T(4,128)}, u32[]{:S(2)}) copy-start(f32[128,4]{0,1:T(4,128)} %param.36) | copy-start | bytes 6148
  379.1 75.8 %all-to-all-start.2 = ((bf16[64,16,2048]{2,1,0:T(8,128)(2,1)}), bf16[64,16,2048]{2,1,0:T(8,128)(2,1)}, u32[]{:S(2)}, u32[]{:S(2)}) async-start(bf16[64,16,2048]{2,1,0:T(8,128)(2,1)} %fusion.44), calls=%async_computation.3 | async-start | bytes 8388608 | tf_op jit(solution)/shard_map/all_to_all | solution.py:201
  (32 other events, 132.3 us)
Sparse Core Ops, SparseCore 0:
  9.7 35.6 all-gather.4
  233.4 51.9 all-gather.6
  308.4 18.8 all-gather.8
  371.5 76.9 reduce-scatter.1
